TPU v7x, 512 devices: a whole 4x4x16 slice. The times are simulated.
512 devices in a mesh: lon: 32 (over z_lo, x, core), lat: 16 (over y, z_hi).
Axes of the slice: x: 4, y: 4, z: 16 (z_hi: 4, z_lo: 4; z = z_hi * 4 + z_lo), core: 2. Of those that a mesh axis runs over, the one named last changes fastest.
Arguments:
- ensemble: float32 [9, 40, 128, 4096], P(None, None, 'lat', 'lon'), may hold values from -6 to 6
- obs_lon: int32 [512], replicated, may hold values from 0 to 4095
- obs_lat: int32 [512], replicated, may hold values from 0 to 127
- observation_field: int32 [512], replicated, may hold values from 0 to 8
- obs_radius: int32 [512], replicated, may hold values from 4 to 8
- batch_order: int32 [512], replicated, may hold values from 0 to 511, each once
- obs_value: float32 [512], replicated, may hold values from -8 to 8
- obs_error: float32 [512], replicated, may hold values from 0.1 to 1
Outputs:
- analysis: bfloat16 [9, 40, 128, 4096], P(None, None, 'lat', 'lon')
Inputs may be any that keep to these rules, and one draw needn't show every extreme that they name: `batch_order`: every observation number appears once. `obs_radius`: radii are at most 8 cells.
All inputs are finite; a program needn't handle non-finite values.
Results may differ from a plain program's by a relative error of at most 0.001.
Values sent between devices are 32-bit elements; how exact they have to be, the bound alone decides.
No kernel may reach another device: no remote copies, remote signals or barrier semaphores. Data moves between devices by JAX's collectives and lax.ppermute only.
A program may use at most 64 MiB of HBM per device.

v0:
```python
import math

import jax
import jax.numpy as jnp
from jax import lax
from jax.sharding import PartitionSpec as P

STEPS = 2
BATCHES = 2
NB = 256


RATE = 0.4
DEPTHS = (1.0, 0.6, 0.35)
COUPLE = ((1.0, 0.5, 0.25), (0.5, 1.0, 0.5), (0.25, 0.5, 1.0))


def ring_pairs(size, step):
    return [(i, (i + step) % size) for i in range(size)]


def line_pairs(size, step):
    return [(i, i + step) for i in range(size) if 0 <= i + step < size]


def lon_edges(array):
    size = lax.axis_size("lon")
    up = [(i, (i + 1) % size) for i in range(size)]
    down = [((i + 1) % size, i) for i in range(size)]
    left = lax.ppermute(array[..., -1:], "lon", up)
    right = lax.ppermute(array[..., :1], "lon", down)
    return left, right


def lat_edges(array):
    size = lax.axis_size("lat")
    up = [(i, i + 1) for i in range(size - 1)]
    down = [(i + 1, i) for i in range(size - 1)]
    before = lax.ppermute(array[:, :, -1:, :], "lat", up)
    after = lax.ppermute(array[:, :, :1, :], "lat", down)
    return before, after


def zonal(values, left, right):
    following = jnp.concatenate([values[..., 1:], right], axis=3)
    preceding = jnp.concatenate([left, values[..., :-1]], axis=3)
    return 0.5 * (following - preceding)


def meridional(values, before, after):
    following = jnp.concatenate([values[:, :, 1:, :], after], axis=2)
    preceding = jnp.concatenate([before, values[:, :, :-1, :]], axis=2)
    return 0.5 * (following - preceding)


def couple(height):
    return jnp.stack(
        [
            COUPLE[k][0] * height[0] + COUPLE[k][1] * height[1] + COUPLE[k][2] * height[2]
            for k in range(3)
        ]
    )


def march_prediction(running_member_set, rotation_frequency):
    height = running_member_set[0:3]
    eastward_speed = running_member_set[3:6]
    merid_vel = running_member_set[6:9]
    depths = jnp.array(DEPTHS, jnp.float32)[:, None, None, None]
    u_left, u_right = lon_edges(eastward_speed)
    v_before, v_after = lat_edges(merid_vel)
    height = height - RATE * depths * (
        zonal(eastward_speed, u_left, u_right) + meridional(merid_vel, v_before, v_after)
    )
    pressure = couple(height)
    p_left, p_right = lon_edges(pressure)
    p_before, p_after = lat_edges(pressure)
    eastward_speed = (
        eastward_speed
        + RATE * rotation_frequency * merid_vel
        - RATE * zonal(pressure, p_left, p_right)
    )
    merid_vel = (
        merid_vel
        - RATE * rotation_frequency * eastward_speed
        - RATE * meridional(pressure, p_before, p_after)
    )
    return jnp.concatenate([height, eastward_speed, merid_vel])


def statistics(priors, values, errors, member_count):
    mean_obs = jnp.mean(priors, axis=1, keepdims=True)
    anomaly = priors - mean_obs
    variance = jnp.sum(anomaly * anomaly, axis=1, keepdims=True) / (member_count - 1)
    obs_err = errors[:, None]
    denominator = variance + obs_err
    shrink = 1.0 / (1.0 + jnp.sqrt(obs_err / denominator))
    gains = (values[:, None] - mean_obs - shrink * anomaly) / denominator
    return (gains, anomaly)


def localize(cell_lon, cell_lat, lon_obs, lat_obs, radius_obs, grid_lon):
    lon_gap = (cell_lon[None, :] - lon_obs[:, None]) % grid_lon
    lon_gap = jnp.minimum(lon_gap, grid_lon - lon_gap)
    lat_gap = cell_lat[None, :] - lat_obs[:, None]
    distance_sq = (lon_gap * lon_gap + lat_gap * lat_gap).astype(jnp.float32)
    radius_sq = (radius_obs * radius_obs).astype(jnp.float32)[:, None]
    return jnp.square(jnp.maximum(1.0 - distance_sq / radius_sq, 0.0))


def neighbourhood_sum(table):
    lon_n = lax.axis_size("lon")
    lat_n = lax.axis_size("lat")
    row = (
        table
        + lax.ppermute(table, "lon", ring_pairs(lon_n, 1))
        + lax.ppermute(table, "lon", ring_pairs(lon_n, -1))
    )
    return (
        row
        + lax.ppermute(row, "lat", line_pairs(lat_n, 1))
        + lax.ppermute(row, "lat", line_pairs(lat_n, -1))
    )


def tile_origin(state):
    _, _, rows_tile, cols_tile = state.shape
    return lax.axis_index("lon") * cols_tile, lax.axis_index("lat") * rows_tile


def at_owner(state, lon_obs, lat_obs, kind_obs):
    _, _, rows_tile, cols_tile = state.shape
    lon_base, lat_base = tile_origin(state)
    owned = (
        (lon_obs >= lon_base)
        & (lon_obs < lon_base + cols_tile)
        & (lat_obs >= lat_base)
        & (lat_obs < lat_base + rows_tile)
    )
    nearby_latitude = jnp.clip(lat_obs - lat_base, 0, rows_tile - 1)
    local_lon = jnp.clip(lon_obs - lon_base, 0, cols_tile - 1)
    rows = state[kind_obs, :, nearby_latitude, :]
    pick = jnp.arange(cols_tile, dtype=jnp.int32)[None, :] == local_lon[:, None]
    values = jnp.sum(jnp.where(pick[:, None, :], rows, 0.0), axis=2)
    return values, owned


def update(state, gains, anomaly, weights):
    return jnp.concatenate(
        [update_group(state[f : f + 3], gains, anomaly, weights) for f in range(0, state.shape[0], 3)]
    )


def update_group(state, gains, anomaly, weights):
    fields_count, member_count, rows_tile, cols_tile = state.shape
    flattened = state.reshape(fields_count, member_count, rows_tile * cols_tile)
    deviation = flattened - jnp.mean(flattened, axis=1, keepdims=True)
    covariance = jnp.einsum(
        "om,fmc->foc", anomaly, deviation, precision=lax.Precision.HIGH
    ) / (member_count - 1)
    increment = jnp.einsum(
        "om,foc->fmc", gains, covariance * weights[None], precision=lax.Precision.HIGH
    )
    return (flattened + increment).reshape(state.shape)


def tile_weights(state, lon_obs, lat_obs, radius_obs):
    _, _, rows_tile, cols_tile = state.shape
    lon_base, lat_base = tile_origin(state)
    grid_lon = cols_tile * lax.axis_size("lon")
    cell_lat = lat_base + jnp.repeat(jnp.arange(rows_tile, dtype=jnp.int32), cols_tile)
    cell_lon = lon_base + jnp.tile(jnp.arange(cols_tile, dtype=jnp.int32), rows_tile)
    return localize(cell_lon, cell_lat, lon_obs, lat_obs, radius_obs, grid_lon)


def shards(
    ensemble, obs_lon, obs_lat, observation_field, obs_radius, batch_order, obs_value, obs_error
):
    fields_count, member_count, rows_tile, cols_tile = ensemble.shape
    lat_index = lax.axis_index("lat")
    lat_count = lax.axis_size("lat")
    lon_size = lax.axis_size("lon")
    lat_size = lax.axis_size("lat")
    grid_lon = cols_tile * lon_size
    mesh_northing = rows_tile * lat_count
    row_global = (lat_index * rows_tile + jnp.arange(rows_tile, dtype=jnp.int32)).astype(
        jnp.float32
    )
    rotation_frequency = (2.0 * jnp.sin(math.pi * ((row_global + 0.5) / mesh_northing - 0.5)))[
        :, None
    ]
    ints = jnp.stack([obs_lon, obs_lat, observation_field, obs_radius])[:, batch_order]
    floats = jnp.stack([obs_value, obs_error])[:, batch_order]
    batches = [
        (ints[:, b * NB : (b + 1) * NB], floats[:, b * NB : (b + 1) * NB]) for b in range(BATCHES)
    ]
    state = ensemble
    for step_index in range(STEPS):
        state = march_prediction(state, rotation_frequency)

    (lon0, lat0, kind0, radius0), (value0, error0) = batches[0]
    values, owned = at_owner(state, lon0, lat0, kind0)
    priors = neighbourhood_sum(jnp.where(owned[:, None], values, 0.0))
    for batch_index in range(BATCHES):
        (lon_b, lat_b, kind_b, radius_b), (value_b, error_b) = batches[batch_index]
        gains, anomaly = statistics(priors, value_b, error_b, member_count)
        if batch_index + 1 < BATCHES:
            (lon_n, lat_n, kind_n, _), _ = batches[batch_index + 1]
            values, owned = at_owner(state, lon_n, lat_n, kind_n)
            deviation = values - jnp.mean(values, axis=1, keepdims=True)
            covariance = jnp.einsum(
                "om,jm->oj", anomaly, deviation, precision=lax.Precision.HIGH
            ) / (member_count - 1)
            weights = localize(lon_n, lat_n, lon_b, lat_b, radius_b, grid_lon)
            increment = jnp.einsum(
                "om,oj->jm", gains, covariance * weights, precision=lax.Precision.HIGH
            )
            table = jnp.where(owned[:, None], values + increment, 0.0)
            weights = tile_weights(state, lon_b, lat_b, radius_b)
            table, head = lax.optimization_barrier((table, state[0:3]))
            row = (
                table
                + lax.ppermute(table, "lon", ring_pairs(lon_size, 1))
                + lax.ppermute(table, "lon", ring_pairs(lon_size, -1))
            )
            head = update(head, gains, anomaly, weights)
            row, tail, head = lax.optimization_barrier((row, state[3:], head))
            priors = (
                row
                + lax.ppermute(row, "lat", line_pairs(lat_size, 1))
                + lax.ppermute(row, "lat", line_pairs(lat_size, -1))
            )
            state = jnp.concatenate([head, update(tail, gains, anomaly, weights)])
        else:
            state = update(state, gains, anomaly, tile_weights(state, lon_b, lat_b, radius_b))
    return state.astype(jnp.bfloat16)


def solution(mesh):
    placed = (P(None, None, "lat", "lon"), P(), P(), P(), P(), P(), P(), P())
    return jax.shard_map(
        shards, mesh=mesh, in_specs=placed, out_specs=P(None, None, "lat", "lon"), check_vma=False
    )
```

profile of v0, /device:TPU:24, one launch (start us, length us, event | category | flops | bytes accessed | tf_op | source)
XLA Modules:
  0.0 215.9 jit_solution(11260098505072654728)
XLA Ops:
  0.0 1.5 fusion.130
  1.5 0.9 copy.89
  2.4 8.2 %collective-permute-start = (f32[3,40,8,1]{3,1,2,0:T(8,128)}, f32[3,40,8,1]{3,1,2,0:T(8,128)}, u32[]{:S(2)}, u32[]{:S(2)}) collective-permute-start(f32[3,40,8,1]{3,1,2,0:T(8,128)} %copy.89), channel_id=1, source_target_pairs={{16,0},{32,16},{48,32},{64,48},{80,64},{96,80},{112,96},{128,112},... | collective-permute-start | bytes 11528 | tf_op jit(solution)/shard_map/ppermute | solution.py:31
  10.5 0.9 copy.90
  11.4 1.9 collective-permute-start.1
  14.1 10.2 %collective-permute-start.2 = (f32[3,40,1,128]{3,1,2,0:T(8,128)}, f32[3,40,1,128]{3,1,2,0:T(8,128)}, u32[]{:S(2)}, u32[]{:S(2)}) collective-permute-start(f32[3,40,1,128]{3,1,2,0:T(8,128)} %bitcast.28), channel_id=1, source_target_pairs={{1,0},{2,1},{3,2},{4,3},{5,4},{6,5},{7,6},{8,7},{9,8},{10,9},{11,1... | collective-permute-start | bytes 184328 | tf_op jit(solution)/shard_map/ppermute | solution.py:40
  24.3 2.1 collective-permute-start.3
  26.4 1.1 fusion.131
  27.9 1.0 gather_fusion
  29.5 0.8 fusion.80
  31.1 1.0 gather_fusion.3
  32.2 0.9 slice_reduce_fusion.3
  35.0 3.4 %multiply_multiply_fusion = (f32[256,1024]{0,1:T(8,128)S(1)}, f32[256,1024]{0,1:T(8,128)}) fusion(f32[256]{0:T(256)} %get-tuple-element.23, s32[256]{0:T(256)} %copy-done.12, s32[256]{0:T(256)S(1)} %get-tuple-element.32, s32[1024]{0:T(1024)} %get-tuple-element.98, s32[1024]{0:T(1024)} %get-tuple-element.99, f32[256]{0:T(256)} %get-tuple-element.24, ...), kind=kLoop, calls=%fused_computation.69 | loop fusion | flops 12582912 | bytes 2111488 | tf_op jit(solution)/shard_map/mul | solution.py:162
  38.5 1.1 copy.88
  39.6 1.1 copy.91
  41.0 1.6 fusion.46
  43.1 8.7 %collective-permute-start.8 = (f32[3,40,1,128]{3,1,2,0:T(8,128)S(1)}, f32[3,40,1,128]{3,1,2,0:T(8,128)S(1)}, u32[]{:S(2)}, u32[]{:S(2)}) collective-permute-start(f32[3,40,1,128]{3,1,2,0:T(8,128)S(1)} %get-tuple-element.78), channel_id=1, source_target_pairs={{1,0},{2,1},{3,2},{4,3},{5,4},{6,5},{7,6},{8,7},{9,8},{10,9},{11,1... | collective-permute-start | bytes 184328 | tf_op jit(solution)/shard_map/ppermute | solution.py:40
  51.8 1.9 collective-permute-start.9
  53.7 1.9 collective-permute-start.5
  55.6 7.5 %collective-permute-start.4 = (f32[3,40,8,1]{3,1,2,0:T(8,128)S(1)}, f32[3,40,8,1]{3,1,2,0:T(8,128)S(1)}, u32[]{:S(2)}, u32[]{:S(2)}) collective-permute-start(f32[3,40,8,1]{3,1,2,0:T(8,128)S(1)} %get-tuple-element.75), channel_id=1, source_target_pairs={{16,0},{32,16},{48,32},{64,48},{80,64},{96,80},{112,96},{128,112},... | collective-permute-start | bytes 11528 | tf_op jit(solution)/shard_map/ppermute | solution.py:31
  63.3 4.5 %collective-permute-done.5 = f32[3,40,8,1]{3,1,2,0:T(8,128)S(1)} collective-permute-done((f32[3,40,8,1]{3,1,2,0:T(8,128)S(1)}, f32[3,40,8,1]{3,1,2,0:T(8,128)S(1)}, u32[]{:S(2)}, u32[]{:S(2)}) %collective-permute-start.5) | collective-permute-done | bytes 3872 | tf_op jit(solution)/shard_map/ppermute | solution.py:30
  67.8 1.8 collective-permute-done.4
  70.4 7.7 %collective-permute-start.6 = (f32[3,40,8,1]{3,1,2,0:T(8,128)S(1)}, f32[3,40,8,1]{3,1,2,0:T(8,128)S(1)}, u32[]{:S(2)}, u32[]{:S(2)}) collective-permute-start(f32[3,40,8,1]{3,1,2,0:T(8,128)S(1)} %get-tuple-element.70), channel_id=1, source_target_pairs={{16,0},{32,16},{48,32},{64,48},{80,64},{96,80},{112,96},{128,112},... | collective-permute-start | bytes 11528 | tf_op jit(solution)/shard_map/ppermute | solution.py:31
  78.2 1.9 collective-permute-start.7
  80.1 8.7 %collective-permute-start.10 = (f32[3,40,1,128]{3,1,2,0:T(8,128)S(1)}, f32[3,40,1,128]{3,1,2,0:T(8,128)S(1)}, u32[]{:S(2)}, u32[]{:S(2)}) collective-permute-start(f32[3,40,1,128]{3,1,2,0:T(8,128)S(1)} %get-tuple-element.66), channel_id=1, source_target_pairs={{1,0},{2,1},{3,2},{4,3},{5,4},{6,5},{7,6},{8,7},{9,8},{10,9},{11,1... | collective-permute-start | bytes 184328 | tf_op jit(solution)/shard_map/ppermute | solution.py:40
  88.9 1.9 collective-permute-start.11
  90.9 4.2 %collective-permute-done.7 = f32[3,40,8,1]{3,1,2,0:T(8,128)S(1)} collective-permute-done((f32[3,40,8,1]{3,1,2,0:T(8,128)S(1)}, f32[3,40,8,1]{3,1,2,0:T(8,128)S(1)}, u32[]{:S(2)}, u32[]{:S(2)}) %collective-permute-start.7) | collective-permute-done | bytes 3872 | tf_op jit(solution)/shard_map/ppermute | solution.py:30
  95.1 4.7 %collective-permute-done.11 = f32[3,40,1,128]{3,1,2,0:T(8,128)S(1)} collective-permute-done((f32[3,40,1,128]{3,1,2,0:T(8,128)S(1)}, f32[3,40,1,128]{3,1,2,0:T(8,128)S(1)}, u32[]{:S(2)}, u32[]{:S(2)}) %collective-permute-start.11) | collective-permute-done | bytes 61472 | tf_op jit(solution)/shard_map/ppermute | solution.py:39
  100.7 2.8 %collective-permute-start.14 = (f32[3,40,1,128]{3,1,2,0:T(8,128)S(1)}, f32[3,40,1,128]{3,1,2,0:T(8,128)S(1)}, u32[]{:S(2)}, u32[]{:S(2)}) collective-permute-start(f32[3,40,1,128]{3,1,2,0:T(8,128)S(1)} %get-tuple-element.59), channel_id=1, source_target_pairs={{1,0},{2,1},{3,2},{4,3},{5,4},{6,5},{7,6},{8,7},{9,8},{10,9},{11,1... | collective-permute-start | bytes 184328 | tf_op jit(solution)/shard_map/ppermute | solution.py:40
  103.5 7.0 %collective-permute-start.15 = (f32[3,40,1,128]{3,1,2,0:T(8,128)S(1)}, f32[3,40,1,128]{3,1,2,0:T(8,128)S(1)}, u32[]{:S(2)}, u32[]{:S(2)}) collective-permute-start(f32[3,40,1,128]{3,1,2,0:T(8,128)S(1)} %get-tuple-element.58), channel_id=1, source_target_pairs={{0,1},{1,2},{2,3},{3,4},{4,5},{5,6},{6,7},{7,8},{8,9},{9,10},{10,1... | collective-permute-start | bytes 184328 | tf_op jit(solution)/shard_map/ppermute | solution.py:39
  110.5 1.9 collective-permute-start.13
  112.4 7.5 %collective-permute-start.12 = (f32[3,40,8,1]{3,1,2,0:T(8,128)S(1)}, f32[3,40,8,1]{3,1,2,0:T(8,128)S(1)}, u32[]{:S(2)}, u32[]{:S(2)}) collective-permute-start(f32[3,40,8,1]{3,1,2,0:T(8,128)S(1)} %get-tuple-element.56), channel_id=1, source_target_pairs={{16,0},{32,16},{48,32},{64,48},{80,64},{96,80},{112,96},{128,112},... | collective-permute-start | bytes 11528 | tf_op jit(solution)/shard_map/ppermute | solution.py:31
  120.0 4.5 %collective-permute-done.13 = f32[3,40,8,1]{3,1,2,0:T(8,128)S(1)} collective-permute-done((f32[3,40,8,1]{3,1,2,0:T(8,128)S(1)}, f32[3,40,8,1]{3,1,2,0:T(8,128)S(1)}, u32[]{:S(2)}, u32[]{:S(2)}) %collective-permute-start.13) | collective-permute-done | bytes 3872 | tf_op jit(solution)/shard_map/ppermute | solution.py:30
  124.5 1.8 collective-permute-done.12
  127.7 3.9 %gather_fusion.2 = f32[256,40,128]{2,1,0:T(8,128)} fusion(f32[9,40,8,128]{3,1,2,0:T(8,128)S(1)} %pad_maximum_fusion, s32[256]{0:T(256)S(1)} %bitcast.196), kind=kCustom, calls=%fused_computation.2 | custom fusion | bytes 10487808 | tf_op jit(solution)/shard_map/gather | solution.py:142
  131.6 4.6 %select_reduce_fusion = f32[256,40]{1,0:T(8,128)} fusion(f32[256,40,128]{2,1,0:T(8,128)} %gather_fusion.2, pred[256,128]{1,0:T(8,128)(4,1)S(1)} %iota_compare_fusion), kind=kLoop, calls=%fused_computation.4 | loop fusion | flops 2611200 | bytes 5316608 | tf_op jit(solution)/shard_map/reduce_sum | solution.py:144
  136.2 1.0 copy.69
  137.8 7.7 %collective-permute-start.17 = (f32[256,40]{0,1:T(8,128)}, f32[256,40]{0,1:T(8,128)}, u32[]{:S(2)}, u32[]{:S(2)}) collective-permute-start(f32[256,40]{0,1:T(8,128)} %broadcast_select_fusion), channel_id=1, source_target_pairs={{0,496},{16,0},{32,16},{48,32},{64,48},{80,64},{96,80},{112,96},{1... | collective-permute-start | bytes 122888 | tf_op jit(solution)/shard_map/ppermute | solution.py:117
  145.5 2.1 collective-permute-start.16
  147.6 3.9 %gather_fusion.1 = f32[256,40,128]{2,1,0:T(8,128)} fusion(f32[9,40,8,128]{3,1,2,0:T(8,128)S(1)} %pad_maximum_fusion, s32[256]{0:T(256)S(1)} %bitcast.195), kind=kCustom, calls=%fused_computation.1 | custom fusion | bytes 10487808 | tf_op jit(solution)/shard_map/gather | solution.py:142
  151.6 4.9 %select_reduce_fusion.1 = (f32[256]{0:T(256)S(1)}, f32[256,40]{1,0:T(8,128)S(1)}) fusion(f32[256,40,128]{2,1,0:T(8,128)} %gather_fusion.1, pred[256,128]{1,0:T(8,128)(4,1)} %iota_compare_fusion.1), kind=kLoop, calls=%fused_computation.5 | loop fusion | flops 3921664 | bytes 5317632 | tf_op jit(solution)/shard_map/reduce_sum | solution.py:210
  156.6 0.8 add_add_fusion.5
  157.4 3.7 %collective-permute-start.19 = (f32[256,40]{0,1:T(8,128)S(1)}, f32[256,40]{0,1:T(8,128)S(1)}, u32[]{:S(2)}, u32[]{:S(2)}) collective-permute-start(f32[256,40]{0,1:T(8,128)S(1)} %add_add_fusion.5), channel_id=1, source_target_pairs={{1,0},{2,1},{3,2},{4,3},{5,4},{6,5},{7,6},{8,7},{9,8},{10,9},{11,1... | collective-permute-start | bytes 122888 | tf_op jit(solution)/shard_map/ppermute | solution.py:122
  161.1 6.1 %collective-permute-start.18 = (f32[256,40]{0,1:T(8,128)S(1)}, f32[256,40]{0,1:T(8,128)S(1)}, u32[]{:S(2)}, u32[]{:S(2)}) collective-permute-start(f32[256,40]{0,1:T(8,128)S(1)} %add_add_fusion.5), channel_id=1, source_target_pairs={{0,1},{1,2},{2,3},{3,4},{4,5},{5,6},{6,7},{7,8},{8,9},{9,10},{10,1... | collective-permute-start | bytes 122888 | tf_op jit(solution)/shard_map/ppermute | solution.py:121
  167.2 1.0 pad_maximum_fusion.1
  168.3 3.5 %collective-permute-done.18 = f32[256,40]{0,1:T(8,128)S(1)} collective-permute-done((f32[256,40]{0,1:T(8,128)S(1)}, f32[256,40]{0,1:T(8,128)S(1)}, u32[]{:S(2)}, u32[]{:S(2)}) %collective-permute-start.18) | collective-permute-done | bytes 40992 | tf_op jit(solution)/shard_map/ppermute | solution.py:121
  172.7 6.1 %collective-permute-start.21 = (f32[256,40]{0,1:T(8,128)S(1)}, f32[256,40]{0,1:T(8,128)S(1)}, u32[]{:S(2)}, u32[]{:S(2)}) collective-permute-start(f32[256,40]{0,1:T(8,128)S(1)} %fusion.28), channel_id=1, source_target_pairs={{0,496},{16,0},{32,16},{48,32},{64,48},{80,64},{96,80},{112,96},{1... | collective-permute-start | bytes 122888 | tf_op jit(solution)/shard_map/ppermute | solution.py:224
  178.8 1.9 collective-permute-start.20
  180.9 1.4 fusion.43
  182.3 1.6 fusion.23
  184.0 4.5 %collective-permute-done.20 = f32[256,40]{0,1:T(8,128)S(1)} collective-permute-done((f32[256,40]{0,1:T(8,128)S(1)}, f32[256,40]{0,1:T(8,128)S(1)}, u32[]{:S(2)}, u32[]{:S(2)}) %collective-permute-start.20) | collective-permute-done | bytes 40992 | tf_op jit(solution)/shard_map/ppermute | solution.py:223
  188.5 2.4 %collective-permute-start.23 = (f32[256,40]{0,1:T(8,128)S(1)}, f32[256,40]{0,1:T(8,128)S(1)}, u32[]{:S(2)}, u32[]{:S(2)}) collective-permute-start(f32[256,40]{0,1:T(8,128)S(1)} %add_add_fusion.3), channel_id=1, source_target_pairs={{1,0},{2,1},{3,2},{4,3},{5,4},{6,5},{7,6},{8,7},{9,8},{10,9},{11,1... | collective-permute-start | bytes 122888 | tf_op jit(solution)/shard_map/ppermute | solution.py:231
  190.9 7.6 %collective-permute-start.22 = (f32[256,40]{0,1:T(8,128)S(1)}, f32[256,40]{0,1:T(8,128)S(1)}, u32[]{:S(2)}, u32[]{:S(2)}) collective-permute-start(f32[256,40]{0,1:T(8,128)S(1)} %add_add_fusion.3), channel_id=1, source_target_pairs={{0,1},{1,2},{2,3},{3,4},{4,5},{5,6},{6,7},{7,8},{8,9},{9,10},{10,1... | collective-permute-start | bytes 122888 | tf_op jit(solution)/shard_map/ppermute | solution.py:230
  198.7 1.4 fusion.41
  200.1 1.6 fusion.144
  201.8 1.4 fusion.42
  203.2 2.4 %fusion.145 = (f32[3,1024]{1,0:T(4,128)S(1)}, f32[3,40,1024]{2,1,0:T(8,128)}) fusion(f32[256]{0:T(256)S(1)} %get-tuple-element.89, f32[256,40]{0,1:T(8,128)S(1)} %get-tuple-element.36, f32[256]{0:T(256)S(1)} %get-tuple-element.93, f32[256]{0:T(256)S(1)} %get-tuple-element.88, f32[256]{0:T(256)S(1)} %get-tuple-element.92, f32[3,1024,256]{2,1,0:T(8,128)S(1)} %fusion.42, ...), kind=kOutput, calls=%fused_computation.264 | convolution fusion | flops 189813760 | bytes 5234688 | tf_op jit(solution)/shard_map/om,foc->fmc/dot_general | solution.py:161
  205.9 1.4 fusion.58
  207.4 1.5 fusion.26
  208.9 1.4 fusion.60
  210.4 1.5 fusion.25
  211.9 1.4 fusion.62
  213.4 1.5 fusion.24
  214.9 0.9 pad_maximum_fusion.2
  (150 shorter events, 10.6 us)
Async XLA Ops:
  0.0 13.3 %copy-start.1 = (f32[9,40,8,128]{3,2,1,0:T(8,128)S(1)}, f32[9,40,8,128]{3,2,1,0:T(8,128)}, u32[]{:S(2)}) copy-start(f32[9,40,8,128]{3,2,1,0:T(8,128)} %param.10) | copy-start | bytes 4423684
  2.4 38.6 %collective-permute-start = (f32[3,40,8,1]{3,1,2,0:T(8,128)}, f32[3,40,8,1]{3,1,2,0:T(8,128)}, u32[]{:S(2)}, u32[]{:S(2)}) collective-permute-start(f32[3,40,8,1]{3,1,2,0:T(8,128)} %copy.89), channel_id=1, source_target_pairs={{16,0},{32,16},{48,32},{64,48},{80,64},{96,80},{112,96},{128,112},... | collective-permute-start | bytes 11528 | tf_op jit(solution)/shard_map/ppermute | solution.py:31
  11.4 29.5 %collective-permute-start.1 = (f32[3,40,8,1]{3,1,2,0:T(8,128)}, f32[3,40,8,1]{3,1,2,0:T(8,128)}, u32[]{:S(2)}, u32[]{:S(2)}) collective-permute-start(f32[3,40,8,1]{3,1,2,0:T(8,128)} %copy.90), channel_id=1, source_target_pairs={{0,16},{16,32},{32,48},{48,64},{64,80},{80,96},{96,112},{112,128},... | collective-permute-start | bytes 11528 | tf_op jit(solution)/shard_map/ppermute | solution.py:30
  14.1 26.9 %collective-permute-start.2 = (f32[3,40,1,128]{3,1,2,0:T(8,128)}, f32[3,40,1,128]{3,1,2,0:T(8,128)}, u32[]{:S(2)}, u32[]{:S(2)}) collective-permute-start(f32[3,40,1,128]{3,1,2,0:T(8,128)} %bitcast.28), channel_id=1, source_target_pairs={{1,0},{2,1},{3,2},{4,3},{5,4},{6,5},{7,6},{8,7},{9,8},{10,9},{11,1... | collective-permute-start | bytes 184328 | tf_op jit(solution)/shard_map/ppermute | solution.py:40
  24.3 3.4 %copy-start.23 = (s32[512]{0:T(512)S(1)}, s32[512]{0:T(512)}, u32[]{:S(2)}) copy-start(s32[512]{0:T(512)} %param.15) | copy-start | bytes 6148
  24.3 3.4 %copy-start.26 = (s32[512]{0:T(512)S(1)}, s32[512]{0:T(512)}, u32[]{:S(2)}) copy-start(s32[512]{0:T(512)} %param.14) | copy-start | bytes 6148
  24.3 3.4 %copy-start.27 = (s32[512]{0:T(512)S(1)}, s32[512]{0:T(512)}, u32[]{:S(2)}) copy-start(s32[512]{0:T(512)} %param.13) | copy-start | bytes 6148
  24.3 3.4 %copy-start.28 = (s32[512]{0:T(512)S(1)}, s32[512]{0:T(512)}, u32[]{:S(2)}) copy-start(s32[512]{0:T(512)} %param.12) | copy-start | bytes 6148
  24.3 3.4 %copy-start.29 = (s32[512]{0:T(512)S(1)}, s32[512]{0:T(512)}, u32[]{:S(2)}) copy-start(s32[512]{0:T(512)} %param.11) | copy-start | bytes 6148
  24.3 16.6 %collective-permute-start.3 = (f32[3,40,1,128]{3,1,2,0:T(8,128)}, f32[3,40,1,128]{3,1,2,0:T(8,128)}, u32[]{:S(2)}, u32[]{:S(2)}) collective-permute-start(f32[3,40,1,128]{3,1,2,0:T(8,128)} %bitcast.29), channel_id=1, source_target_pairs={{0,1},{1,2},{2,3},{3,4},{4,5},{5,6},{6,7},{7,8},{8,9},{9,10},{10,1... | collective-permute-start | bytes 184328 | tf_op jit(solution)/shard_map/ppermute | solution.py:39
  27.5 3.5 %copy-start.24 = (f32[512]{0:T(512)S(1)}, f32[512]{0:T(512)}, u32[]{:S(2)}) copy-start(f32[512]{0:T(512)} %param.17) | copy-start | bytes 6148
  27.5 3.5 %copy-start.25 = (f32[512]{0:T(512)S(1)}, f32[512]{0:T(512)}, u32[]{:S(2)}) copy-start(f32[512]{0:T(512)} %param.16) | copy-start | bytes 6148
  29.5 5.5 %copy-start.10 = (s32[256]{0:T(256)}, s32[256]{0:T(256)S(1)}, u32[]{:S(2)}) copy-start(s32[256]{0:T(256)S(1)} %get-tuple-element.28) | copy-start | bytes 3076
  29.5 5.5 %copy-start.12 = (s32[256]{0:T(256)}, s32[256]{0:T(256)S(1)}, u32[]{:S(2)}) copy-start(s32[256]{0:T(256)S(1)} %get-tuple-element.31) | copy-start | bytes 3076
  29.5 11.4 %copy-start.6 = (s32[256]{0:T(256)}, s32[256]{0:T(256)S(1)}, u32[]{:S(2)}) copy-start(s32[256]{0:T(256)S(1)} %get-tuple-element.29) | copy-start | bytes 3076
  29.5 11.4 %copy-start.8 = (s32[256]{0:T(256)}, s32[256]{0:T(256)S(1)}, u32[]{:S(2)}) copy-start(s32[256]{0:T(256)S(1)} %get-tuple-element.32) | copy-start | bytes 3076
  33.1 7.9 %copy-start.21 = (f32[3]{0:T(128)S(1)}, f32[3]{0:T(128)}, u32[]{:S(2)}) copy-start(f32[3]{0:T(128)} %constant.118) | copy-start | bytes 40
  43.1 26.5 %collective-permute-start.8 = (f32[3,40,1,128]{3,1,2,0:T(8,128)S(1)}, f32[3,40,1,128]{3,1,2,0:T(8,128)S(1)}, u32[]{:S(2)}, u32[]{:S(2)}) collective-permute-start(f32[3,40,1,128]{3,1,2,0:T(8,128)S(1)} %get-tuple-element.78), channel_id=1, source_target_pairs={{1,0},{2,1},{3,2},{4,3},{5,4},{6,5},{7,6},{8,7},{9,8},{10,9},{11,1... | collective-permute-start | bytes 184328 | tf_op jit(solution)/shard_map/ppermute | solution.py:40
  51.8 17.7 %collective-permute-start.9 = (f32[3,40,1,128]{3,1,2,0:T(8,128)S(1)}, f32[3,40,1,128]{3,1,2,0:T(8,128)S(1)}, u32[]{:S(2)}, u32[]{:S(2)}) collective-permute-start(f32[3,40,1,128]{3,1,2,0:T(8,128)S(1)} %get-tuple-element.77), channel_id=1, source_target_pairs={{0,1},{1,2},{2,3},{3,4},{4,5},{5,6},{6,7},{7,8},{8,9},{9,10},{10,1... | collective-permute-start | bytes 184328 | tf_op jit(solution)/shard_map/ppermute | solution.py:39
  53.7 14.1 %collective-permute-start.5 = (f32[3,40,8,1]{3,1,2,0:T(8,128)S(1)}, f32[3,40,8,1]{3,1,2,0:T(8,128)S(1)}, u32[]{:S(2)}, u32[]{:S(2)}) collective-permute-start(f32[3,40,8,1]{3,1,2,0:T(8,128)S(1)} %get-tuple-element.76), channel_id=1, source_target_pairs={{0,16},{16,32},{32,48},{48,64},{64,80},{80,96},{96,112},{112,128},... | collective-permute-start | bytes 11528 | tf_op jit(solution)/shard_map/ppermute | solution.py:30
  55.6 13.9 %collective-permute-start.4 = (f32[3,40,8,1]{3,1,2,0:T(8,128)S(1)}, f32[3,40,8,1]{3,1,2,0:T(8,128)S(1)}, u32[]{:S(2)}, u32[]{:S(2)}) collective-permute-start(f32[3,40,8,1]{3,1,2,0:T(8,128)S(1)} %get-tuple-element.75), channel_id=1, source_target_pairs={{16,0},{32,16},{48,32},{64,48},{80,64},{96,80},{112,96},{128,112},... | collective-permute-start | bytes 11528 | tf_op jit(solution)/shard_map/ppermute | solution.py:31
  70.4 20.4 %collective-permute-start.6 = (f32[3,40,8,1]{3,1,2,0:T(8,128)S(1)}, f32[3,40,8,1]{3,1,2,0:T(8,128)S(1)}, u32[]{:S(2)}, u32[]{:S(2)}) collective-permute-start(f32[3,40,8,1]{3,1,2,0:T(8,128)S(1)} %get-tuple-element.70), channel_id=1, source_target_pairs={{16,0},{32,16},{48,32},{64,48},{80,64},{96,80},{112,96},{128,112},... | collective-permute-start | bytes 11528 | tf_op jit(solution)/shard_map/ppermute | solution.py:31
  78.2 16.9 %collective-permute-start.7 = (f32[3,40,8,1]{3,1,2,0:T(8,128)S(1)}, f32[3,40,8,1]{3,1,2,0:T(8,128)S(1)}, u32[]{:S(2)}, u32[]{:S(2)}) collective-permute-start(f32[3,40,8,1]{3,1,2,0:T(8,128)S(1)} %get-tuple-element.69), channel_id=1, source_target_pairs={{0,16},{16,32},{32,48},{48,64},{64,80},{80,96},{96,112},{112,128},... | collective-permute-start | bytes 11528 | tf_op jit(solution)/shard_map/ppermute | solution.py:30
  80.1 15.0 %collective-permute-start.10 = (f32[3,40,1,128]{3,1,2,0:T(8,128)S(1)}, f32[3,40,1,128]{3,1,2,0:T(8,128)S(1)}, u32[]{:S(2)}, u32[]{:S(2)}) collective-permute-start(f32[3,40,1,128]{3,1,2,0:T(8,128)S(1)} %get-tuple-element.66), channel_id=1, source_target_pairs={{1,0},{2,1},{3,2},{4,3},{5,4},{6,5},{7,6},{8,7},{9,8},{10,9},{11,1... | collective-permute-start | bytes 184328 | tf_op jit(solution)/shard_map/ppermute | solution.py:40
  88.9 10.9 %collective-permute-start.11 = (f32[3,40,1,128]{3,1,2,0:T(8,128)S(1)}, f32[3,40,1,128]{3,1,2,0:T(8,128)S(1)}, u32[]{:S(2)}, u32[]{:S(2)}) collective-permute-start(f32[3,40,1,128]{3,1,2,0:T(8,128)S(1)} %get-tuple-element.65), channel_id=1, source_target_pairs={{0,1},{1,2},{2,3},{3,4},{4,5},{5,6},{6,7},{7,8},{8,9},{9,10},{10,1... | collective-permute-start | bytes 184328 | tf_op jit(solution)/shard_map/ppermute | solution.py:39
  100.7 25.6 %collective-permute-start.14 = (f32[3,40,1,128]{3,1,2,0:T(8,128)S(1)}, f32[3,40,1,128]{3,1,2,0:T(8,128)S(1)}, u32[]{:S(2)}, u32[]{:S(2)}) collective-permute-start(f32[3,40,1,128]{3,1,2,0:T(8,128)S(1)} %get-tuple-element.59), channel_id=1, source_target_pairs={{1,0},{2,1},{3,2},{4,3},{5,4},{6,5},{7,6},{8,7},{9,8},{10,9},{11,1... | collective-permute-start | bytes 184328 | tf_op jit(solution)/shard_map/ppermute | solution.py:40
  103.5 22.8 %collective-permute-start.15 = (f32[3,40,1,128]{3,1,2,0:T(8,128)S(1)}, f32[3,40,1,128]{3,1,2,0:T(8,128)S(1)}, u32[]{:S(2)}, u32[]{:S(2)}) collective-permute-start(f32[3,40,1,128]{3,1,2,0:T(8,128)S(1)} %get-tuple-element.58), channel_id=1, source_target_pairs={{0,1},{1,2},{2,3},{3,4},{4,5},{5,6},{6,7},{7,8},{8,9},{9,10},{10,1... | collective-permute-start | bytes 184328 | tf_op jit(solution)/shard_map/ppermute | solution.py:39
  110.5 14.1 %collective-permute-start.13 = (f32[3,40,8,1]{3,1,2,0:T(8,128)S(1)}, f32[3,40,8,1]{3,1,2,0:T(8,128)S(1)}, u32[]{:S(2)}, u32[]{:S(2)}) collective-permute-start(f32[3,40,8,1]{3,1,2,0:T(8,128)S(1)} %get-tuple-element.57), channel_id=1, source_target_pairs={{0,16},{16,32},{32,48},{48,64},{64,80},{80,96},{96,112},{112,128},... | collective-permute-start | bytes 11528 | tf_op jit(solution)/shard_map/ppermute | solution.py:30
  112.4 13.9 %collective-permute-start.12 = (f32[3,40,8,1]{3,1,2,0:T(8,128)S(1)}, f32[3,40,8,1]{3,1,2,0:T(8,128)S(1)}, u32[]{:S(2)}, u32[]{:S(2)}) collective-permute-start(f32[3,40,8,1]{3,1,2,0:T(8,128)S(1)} %get-tuple-element.56), channel_id=1, source_target_pairs={{16,0},{32,16},{48,32},{64,48},{80,64},{96,80},{112,96},{128,112},... | collective-permute-start | bytes 11528 | tf_op jit(solution)/shard_map/ppermute | solution.py:31
  126.8 0.8 copy-start.2
  131.6 5.6 %copy-start.14 = (pred[256]{0:T(512)(128)(4,1)S(1)}, pred[256]{0:T(512)(128)(4,1)}, u32[]{:S(2)}) copy-start(pred[256]{0:T(512)(128)(4,1)} %compare_and_fusion) | copy-start | bytes 772
  137.8 18.8 %collective-permute-start.17 = (f32[256,40]{0,1:T(8,128)}, f32[256,40]{0,1:T(8,128)}, u32[]{:S(2)}, u32[]{:S(2)}) collective-permute-start(f32[256,40]{0,1:T(8,128)} %broadcast_select_fusion), channel_id=1, source_target_pairs={{0,496},{16,0},{32,16},{48,32},{64,48},{80,64},{96,80},{112,96},{1... | collective-permute-start | bytes 122888 | tf_op jit(solution)/shard_map/ppermute | solution.py:117
  145.5 11.1 %collective-permute-start.16 = (f32[256,40]{0,1:T(8,128)}, f32[256,40]{0,1:T(8,128)}, u32[]{:S(2)}, u32[]{:S(2)}) collective-permute-start(f32[256,40]{0,1:T(8,128)} %broadcast_select_fusion), channel_id=1, source_target_pairs={{0,16},{16,32},{32,48},{48,64},{64,80},{80,96},{96,112},{112,128},... | collective-permute-start | bytes 122888 | tf_op jit(solution)/shard_map/ppermute | solution.py:116
  151.6 5.1 %copy-start.15 = (pred[256]{0:T(512)(128)(4,1)S(1)}, pred[256]{0:T(512)(128)(4,1)}, u32[]{:S(2)}) copy-start(pred[256]{0:T(512)(128)(4,1)} %compare_and_fusion) | copy-start | bytes 772
  151.6 15.6 %copy-start.3 = (f32[3,40,8,128]{3,1,2,0:T(8,128)S(1)}, f32[3,40,8,128]{3,1,2,0:T(8,128)}, u32[]{:S(2)}) copy-start(f32[3,40,8,128]{3,1,2,0:T(8,128)} %copy-done.2) | copy-start | bytes 1474564
  151.6 20.3 %copy-start.20 = (f32[256]{0:T(256)S(1)}, f32[256]{0:T(256)}, u32[]{:S(2)}) copy-start(f32[256]{0:T(256)} %get-tuple-element.21) | copy-start | bytes 3076
  151.6 20.3 %copy-start.7 = (s32[256]{0:T(256)S(1)}, s32[256]{0:T(256)}, u32[]{:S(2)}) copy-start(s32[256]{0:T(256)} %copy-done.6) | copy-start | bytes 3076
  151.6 20.3 %copy-start.9 = (s32[256]{0:T(256)S(1)}, s32[256]{0:T(256)}, u32[]{:S(2)}) copy-start(s32[256]{0:T(256)} %copy-done.8) | copy-start | bytes 3076
  151.6 20.3 %copy-start.11 = (s32[256]{0:T(256)S(1)}, s32[256]{0:T(256)}, u32[]{:S(2)}) copy-start(s32[256]{0:T(256)} %copy-done.10) | copy-start | bytes 3076
  151.6 20.3 %copy-start.13 = (s32[256]{0:T(256)S(1)}, s32[256]{0:T(256)}, u32[]{:S(2)}) copy-start(s32[256]{0:T(256)} %copy-done.12) | copy-start | bytes 3076
  151.6 20.3 %copy-start.16 = (f32[256]{0:T(256)S(1)}, f32[256]{0:T(256)}, u32[]{:S(2)}) copy-start(f32[256]{0:T(256)} %get-tuple-element.24) | copy-start | bytes 3076
  156.6 15.9 %copy-start.19 = (f32[256]{0:T(256)S(1)}, f32[256]{0:T(256)}, u32[]{:S(2)}) copy-start(f32[256]{0:T(256)} %get-tuple-element.20) | copy-start | bytes 3076
  156.6 15.9 %copy-start.22 = (pred[256]{0:T(512)(128)(4,1)S(1)}, pred[256]{0:T(512)(128)(4,1)}, u32[]{:S(2)}) copy-start(pred[256]{0:T(512)(128)(4,1)} %compare_and_fusion.1) | copy-start | bytes 772
  157.4 10.9 %collective-permute-start.19 = (f32[256,40]{0,1:T(8,128)S(1)}, f32[256,40]{0,1:T(8,128)S(1)}, u32[]{:S(2)}, u32[]{:S(2)}) collective-permute-start(f32[256,40]{0,1:T(8,128)S(1)} %add_add_fusion.5), channel_id=1, source_target_pairs={{1,0},{2,1},{3,2},{4,3},{5,4},{6,5},{7,6},{8,7},{9,8},{10,9},{11,1... | collective-permute-start | bytes 122888 | tf_op jit(solution)/shard_map/ppermute | solution.py:122
  161.1 10.7 %collective-permute-start.18 = (f32[256,40]{0,1:T(8,128)S(1)}, f32[256,40]{0,1:T(8,128)S(1)}, u32[]{:S(2)}, u32[]{:S(2)}) collective-permute-start(f32[256,40]{0,1:T(8,128)S(1)} %add_add_fusion.5), channel_id=1, source_target_pairs={{0,1},{1,2},{2,3},{3,4},{4,5},{5,6},{6,7},{7,8},{8,9},{9,10},{10,1... | collective-permute-start | bytes 122888 | tf_op jit(solution)/shard_map/ppermute | solution.py:121
  171.9 10.4 %copy-start = (f32[256,1024]{0,1:T(8,128)S(1)}, f32[256,1024]{0,1:T(8,128)}, u32[]{:S(2)}) copy-start(f32[256,1024]{0,1:T(8,128)} %get-tuple-element.85) | copy-start | bytes 3145732
  172.7 11.3 %collective-permute-start.21 = (f32[256,40]{0,1:T(8,128)S(1)}, f32[256,40]{0,1:T(8,128)S(1)}, u32[]{:S(2)}, u32[]{:S(2)}) collective-permute-start(f32[256,40]{0,1:T(8,128)S(1)} %fusion.28), channel_id=1, source_target_pairs={{0,496},{16,0},{32,16},{48,32},{64,48},{80,64},{96,80},{112,96},{1... | collective-permute-start | bytes 122888 | tf_op jit(solution)/shard_map/ppermute | solution.py:224
  178.8 9.7 %collective-permute-start.20 = (f32[256,40]{0,1:T(8,128)S(1)}, f32[256,40]{0,1:T(8,128)S(1)}, u32[]{:S(2)}, u32[]{:S(2)}) collective-permute-start(f32[256,40]{0,1:T(8,128)S(1)} %fusion.28), channel_id=1, source_target_pairs={{0,16},{16,32},{32,48},{48,64},{64,80},{80,96},{96,112},{112,128},... | collective-permute-start | bytes 122888 | tf_op jit(solution)/shard_map/ppermute | solution.py:223
  182.3 16.2 %copy-start.5 = (f32[6,40,8,128]{3,1,2,0:T(8,128)S(1)}, f32[6,40,8,128]{3,1,2,0:T(8,128)}, u32[]{:S(2)}) copy-start(f32[6,40,8,128]{3,1,2,0:T(8,128)} %pad_maximum_fusion.1) | copy-start | bytes 2949124
  188.5 17.2 %collective-permute-start.23 = (f32[256,40]{0,1:T(8,128)S(1)}, f32[256,40]{0,1:T(8,128)S(1)}, u32[]{:S(2)}, u32[]{:S(2)}) collective-permute-start(f32[256,40]{0,1:T(8,128)S(1)} %add_add_fusion.3), channel_id=1, source_target_pairs={{1,0},{2,1},{3,2},{4,3},{5,4},{6,5},{7,6},{8,7},{9,8},{10,9},{11,1... | collective-permute-start | bytes 122888 | tf_op jit(solution)/shard_map/ppermute | solution.py:231
  190.9 14.9 %collective-permute-start.22 = (f32[256,40]{0,1:T(8,128)S(1)}, f32[256,40]{0,1:T(8,128)S(1)}, u32[]{:S(2)}, u32[]{:S(2)}) collective-permute-start(f32[256,40]{0,1:T(8,128)S(1)} %add_add_fusion.3), channel_id=1, source_target_pairs={{0,1},{1,2},{2,3},{3,4},{4,5},{5,6},{6,7},{7,8},{8,9},{9,10},{10,1... | collective-permute-start | bytes 122888 | tf_op jit(solution)/shard_map/ppermute | solution.py:230
  203.2 2.6 %copy-start.18 = (f32[256]{0:T(256)S(1)}, f32[256]{0:T(256)}, u32[]{:S(2)}) copy-start(f32[256]{0:T(256)} %get-tuple-element.19) | copy-start | bytes 3076
  205.6 1.7 copy-start.17
  207.3 1.6 copy-start.4
where the time goes:
time: 217 us; the launch traced here: 216 us
  starting transfers between devices  120 us (55%)
  waiting for transfers between devices  29.5 us (14%)
  other arithmetic  23.9 us (11%)
  local copies, waits for them, and re-layouts  22.3 us (10%)
  matrix products  19.4 us (9%)
    ppermute x4, starting transfers between devices, lon_edges(): right = lax.ppermute(array[..., :1], 'lon', down)  31 us
    ppermute x4, starting transfers between devices, lat_edges(): after = lax.ppermute(array[:, :, :1, :], 'lat', down)  30.4 us
    ppermute x4, waiting for transfers between devices, lon_edges(): left = lax.ppermute(array[..., -1:], 'lon', up)  13.3 us
    ppermute x4, starting transfers between devices, lat_edges(): before = lax.ppermute(array[:, :, -1:, :], 'lat', up)  12.9 us
    dot_general x6, matrix products, update_group(): jnp.einsum('om,foc->fmc', gains, covariance * weights[None], precision=la...  10.1 us
    dot_general x6, matrix products, update_group(): jnp.einsum('om,fmc->foc', anomaly, deviation, precision=lax.Precision.HIGH)  8.6 us
    gather x2, local copies, waits for them, and re-layouts, at_owner(): rows = state[kind_obs, :, nearby_latitude, :]  7.85 us
    ppermute x1, starting transfers between devices, neighbourhood_sum(): lax.ppermute(table, 'lon', ring_pairs(lon_n, -1))  7.71 us
  transfers between devices with their start and end apart: 24, of which 8 were waited for; matrix products, arithmetic and copies ran while one was open for 17% of the time, Pallas kernels for 0%

commit v1 on v0

--- a/solution.py
+++ b/solution.py
@@ -199,40 +199,45 @@
         state = march_prediction(state, rotation_frequency)
 
     (lon0, lat0, kind0, radius0), (value0, error0) = batches[0]
-    values, owned = at_owner(state, lon0, lat0, kind0)
-    priors = neighbourhood_sum(jnp.where(owned[:, None], values, 0.0))
-    for batch_index in range(BATCHES):
-        (lon_b, lat_b, kind_b, radius_b), (value_b, error_b) = batches[batch_index]
-        gains, anomaly = statistics(priors, value_b, error_b, member_count)
-        if batch_index + 1 < BATCHES:
-            (lon_n, lat_n, kind_n, _), _ = batches[batch_index + 1]
-            values, owned = at_owner(state, lon_n, lat_n, kind_n)
-            deviation = values - jnp.mean(values, axis=1, keepdims=True)
-            covariance = jnp.einsum(
-                "om,jm->oj", anomaly, deviation, precision=lax.Precision.HIGH
-            ) / (member_count - 1)
-            weights = localize(lon_n, lat_n, lon_b, lat_b, radius_b, grid_lon)
-            increment = jnp.einsum(
-                "om,oj->jm", gains, covariance * weights, precision=lax.Precision.HIGH
-            )
-            table = jnp.where(owned[:, None], values + increment, 0.0)
-            weights = tile_weights(state, lon_b, lat_b, radius_b)
-            table, head = lax.optimization_barrier((table, state[0:3]))
-            row = (
-                table
-                + lax.ppermute(table, "lon", ring_pairs(lon_size, 1))
-                + lax.ppermute(table, "lon", ring_pairs(lon_size, -1))
-            )
-            head = update(head, gains, anomaly, weights)
-            row, tail, head = lax.optimization_barrier((row, state[3:], head))
-            priors = (
-                row
-                + lax.ppermute(row, "lat", line_pairs(lat_size, 1))
-                + lax.ppermute(row, "lat", line_pairs(lat_size, -1))
-            )
-            state = jnp.concatenate([head, update(tail, gains, anomaly, weights)])
-        else:
-            state = update(state, gains, anomaly, tile_weights(state, lon_b, lat_b, radius_b))
+    (lon1, lat1, kind1, radius1), (value1, error1) = batches[1]
+    values0, owned0 = at_owner(state, lon0, lat0, kind0)
+    values1, owned1 = at_owner(state, lon1, lat1, kind1)
+    table0 = jnp.where(owned0[:, None], values0, 0.0)
+    table1 = jnp.where(owned1[:, None], values1, 0.0)
+    both = jnp.concatenate([table0, table1])
+    both = (
+        both
+        + lax.ppermute(both, "lon", ring_pairs(lon_size, 1))
+        + lax.ppermute(both, "lon", ring_pairs(lon_size, -1))
+    )
+    wide0 = (
+        both[:NB]
+        + lax.ppermute(table0, "lon", ring_pairs(lon_size, 2))
+        + lax.ppermute(table0, "lon", ring_pairs(lon_size, -2))
+    )
+    both = jnp.concatenate([wide0, both[NB:]])
+    both = (
+        both
+        + lax.ppermute(both, "lat", line_pairs(lat_size, 1))
+        + lax.ppermute(both, "lat", line_pairs(lat_size, -1))
+    )
+    priors = (
+        both[:NB]
+        + lax.ppermute(wide0, "lat", line_pairs(lat_size, 2))
+        + lax.ppermute(wide0, "lat", line_pairs(lat_size, -2))
+    )
+    raw1 = both[NB:]
+    gains, anomaly = statistics(priors, value0, error0, member_count)
+    deviation = raw1 - jnp.mean(raw1, axis=1, keepdims=True)
+    covariance = jnp.einsum(
+        "om,jm->oj", anomaly, deviation, precision=lax.Precision.HIGH
+    ) / (member_count - 1)
+    weights = localize(lon1, lat1, lon0, lat0, radius0, grid_lon)
+    increment = jnp.einsum("om,oj->jm", gains, covariance * weights, precision=lax.Precision.HIGH)
+    priors1 = raw1 + increment
+    state = update(state, gains, anomaly, tile_weights(state, lon0, lat0, radius0))
+    gains, anomaly = statistics(priors1, value1, error1, member_count)
+    state = update(state, gains, anomaly, tile_weights(state, lon1, lat1, radius1))
     return state.astype(jnp.bfloat16)
 
 

time: 217 us -> 213 us (0.982)
  waiting for transfers between devices: 29.5 us -> 24.5 us
  starting transfers between devices: 120 us -> 123 us
  other arithmetic: 23.9 us -> 21.7 us
    ppermute x8, starting transfers between devices: 37.6 us -> 45.7 us  [the longest x1 10.3 us: shards(): lax.ppermute(wide0, 'lat', line_pairs(lat_size, -2))]
    reduce_sum x1 -> x0, other arithmetic: 4.94 us -> none  [shards(): deviation = values - jnp.mean(values, axis=1, keepdims=True)]
    reduce_sum x1 -> x2, other arithmetic: 4.58 us -> 8.51 us  [at_owner(): values = jnp.sum(jnp.where(pick[:, None, :], rows, 0.0), axis=2)]
    ppermute x4, starting transfers between devices: 31 us -> 27.5 us  [lon_edges(): right = lax.ppermute(array[..., :1], 'lon', down)]
    ppermute x4, waiting for transfers between devices: 3.52 us -> 0.01 us  [lon_edges(): right = lax.ppermute(array[..., :1], 'lon', down)]
    ppermute x4, starting transfers between devices: 30.4 us -> 27.7 us  [lat_edges(): after = lax.ppermute(array[:, :, :1, :], 'lat', down)]
    ppermute x8, waiting for transfers between devices: 8.04 us -> 5.86 us  [the longest x1 2.73 us: shards(): lax.ppermute(wide0, 'lat', line_pairs(lat_size, -2))]
    unnamed x74 -> x72, local copies, waits for them, and re-layouts: 5.28 us -> 5.8 us
  transfers between devices with their start and end apart: 24 -> 24, of which waited for: 8 -> 8; matrix products, arithmetic and copies ran while one was open for 17% -> 8% of each run, Pallas kernels for 0% -> 0%
where the time goes in v1:
time: 213 us; the launch traced here: 212 us
  starting transfers between devices  123 us (58%)
  waiting for transfers between devices  24.5 us (12%)
  local copies, waits for them, and re-layouts  22.7 us (11%)
  other arithmetic  21.7 us (10%)
  matrix products  18.9 us (9%)
    ppermute x4, starting transfers between devices, lat_edges(): after = lax.ppermute(array[:, :, :1, :], 'lat', down)  27.7 us
    ppermute x4, starting transfers between devices, lon_edges(): right = lax.ppermute(array[..., :1], 'lon', down)  27.5 us
    ppermute x4, waiting for transfers between devices, lon_edges(): left = lax.ppermute(array[..., -1:], 'lon', up)  15.3 us
    ppermute x4, starting transfers between devices, lat_edges(): before = lax.ppermute(array[:, :, -1:, :], 'lat', up)  14.6 us
    ppermute x1, starting transfers between devices, shards(): lax.ppermute(wide0, 'lat', line_pairs(lat_size, -2))  10.3 us
    dot_general x6, matrix products, update_group(): jnp.einsum('om,foc->fmc', gains, covariance * weights[None], precision=la...  9.37 us
    dot_general x6, matrix products, update_group(): jnp.einsum('om,fmc->foc', anomaly, deviation, precision=lax.Precision.HIGH)  8.88 us
    reduce_sum x2, other arithmetic, at_owner(): values = jnp.sum(jnp.where(pick[:, None, :], rows, 0.0), axis=2)  8.51 us
  transfers between devices with their start and end apart: 24, of which 8 were waited for; matrix products, arithmetic and copies ran while one was open for 8% of the time, Pallas kernels for 0%

profile of v1, /device:TPU:24, one launch (start us, length us, event | category | flops | bytes accessed | tf_op | source)
XLA Modules:
  0.0 212.2 jit_solution(5590321152808422886)
XLA Ops:
  0.0 1.5 fusion.137
  1.5 0.9 copy.89
  2.4 8.2 %collective-permute-start = (f32[3,40,8,1]{3,1,2,0:T(8,128)}, f32[3,40,8,1]{3,1,2,0:T(8,128)}, u32[]{:S(2)}, u32[]{:S(2)}) collective-permute-start(f32[3,40,8,1]{3,1,2,0:T(8,128)} %copy.89), channel_id=1, source_target_pairs={{16,0},{32,16},{48,32},{64,48},{80,64},{96,80},{112,96},{128,112},... | collective-permute-start | bytes 11528 | tf_op jit(solution)/shard_map/ppermute | solution.py:31
  10.5 0.9 copy.90
  11.4 1.9 collective-permute-start.1
  14.1 10.2 %collective-permute-start.2 = (f32[3,40,1,128]{3,1,2,0:T(8,128)}, f32[3,40,1,128]{3,1,2,0:T(8,128)}, u32[]{:S(2)}, u32[]{:S(2)}) collective-permute-start(f32[3,40,1,128]{3,1,2,0:T(8,128)} %bitcast.28), channel_id=1, source_target_pairs={{1,0},{2,1},{3,2},{4,3},{5,4},{6,5},{7,6},{8,7},{9,8},{10,9},{11,1... | collective-permute-start | bytes 184328 | tf_op jit(solution)/shard_map/ppermute | solution.py:40
  24.3 2.1 collective-permute-start.3
  26.5 1.1 fusion.138
  28.5 1.0 gather_fusion
  30.1 0.8 fusion.79
  33.1 1.0 gather_fusion.3
  34.1 0.9 slice_reduce_fusion.1
  35.1 3.4 %multiply_multiply_fusion = (f32[256,1024]{0,1:T(8,128)S(1)}, f32[256,1024]{0,1:T(8,128)}) fusion(f32[256]{0:T(256)} %get-tuple-element.9, s32[256]{0:T(256)} %copy-done.11, s32[256]{0:T(256)S(1)} %get-tuple-element.15, s32[1024]{0:T(1024)} %get-tuple-element.92, s32[1024]{0:T(1024)} %get-tuple-element.93, f32[256]{0:T(256)} %get-tuple-element.10, ...), kind=kLoop, calls=%fused_computation.67 | loop fusion | flops 12582912 | bytes 2111488 | tf_op jit(solution)/shard_map/mul | solution.py:162
  38.5 1.1 copy.88
  39.6 1.1 copy.91
  41.0 1.6 fusion.45
  43.1 7.3 %collective-permute-start.4 = (f32[3,40,8,1]{3,1,2,0:T(8,128)S(1)}, f32[3,40,8,1]{3,1,2,0:T(8,128)S(1)}, u32[]{:S(2)}, u32[]{:S(2)}) collective-permute-start(f32[3,40,8,1]{3,1,2,0:T(8,128)S(1)} %get-tuple-element.61), channel_id=1, source_target_pairs={{16,0},{32,16},{48,32},{64,48},{80,64},{96,80},{112,96},{128,112},... | collective-permute-start | bytes 11528 | tf_op jit(solution)/shard_map/ppermute | solution.py:31
  50.4 1.9 collective-permute-start.5
  52.3 8.4 %collective-permute-start.8 = (f32[3,40,1,128]{3,1,2,0:T(8,128)S(1)}, f32[3,40,1,128]{3,1,2,0:T(8,128)S(1)}, u32[]{:S(2)}, u32[]{:S(2)}) collective-permute-start(f32[3,40,1,128]{3,1,2,0:T(8,128)S(1)} %get-tuple-element.64), channel_id=1, source_target_pairs={{1,0},{2,1},{3,2},{4,3},{5,4},{6,5},{7,6},{8,7},{9,8},{10,9},{11,1... | collective-permute-start | bytes 184328 | tf_op jit(solution)/shard_map/ppermute | solution.py:40
  60.8 1.9 collective-permute-start.9
  62.8 5.6 %collective-permute-done.5 = f32[3,40,8,1]{3,1,2,0:T(8,128)S(1)} collective-permute-done((f32[3,40,8,1]{3,1,2,0:T(8,128)S(1)}, f32[3,40,8,1]{3,1,2,0:T(8,128)S(1)}, u32[]{:S(2)}, u32[]{:S(2)}) %collective-permute-start.5) | collective-permute-done | bytes 3872 | tf_op jit(solution)/shard_map/ppermute | solution.py:30
  68.4 3.3 %collective-permute-done.9 = f32[3,40,1,128]{3,1,2,0:T(8,128)S(1)} collective-permute-done((f32[3,40,1,128]{3,1,2,0:T(8,128)S(1)}, f32[3,40,1,128]{3,1,2,0:T(8,128)S(1)}, u32[]{:S(2)}, u32[]{:S(2)}) %collective-permute-start.9) | collective-permute-done | bytes 61472 | tf_op jit(solution)/shard_map/ppermute | solution.py:39
  72.6 6.1 %collective-permute-start.6 = (f32[3,40,8,1]{3,1,2,0:T(8,128)S(1)}, f32[3,40,8,1]{3,1,2,0:T(8,128)S(1)}, u32[]{:S(2)}, u32[]{:S(2)}) collective-permute-start(f32[3,40,8,1]{3,1,2,0:T(8,128)S(1)} %get-tuple-element.53), channel_id=1, source_target_pairs={{16,0},{32,16},{48,32},{64,48},{80,64},{96,80},{112,96},{128,112},... | collective-permute-start | bytes 11528 | tf_op jit(solution)/shard_map/ppermute | solution.py:31
  78.7 1.9 collective-permute-start.7
  80.7 3.7 %collective-permute-start.10 = (f32[3,40,1,128]{3,1,2,0:T(8,128)S(1)}, f32[3,40,1,128]{3,1,2,0:T(8,128)S(1)}, u32[]{:S(2)}, u32[]{:S(2)}) collective-permute-start(f32[3,40,1,128]{3,1,2,0:T(8,128)S(1)} %get-tuple-element.57), channel_id=1, source_target_pairs={{1,0},{2,1},{3,2},{4,3},{5,4},{6,5},{7,6},{8,7},{9,8},{10,9},{11,1... | collective-permute-start | bytes 184328 | tf_op jit(solution)/shard_map/ppermute | solution.py:40
  84.3 6.1 %collective-permute-start.11 = (f32[3,40,1,128]{3,1,2,0:T(8,128)S(1)}, f32[3,40,1,128]{3,1,2,0:T(8,128)S(1)}, u32[]{:S(2)}, u32[]{:S(2)}) collective-permute-start(f32[3,40,1,128]{3,1,2,0:T(8,128)S(1)} %get-tuple-element.58), channel_id=1, source_target_pairs={{0,1},{1,2},{2,3},{3,4},{4,5},{5,6},{6,7},{7,8},{8,9},{9,10},{10,1... | collective-permute-start | bytes 184328 | tf_op jit(solution)/shard_map/ppermute | solution.py:39
  90.5 4.9 %collective-permute-done.7 = f32[3,40,8,1]{3,1,2,0:T(8,128)S(1)} collective-permute-done((f32[3,40,8,1]{3,1,2,0:T(8,128)S(1)}, f32[3,40,8,1]{3,1,2,0:T(8,128)S(1)}, u32[]{:S(2)}, u32[]{:S(2)}) %collective-permute-start.7) | collective-permute-done | bytes 3872 | tf_op jit(solution)/shard_map/ppermute | solution.py:30
  96.5 5.9 %collective-permute-start.12 = (f32[3,40,8,1]{3,1,2,0:T(8,128)S(1)}, f32[3,40,8,1]{3,1,2,0:T(8,128)S(1)}, u32[]{:S(2)}, u32[]{:S(2)}) collective-permute-start(f32[3,40,8,1]{3,1,2,0:T(8,128)S(1)} %get-tuple-element.42), channel_id=1, source_target_pairs={{16,0},{32,16},{48,32},{64,48},{80,64},{96,80},{112,96},{128,112},... | collective-permute-start | bytes 11528 | tf_op jit(solution)/shard_map/ppermute | solution.py:31
  102.4 1.9 collective-permute-start.13
  104.3 5.4 %collective-permute-start.14 = (f32[3,40,1,128]{3,1,2,0:T(8,128)S(1)}, f32[3,40,1,128]{3,1,2,0:T(8,128)S(1)}, u32[]{:S(2)}, u32[]{:S(2)}) collective-permute-start(f32[3,40,1,128]{3,1,2,0:T(8,128)S(1)} %get-tuple-element.46), channel_id=1, source_target_pairs={{1,0},{2,1},{3,2},{4,3},{5,4},{6,5},{7,6},{8,7},{9,8},{10,9},{11,1... | collective-permute-start | bytes 184328 | tf_op jit(solution)/shard_map/ppermute | solution.py:40
  109.8 4.5 %collective-permute-start.15 = (f32[3,40,1,128]{3,1,2,0:T(8,128)S(1)}, f32[3,40,1,128]{3,1,2,0:T(8,128)S(1)}, u32[]{:S(2)}, u32[]{:S(2)}) collective-permute-start(f32[3,40,1,128]{3,1,2,0:T(8,128)S(1)} %get-tuple-element.47), channel_id=1, source_target_pairs={{0,1},{1,2},{2,3},{3,4},{4,5},{5,6},{6,7},{7,8},{8,9},{9,10},{10,1... | collective-permute-start | bytes 184328 | tf_op jit(solution)/shard_map/ppermute | solution.py:39
  114.9 4.7 %collective-permute-done.13 = f32[3,40,8,1]{3,1,2,0:T(8,128)S(1)} collective-permute-done((f32[3,40,8,1]{3,1,2,0:T(8,128)S(1)}, f32[3,40,8,1]{3,1,2,0:T(8,128)S(1)}, u32[]{:S(2)}, u32[]{:S(2)}) %collective-permute-start.13) | collective-permute-done | bytes 3872 | tf_op jit(solution)/shard_map/ppermute | solution.py:30
  119.6 1.0 fusion.127
  120.7 0.8 fusion.131
  121.5 0.8 copy-done.2
  122.4 3.9 %gather_fusion.1 = f32[256,40,128]{2,1,0:T(8,128)} fusion(f32[9,40,8,128]{3,1,2,0:T(8,128)S(1)} %pad_maximum_fusion, s32[256]{0:T(256)S(1)} %bitcast.197), kind=kCustom, calls=%fused_computation.1 | custom fusion | bytes 10487808 | tf_op jit(solution)/shard_map/gather | solution.py:142
  126.3 4.6 %select_reduce_fusion.1 = f32[256,40]{1,0:T(8,128)} fusion(f32[256,40,128]{2,1,0:T(8,128)} %gather_fusion.1, pred[256,128]{1,0:T(8,128)(4,1)S(1)} %iota_compare_fusion.1), kind=kLoop, calls=%fused_computation.5 | loop fusion | flops 2611200 | bytes 5316608 | tf_op jit(solution)/shard_map/reduce_sum | solution.py:144
  130.9 1.0 copy.70
  131.9 3.9 %gather_fusion.2 = f32[256,40,128]{2,1,0:T(8,128)} fusion(f32[9,40,8,128]{3,1,2,0:T(8,128)S(1)} %pad_maximum_fusion, s32[256]{0:T(256)S(1)} %bitcast.196), kind=kCustom, calls=%fused_computation.2 | custom fusion | bytes 10487808 | tf_op jit(solution)/shard_map/gather | solution.py:142
  135.8 3.9 %select_reduce_fusion = f32[256,40]{1,0:T(8,128)S(1)} fusion(f32[256,40,128]{2,1,0:T(8,128)} %gather_fusion.2, pred[256,128]{1,0:T(8,128)(4,1)} %iota_compare_fusion), kind=kLoop, calls=%fused_computation.4 | loop fusion | flops 2611200 | bytes 5316608 | tf_op jit(solution)/shard_map/reduce_sum | solution.py:144
  139.9 2.1 collective-permute-start.16
  142.0 7.5 %collective-permute-start.17 = (f32[512,40]{0,1:T(8,128)S(1)}, f32[512,40]{0,1:T(8,128)S(1)}, u32[]{:S(2)}, u32[]{:S(2)}) collective-permute-start(f32[512,40]{0,1:T(8,128)S(1)} %pad_maximum_fusion.4), channel_id=1, source_target_pairs={{0,496},{16,0},{32,16},{48,32},{64,48},{80,64},{96,80},{112,96},{1... | collective-permute-start | bytes 245768 | tf_op jit(solution)/shard_map/ppermute | solution.py:211
  149.6 1.9 collective-permute-start.18
  151.5 7.8 %collective-permute-start.19 = (f32[256,40]{0,1:T(8,128)S(1)}, f32[256,40]{0,1:T(8,128)S(1)}, u32[]{:S(2)}, u32[]{:S(2)}) collective-permute-start(f32[256,40]{0,1:T(8,128)S(1)} %broadcast_select_fusion.1), channel_id=1, source_target_pairs={{0,480},{16,496},{32,0},{48,16},{64,32},{80,48},{96,64},{112,80},{... | collective-permute-start | bytes 122888 | tf_op jit(solution)/shard_map/ppermute | solution.py:216
  159.4 1.6 collective-permute-done.19
  161.0 4.2 %collective-permute-start.20 = (f32[512,40]{0,1:T(8,128)S(1)}, f32[512,40]{0,1:T(8,128)S(1)}, u32[]{:S(2)}, u32[]{:S(2)}) collective-permute-start(f32[512,40]{0,1:T(8,128)S(1)} %pad_maximum_fusion.5), channel_id=1, source_target_pairs={{0,1},{1,2},{2,3},{3,4},{4,5},{5,6},{6,7},{7,8},{8,9},{9,10},{10,1... | collective-permute-start | bytes 245768 | tf_op jit(solution)/shard_map/ppermute | solution.py:221
  165.2 6.4 %collective-permute-start.21 = (f32[512,40]{0,1:T(8,128)S(1)}, f32[512,40]{0,1:T(8,128)S(1)}, u32[]{:S(2)}, u32[]{:S(2)}) collective-permute-start(f32[512,40]{0,1:T(8,128)S(1)} %pad_maximum_fusion.5), channel_id=1, source_target_pairs={{1,0},{2,1},{3,2},{4,3},{5,4},{6,5},{7,6},{8,7},{9,8},{10,9},{11,1... | collective-permute-start | bytes 245768 | tf_op jit(solution)/shard_map/ppermute | solution.py:222
  171.7 5.3 %collective-permute-start.22 = (f32[256,40]{0,1:T(8,128)S(1)}, f32[256,40]{0,1:T(8,128)S(1)}, u32[]{:S(2)}, u32[]{:S(2)}) collective-permute-start(f32[256,40]{0,1:T(8,128)S(1)} %get-tuple-element.72), channel_id=1, source_target_pairs={{0,2},{1,3},{2,4},{3,5},{4,6},{5,7},{6,8},{7,9},{8,10},{9,11},{10,... | collective-permute-start | bytes 122888 | tf_op jit(solution)/shard_map/ppermute | solution.py:226
  177.1 10.3 %collective-permute-start.23 = (f32[256,40]{0,1:T(8,128)S(1)}, f32[256,40]{0,1:T(8,128)S(1)}, u32[]{:S(2)}, u32[]{:S(2)}) collective-permute-start(f32[256,40]{0,1:T(8,128)S(1)} %get-tuple-element.72), channel_id=1, source_target_pairs={{2,0},{3,1},{4,2},{5,3},{6,4},{7,5},{8,6},{9,7},{10,8},{11,9},{12,... | collective-permute-start | bytes 122888 | tf_op jit(solution)/shard_map/ppermute | solution.py:227
  187.5 1.5 collective-permute-done.22
  189.0 2.7 %collective-permute-done.23 = f32[256,40]{0,1:T(8,128)S(1)} collective-permute-done((f32[256,40]{0,1:T(8,128)S(1)}, f32[256,40]{0,1:T(8,128)S(1)}, u32[]{:S(2)}, u32[]{:S(2)}) %collective-permute-start.23) | collective-permute-done | bytes 40992 | tf_op jit(solution)/shard_map/ppermute | solution.py:227
  191.8 1.4 fusion.42
  193.4 1.5 fusion.155
  195.7 1.4 fusion.61
  197.2 1.6 fusion.24
  198.8 1.4 fusion.41
  200.3 1.5 fusion.154
  201.8 1.4 fusion.59
  203.3 1.6 fusion.25
  204.9 1.7 fusion.40
  206.6 1.5 fusion.152
  208.2 1.4 fusion.57
  209.6 1.6 fusion.26
  211.3 0.9 pad_maximum_fusion.1
  (146 shorter events, 9.1 us)
Async XLA Ops:
  0.0 13.3 %copy-start.1 = (f32[9,40,8,128]{3,2,1,0:T(8,128)S(1)}, f32[9,40,8,128]{3,2,1,0:T(8,128)}, u32[]{:S(2)}) copy-start(f32[9,40,8,128]{3,2,1,0:T(8,128)} %param.10) | copy-start | bytes 4423684
  2.4 38.6 %collective-permute-start = (f32[3,40,8,1]{3,1,2,0:T(8,128)}, f32[3,40,8,1]{3,1,2,0:T(8,128)}, u32[]{:S(2)}, u32[]{:S(2)}) collective-permute-start(f32[3,40,8,1]{3,1,2,0:T(8,128)} %copy.89), channel_id=1, source_target_pairs={{16,0},{32,16},{48,32},{64,48},{80,64},{96,80},{112,96},{128,112},... | collective-permute-start | bytes 11528 | tf_op jit(solution)/shard_map/ppermute | solution.py:31
  11.4 29.6 %collective-permute-start.1 = (f32[3,40,8,1]{3,1,2,0:T(8,128)}, f32[3,40,8,1]{3,1,2,0:T(8,128)}, u32[]{:S(2)}, u32[]{:S(2)}) collective-permute-start(f32[3,40,8,1]{3,1,2,0:T(8,128)} %copy.90), channel_id=1, source_target_pairs={{0,16},{16,32},{32,48},{48,64},{64,80},{80,96},{96,112},{112,128},... | collective-permute-start | bytes 11528 | tf_op jit(solution)/shard_map/ppermute | solution.py:30
  14.1 26.9 %collective-permute-start.2 = (f32[3,40,1,128]{3,1,2,0:T(8,128)}, f32[3,40,1,128]{3,1,2,0:T(8,128)}, u32[]{:S(2)}, u32[]{:S(2)}) collective-permute-start(f32[3,40,1,128]{3,1,2,0:T(8,128)} %bitcast.28), channel_id=1, source_target_pairs={{1,0},{2,1},{3,2},{4,3},{5,4},{6,5},{7,6},{8,7},{9,8},{10,9},{11,1... | collective-permute-start | bytes 184328 | tf_op jit(solution)/shard_map/ppermute | solution.py:40
  24.3 4.0 %copy-start.23 = (s32[512]{0:T(512)S(1)}, s32[512]{0:T(512)}, u32[]{:S(2)}) copy-start(s32[512]{0:T(512)} %param.15) | copy-start | bytes 6148
  24.3 4.0 %copy-start.26 = (s32[512]{0:T(512)S(1)}, s32[512]{0:T(512)}, u32[]{:S(2)}) copy-start(s32[512]{0:T(512)} %param.14) | copy-start | bytes 6148
  24.3 4.0 %copy-start.27 = (s32[512]{0:T(512)S(1)}, s32[512]{0:T(512)}, u32[]{:S(2)}) copy-start(s32[512]{0:T(512)} %param.13) | copy-start | bytes 6148
  24.3 4.0 %copy-start.28 = (s32[512]{0:T(512)S(1)}, s32[512]{0:T(512)}, u32[]{:S(2)}) copy-start(s32[512]{0:T(512)} %param.12) | copy-start | bytes 6148
  24.3 4.0 %copy-start.29 = (s32[512]{0:T(512)S(1)}, s32[512]{0:T(512)}, u32[]{:S(2)}) copy-start(s32[512]{0:T(512)} %param.11) | copy-start | bytes 6148
  24.3 16.7 %collective-permute-start.3 = (f32[3,40,1,128]{3,1,2,0:T(8,128)}, f32[3,40,1,128]{3,1,2,0:T(8,128)}, u32[]{:S(2)}, u32[]{:S(2)}) collective-permute-start(f32[3,40,1,128]{3,1,2,0:T(8,128)} %bitcast.29), channel_id=1, source_target_pairs={{0,1},{1,2},{2,3},{3,4},{4,5},{5,6},{6,7},{7,8},{8,9},{9,10},{10,1... | collective-permute-start | bytes 184328 | tf_op jit(solution)/shard_map/ppermute | solution.py:39
  26.5 6.4 %copy-start.24 = (f32[512]{0:T(512)S(1)}, f32[512]{0:T(512)}, u32[]{:S(2)}) copy-start(f32[512]{0:T(512)} %param.17) | copy-start | bytes 6148
  26.5 6.4 %copy-start.25 = (f32[512]{0:T(512)S(1)}, f32[512]{0:T(512)}, u32[]{:S(2)}) copy-start(f32[512]{0:T(512)} %param.16) | copy-start | bytes 6148
  30.1 2.8 %copy-start.11 = (s32[256]{0:T(256)}, s32[256]{0:T(256)S(1)}, u32[]{:S(2)}) copy-start(s32[256]{0:T(256)S(1)} %get-tuple-element.11) | copy-start | bytes 3076
  30.1 2.8 %copy-start.13 = (s32[256]{0:T(256)}, s32[256]{0:T(256)S(1)}, u32[]{:S(2)}) copy-start(s32[256]{0:T(256)S(1)} %get-tuple-element.17) | copy-start | bytes 3076
  30.1 10.8 %copy-start.7 = (s32[256]{0:T(256)}, s32[256]{0:T(256)S(1)}, u32[]{:S(2)}) copy-start(s32[256]{0:T(256)S(1)} %get-tuple-element.15) | copy-start | bytes 3076
  30.1 10.8 %copy-start.9 = (s32[256]{0:T(256)}, s32[256]{0:T(256)S(1)}, u32[]{:S(2)}) copy-start(s32[256]{0:T(256)S(1)} %get-tuple-element.18) | copy-start | bytes 3076
  34.1 6.9 %copy-start.20 = (f32[3]{0:T(128)S(1)}, f32[3]{0:T(128)}, u32[]{:S(2)}) copy-start(f32[3]{0:T(128)} %constant.118) | copy-start | bytes 40
  43.1 19.7 %collective-permute-start.4 = (f32[3,40,8,1]{3,1,2,0:T(8,128)S(1)}, f32[3,40,8,1]{3,1,2,0:T(8,128)S(1)}, u32[]{:S(2)}, u32[]{:S(2)}) collective-permute-start(f32[3,40,8,1]{3,1,2,0:T(8,128)S(1)} %get-tuple-element.61), channel_id=1, source_target_pairs={{16,0},{32,16},{48,32},{64,48},{80,64},{96,80},{112,96},{128,112},... | collective-permute-start | bytes 11528 | tf_op jit(solution)/shard_map/ppermute | solution.py:31
  50.4 18.0 %collective-permute-start.5 = (f32[3,40,8,1]{3,1,2,0:T(8,128)S(1)}, f32[3,40,8,1]{3,1,2,0:T(8,128)S(1)}, u32[]{:S(2)}, u32[]{:S(2)}) collective-permute-start(f32[3,40,8,1]{3,1,2,0:T(8,128)S(1)} %get-tuple-element.62), channel_id=1, source_target_pairs={{0,16},{16,32},{32,48},{48,64},{64,80},{80,96},{96,112},{112,128},... | collective-permute-start | bytes 11528 | tf_op jit(solution)/shard_map/ppermute | solution.py:30
  52.3 16.1 %collective-permute-start.8 = (f32[3,40,1,128]{3,1,2,0:T(8,128)S(1)}, f32[3,40,1,128]{3,1,2,0:T(8,128)S(1)}, u32[]{:S(2)}, u32[]{:S(2)}) collective-permute-start(f32[3,40,1,128]{3,1,2,0:T(8,128)S(1)} %get-tuple-element.64), channel_id=1, source_target_pairs={{1,0},{2,1},{3,2},{4,3},{5,4},{6,5},{7,6},{8,7},{9,8},{10,9},{11,1... | collective-permute-start | bytes 184328 | tf_op jit(solution)/shard_map/ppermute | solution.py:40
  60.8 10.9 %collective-permute-start.9 = (f32[3,40,1,128]{3,1,2,0:T(8,128)S(1)}, f32[3,40,1,128]{3,1,2,0:T(8,128)S(1)}, u32[]{:S(2)}, u32[]{:S(2)}) collective-permute-start(f32[3,40,1,128]{3,1,2,0:T(8,128)S(1)} %get-tuple-element.63), channel_id=1, source_target_pairs={{0,1},{1,2},{2,3},{3,4},{4,5},{5,6},{6,7},{7,8},{8,9},{9,10},{10,1... | collective-permute-start | bytes 184328 | tf_op jit(solution)/shard_map/ppermute | solution.py:39
  72.6 17.9 %collective-permute-start.6 = (f32[3,40,8,1]{3,1,2,0:T(8,128)S(1)}, f32[3,40,8,1]{3,1,2,0:T(8,128)S(1)}, u32[]{:S(2)}, u32[]{:S(2)}) collective-permute-start(f32[3,40,8,1]{3,1,2,0:T(8,128)S(1)} %get-tuple-element.53), channel_id=1, source_target_pairs={{16,0},{32,16},{48,32},{64,48},{80,64},{96,80},{112,96},{128,112},... | collective-permute-start | bytes 11528 | tf_op jit(solution)/shard_map/ppermute | solution.py:31
  78.7 16.7 %collective-permute-start.7 = (f32[3,40,8,1]{3,1,2,0:T(8,128)S(1)}, f32[3,40,8,1]{3,1,2,0:T(8,128)S(1)}, u32[]{:S(2)}, u32[]{:S(2)}) collective-permute-start(f32[3,40,8,1]{3,1,2,0:T(8,128)S(1)} %get-tuple-element.54), channel_id=1, source_target_pairs={{0,16},{16,32},{32,48},{48,64},{64,80},{80,96},{96,112},{112,128},... | collective-permute-start | bytes 11528 | tf_op jit(solution)/shard_map/ppermute | solution.py:30
  80.7 14.8 %collective-permute-start.10 = (f32[3,40,1,128]{3,1,2,0:T(8,128)S(1)}, f32[3,40,1,128]{3,1,2,0:T(8,128)S(1)}, u32[]{:S(2)}, u32[]{:S(2)}) collective-permute-start(f32[3,40,1,128]{3,1,2,0:T(8,128)S(1)} %get-tuple-element.57), channel_id=1, source_target_pairs={{1,0},{2,1},{3,2},{4,3},{5,4},{6,5},{7,6},{8,7},{9,8},{10,9},{11,1... | collective-permute-start | bytes 184328 | tf_op jit(solution)/shard_map/ppermute | solution.py:40
  84.3 11.1 %collective-permute-start.11 = (f32[3,40,1,128]{3,1,2,0:T(8,128)S(1)}, f32[3,40,1,128]{3,1,2,0:T(8,128)S(1)}, u32[]{:S(2)}, u32[]{:S(2)}) collective-permute-start(f32[3,40,1,128]{3,1,2,0:T(8,128)S(1)} %get-tuple-element.58), channel_id=1, source_target_pairs={{0,1},{1,2},{2,3},{3,4},{4,5},{5,6},{6,7},{7,8},{8,9},{9,10},{10,1... | collective-permute-start | bytes 184328 | tf_op jit(solution)/shard_map/ppermute | solution.py:39
  96.5 18.4 %collective-permute-start.12 = (f32[3,40,8,1]{3,1,2,0:T(8,128)S(1)}, f32[3,40,8,1]{3,1,2,0:T(8,128)S(1)}, u32[]{:S(2)}, u32[]{:S(2)}) collective-permute-start(f32[3,40,8,1]{3,1,2,0:T(8,128)S(1)} %get-tuple-element.42), channel_id=1, source_target_pairs={{16,0},{32,16},{48,32},{64,48},{80,64},{96,80},{112,96},{128,112},... | collective-permute-start | bytes 11528 | tf_op jit(solution)/shard_map/ppermute | solution.py:31
  102.4 17.2 %collective-permute-start.13 = (f32[3,40,8,1]{3,1,2,0:T(8,128)S(1)}, f32[3,40,8,1]{3,1,2,0:T(8,128)S(1)}, u32[]{:S(2)}, u32[]{:S(2)}) collective-permute-start(f32[3,40,8,1]{3,1,2,0:T(8,128)S(1)} %get-tuple-element.43), channel_id=1, source_target_pairs={{0,16},{16,32},{32,48},{48,64},{64,80},{80,96},{96,112},{112,128},... | collective-permute-start | bytes 11528 | tf_op jit(solution)/shard_map/ppermute | solution.py:30
  104.3 16.3 %collective-permute-start.14 = (f32[3,40,1,128]{3,1,2,0:T(8,128)S(1)}, f32[3,40,1,128]{3,1,2,0:T(8,128)S(1)}, u32[]{:S(2)}, u32[]{:S(2)}) collective-permute-start(f32[3,40,1,128]{3,1,2,0:T(8,128)S(1)} %get-tuple-element.46), channel_id=1, source_target_pairs={{1,0},{2,1},{3,2},{4,3},{5,4},{6,5},{7,6},{8,7},{9,8},{10,9},{11,1... | collective-permute-start | bytes 184328 | tf_op jit(solution)/shard_map/ppermute | solution.py:40
  109.8 10.9 %collective-permute-start.15 = (f32[3,40,1,128]{3,1,2,0:T(8,128)S(1)}, f32[3,40,1,128]{3,1,2,0:T(8,128)S(1)}, u32[]{:S(2)}, u32[]{:S(2)}) collective-permute-start(f32[3,40,1,128]{3,1,2,0:T(8,128)S(1)} %get-tuple-element.47), channel_id=1, source_target_pairs={{0,1},{1,2},{2,3},{3,4},{4,5},{5,6},{6,7},{7,8},{8,9},{9,10},{10,1... | collective-permute-start | bytes 184328 | tf_op jit(solution)/shard_map/ppermute | solution.py:39
  121.5 0.8 copy-start.2
  135.8 4.1 %copy-start.22 = (pred[256]{0:T(512)(128)(4,1)S(1)}, pred[256]{0:T(512)(128)(4,1)}, u32[]{:S(2)}) copy-start(pred[256]{0:T(512)(128)(4,1)} %compare_and_fusion.1) | copy-start | bytes 772
  135.8 4.1 %copy-start.21 = (pred[256]{0:T(512)(128)(4,1)S(1)}, pred[256]{0:T(512)(128)(4,1)}, u32[]{:S(2)}) copy-start(pred[256]{0:T(512)(128)(4,1)} %compare_and_fusion) | copy-start | bytes 772
  135.8 13.7 %copy-start.6 = (f32[3,8,128]{2,1,0:T(8,128)S(1)}, f32[3,8,128]{2,1,0:T(8,128)}, u32[]{:S(2)}) copy-start(f32[3,8,128]{2,1,0:T(8,128)} %get-tuple-element.21) | copy-start | bytes 36868
  135.8 35.9 %copy-start.5 = (f32[3,8,128]{2,1,0:T(8,128)S(1)}, f32[3,8,128]{2,1,0:T(8,128)}, u32[]{:S(2)}) copy-start(f32[3,8,128]{2,1,0:T(8,128)} %get-tuple-element.25) | copy-start | bytes 36868
  135.8 55.9 %copy-start.19 = (f32[256]{0:T(256)S(1)}, f32[256]{0:T(256)}, u32[]{:S(2)}) copy-start(f32[256]{0:T(256)} %get-tuple-element.7) | copy-start | bytes 3076
  135.8 56.0 %copy-start.4 = (f32[1,3,8,128]{3,1,2,0:T(4,128)S(1)}, f32[1,3,8,128]{3,1,2,0:T(4,128)}, u32[]{:S(2)}) copy-start(f32[1,3,8,128]{3,1,2,0:T(4,128)} %copy.135) | copy-start | bytes 36868
  139.8 53.5 %copy-start.18 = (f32[256]{0:T(256)S(1)}, f32[256]{0:T(256)}, u32[]{:S(2)}) copy-start(f32[256]{0:T(256)} %get-tuple-element.6) | copy-start | bytes 3076
  139.8 53.6 %copy-start = (f32[256,1024]{0,1:T(8,128)S(1)}, f32[256,1024]{0,1:T(8,128)}, u32[]{:S(2)}) copy-start(f32[256,1024]{0,1:T(8,128)} %get-tuple-element.74) | copy-start | bytes 3145732
  139.9 19.4 %collective-permute-start.16 = (f32[512,40]{0,1:T(8,128)S(1)}, f32[512,40]{0,1:T(8,128)S(1)}, u32[]{:S(2)}, u32[]{:S(2)}) collective-permute-start(f32[512,40]{0,1:T(8,128)S(1)} %pad_maximum_fusion.4), channel_id=1, source_target_pairs={{0,16},{16,32},{32,48},{48,64},{64,80},{80,96},{96,112},{112,128},... | collective-permute-start | bytes 245768 | tf_op jit(solution)/shard_map/ppermute | solution.py:210
  142.0 17.4 %collective-permute-start.17 = (f32[512,40]{0,1:T(8,128)S(1)}, f32[512,40]{0,1:T(8,128)S(1)}, u32[]{:S(2)}, u32[]{:S(2)}) collective-permute-start(f32[512,40]{0,1:T(8,128)S(1)} %pad_maximum_fusion.4), channel_id=1, source_target_pairs={{0,496},{16,0},{32,16},{48,32},{64,48},{80,64},{96,80},{112,96},{1... | collective-permute-start | bytes 245768 | tf_op jit(solution)/shard_map/ppermute | solution.py:211
  149.6 9.8 %collective-permute-start.18 = (f32[256,40]{0,1:T(8,128)S(1)}, f32[256,40]{0,1:T(8,128)S(1)}, u32[]{:S(2)}, u32[]{:S(2)}) collective-permute-start(f32[256,40]{0,1:T(8,128)S(1)} %broadcast_select_fusion.1), channel_id=1, source_target_pairs={{0,32},{16,48},{32,64},{48,80},{64,96},{80,112},{96,128},{112,144}... | collective-permute-start | bytes 122888 | tf_op jit(solution)/shard_map/ppermute | solution.py:215
  151.5 9.5 %collective-permute-start.19 = (f32[256,40]{0,1:T(8,128)S(1)}, f32[256,40]{0,1:T(8,128)S(1)}, u32[]{:S(2)}, u32[]{:S(2)}) collective-permute-start(f32[256,40]{0,1:T(8,128)S(1)} %broadcast_select_fusion.1), channel_id=1, source_target_pairs={{0,480},{16,496},{32,0},{48,16},{64,32},{80,48},{96,64},{112,80},{... | collective-permute-start | bytes 122888 | tf_op jit(solution)/shard_map/ppermute | solution.py:216
  161.0 26.4 %collective-permute-start.20 = (f32[512,40]{0,1:T(8,128)S(1)}, f32[512,40]{0,1:T(8,128)S(1)}, u32[]{:S(2)}, u32[]{:S(2)}) collective-permute-start(f32[512,40]{0,1:T(8,128)S(1)} %pad_maximum_fusion.5), channel_id=1, source_target_pairs={{0,1},{1,2},{2,3},{3,4},{4,5},{5,6},{6,7},{7,8},{8,9},{9,10},{10,1... | collective-permute-start | bytes 245768 | tf_op jit(solution)/shard_map/ppermute | solution.py:221
  165.2 22.2 %collective-permute-start.21 = (f32[512,40]{0,1:T(8,128)S(1)}, f32[512,40]{0,1:T(8,128)S(1)}, u32[]{:S(2)}, u32[]{:S(2)}) collective-permute-start(f32[512,40]{0,1:T(8,128)S(1)} %pad_maximum_fusion.5), channel_id=1, source_target_pairs={{1,0},{2,1},{3,2},{4,3},{5,4},{6,5},{7,6},{8,7},{9,8},{10,9},{11,1... | collective-permute-start | bytes 245768 | tf_op jit(solution)/shard_map/ppermute | solution.py:222
  171.7 17.3 %collective-permute-start.22 = (f32[256,40]{0,1:T(8,128)S(1)}, f32[256,40]{0,1:T(8,128)S(1)}, u32[]{:S(2)}, u32[]{:S(2)}) collective-permute-start(f32[256,40]{0,1:T(8,128)S(1)} %get-tuple-element.72), channel_id=1, source_target_pairs={{0,2},{1,3},{2,4},{3,5},{4,6},{5,7},{6,8},{7,9},{8,10},{9,11},{10,... | collective-permute-start | bytes 122888 | tf_op jit(solution)/shard_map/ppermute | solution.py:226
  177.1 14.7 %collective-permute-start.23 = (f32[256,40]{0,1:T(8,128)S(1)}, f32[256,40]{0,1:T(8,128)S(1)}, u32[]{:S(2)}, u32[]{:S(2)}) collective-permute-start(f32[256,40]{0,1:T(8,128)S(1)} %get-tuple-element.72), channel_id=1, source_target_pairs={{2,0},{3,1},{4,2},{5,3},{6,4},{7,5},{8,6},{9,7},{10,8},{11,9},{12,... | collective-permute-start | bytes 122888 | tf_op jit(solution)/shard_map/ppermute | solution.py:227
  193.3 1.6 copy-start.8
  193.3 1.6 copy-start.10
  193.3 1.6 copy-start.12
  193.3 1.6 copy-start.14
  193.3 1.6 copy-start.15
  193.3 2.3 %copy-start.17 = (f32[256]{0:T(256)S(1)}, f32[256]{0:T(256)}, u32[]{:S(2)}) copy-start(f32[256]{0:T(256)} %get-tuple-element.5) | copy-start | bytes 3076
  194.9 2.2 %copy-start.16 = (f32[256]{0:T(256)S(1)}, f32[256]{0:T(256)}, u32[]{:S(2)}) copy-start(f32[256]{0:T(256)} %get-tuple-element.8) | copy-start | bytes 3076
  203.2 1.7 copy-start.3

commit v2 on v1

--- a/solution.py
+++ b/solution.py
@@ -128,21 +128,15 @@
     return lax.axis_index("lon") * cols_tile, lax.axis_index("lat") * rows_tile
 
 
-def at_owner(state, lon_obs, lat_obs, kind_obs):
-    _, _, rows_tile, cols_tile = state.shape
+def owner_table(state, lon_obs, lat_obs, kind_obs):
+    fields_count, _, rows_tile, cols_tile = state.shape
     lon_base, lat_base = tile_origin(state)
-    owned = (
-        (lon_obs >= lon_base)
-        & (lon_obs < lon_base + cols_tile)
-        & (lat_obs >= lat_base)
-        & (lat_obs < lat_base + rows_tile)
-    )
-    nearby_latitude = jnp.clip(lat_obs - lat_base, 0, rows_tile - 1)
-    local_lon = jnp.clip(lon_obs - lon_base, 0, cols_tile - 1)
-    rows = state[kind_obs, :, nearby_latitude, :]
-    pick = jnp.arange(cols_tile, dtype=jnp.int32)[None, :] == local_lon[:, None]
-    values = jnp.sum(jnp.where(pick[:, None, :], rows, 0.0), axis=2)
-    return values, owned
+    row_hit = jnp.arange(rows_tile, dtype=jnp.int32)[None, :] == (lat_obs - lat_base)[:, None]
+    col_hit = jnp.arange(cols_tile, dtype=jnp.int32)[None, :] == (lon_obs - lon_base)[:, None]
+    cell = (row_hit[:, :, None] & col_hit[:, None, :]).astype(jnp.float32)
+    picked = jnp.einsum("jrc,fmrc->jfm", cell, state, precision=lax.Precision.HIGHEST)
+    field_hit = jnp.arange(fields_count, dtype=jnp.int32)[None, :] == kind_obs[:, None]
+    return jnp.sum(jnp.where(field_hit[:, :, None], picked, 0.0), axis=1)
 
 
 def update(state, gains, anomaly, weights):
@@ -200,10 +194,7 @@
 
     (lon0, lat0, kind0, radius0), (value0, error0) = batches[0]
     (lon1, lat1, kind1, radius1), (value1, error1) = batches[1]
-    values0, owned0 = at_owner(state, lon0, lat0, kind0)
-    values1, owned1 = at_owner(state, lon1, lat1, kind1)
-    table0 = jnp.where(owned0[:, None], values0, 0.0)
-    table1 = jnp.where(owned1[:, None], values1, 0.0)
+    table0, table1 = jnp.split(owner_table(state, ints[0], ints[1], ints[2]), 2)
     both = jnp.concatenate([table0, table1])
     both = (
         both

time: 213 us -> 202 us (0.948); the launches traced: 212 us -> 198 us
  waiting for transfers between devices: 24.5 us -> 45.5 us
  starting transfers between devices: 123 us -> 108 us
  other arithmetic: 21.7 us -> 7.78 us
  local copies, waits for them, and re-layouts: 22.7 us -> 15.4 us
    ppermute x4, starting transfers between devices: 27.5 us -> 15.9 us  [lon_edges(): right = lax.ppermute(array[..., :1], 'lon', down)]
    reduce_sum x2 -> x0, other arithmetic: 8.51 us -> none  [at_owner(): values = jnp.sum(jnp.where(pick[:, None, :], rows, 0.0), axis=2)]
    ppermute x4, waiting for transfers between devices: 0.01 us -> 8.18 us  [lon_edges(): right = lax.ppermute(array[..., :1], 'lon', down)]
    gather x2 -> x0, local copies, waits for them, and re-layouts: 7.85 us -> none  [at_owner(): rows = state[kind_obs, :, nearby_latitude, :]]
    ppermute x1, waiting for transfers between devices: 0.01 us -> 7.61 us  [shards(): lax.ppermute(table0, 'lon', ring_pairs(lon_size, 2))]
    ppermute x1, starting transfers between devices: 10.3 us -> 2.86 us  [shards(): lax.ppermute(wide0, 'lat', line_pairs(lat_size, -2))]
    ppermute x1, starting transfers between devices: 5.33 us -> 11.9 us  [shards(): lax.ppermute(wide0, 'lat', line_pairs(lat_size, 2))]
    ppermute x4, starting transfers between devices: 27.7 us -> 33.3 us  [lat_edges(): after = lax.ppermute(array[:, :, :1, :], 'lat', down)]
  transfers between devices with their start and end apart: 24 -> 24, of which waited for: 8 -> 11; matrix products, arithmetic and copies ran while one was open for 8% -> 8% of each run, Pallas kernels for 0% -> 0%
where the time goes in v2:
time: 202 us; the launch traced here: 198 us
  starting transfers between devices  108 us (53%)
  waiting for transfers between devices  45.5 us (23%)
  matrix products  20.3 us (10%)
  local copies, waits for them, and re-layouts  15.4 us (8%)
  other arithmetic  7.78 us (4%)
    ppermute x4, starting transfers between devices, lat_edges(): after = lax.ppermute(array[:, :, :1, :], 'lat', down)  33.3 us
    ppermute x4, waiting for transfers between devices, lon_edges(): left = lax.ppermute(array[..., -1:], 'lon', up)  18.1 us
    ppermute x4, starting transfers between devices, lon_edges(): right = lax.ppermute(array[..., :1], 'lon', down)  15.9 us
    ppermute x4, starting transfers between devices, lat_edges(): before = lax.ppermute(array[:, :, -1:, :], 'lat', up)  12.4 us
    ppermute x1, starting transfers between devices, shards(): lax.ppermute(wide0, 'lat', line_pairs(lat_size, 2))  11.9 us
    dot_general x6, matrix products, update_group(): jnp.einsum('om,foc->fmc', gains, covariance * weights[None], precision=la...  9.11 us
    dot_general x6, matrix products, update_group(): jnp.einsum('om,fmc->foc', anomaly, deviation, precision=lax.Precision.HIGH)  8.84 us
    ppermute x4, starting transfers between devices, lon_edges(): left = lax.ppermute(array[..., -1:], 'lon', up)  8.64 us
  transfers between devices with their start and end apart: 24, of which 11 were waited for; matrix products, arithmetic and copies ran while one was open for 8% of the time, Pallas kernels for 0%

profile of v2, /device:TPU:24, one launch (start us, length us, event | category | flops | bytes accessed | tf_op | source)
XLA Modules:
  0.0 198.0 jit_solution(8200540811244662637)
XLA Ops:
  0.0 2.0 %fusion.153 = (f32[3,40,1,128]{3,2,1,0:T(1,128)}, f32[3,40,1,128]{3,2,1,0:T(1,128)}) fusion(f32[9,40,8,128]{3,2,1,0:T(8,128)} %param.10), kind=kLoop, calls=%fused_computation.238 | loop fusion | bytes 245760 | tf_op jit(solution)/shard_map/slice | solution.py:39
  2.0 12.9 %collective-permute-start.2 = (f32[3,40,1,128]{3,1,2,0:T(8,128)}, f32[3,40,1,128]{3,1,2,0:T(8,128)}, u32[]{:S(2)}, u32[]{:S(2)}) collective-permute-start(f32[3,40,1,128]{3,1,2,0:T(8,128)} %bitcast.29), channel_id=1, source_target_pairs={{1,0},{2,1},{3,2},{4,3},{5,4},{6,5},{7,6},{8,7},{9,8},{10,9},{11,1... | collective-permute-start | bytes 184328 | tf_op jit(solution)/shard_map/ppermute | solution.py:40
  15.0 1.9 collective-permute-start.3
  16.9 1.4 fusion.155
  18.3 0.9 copy.73
  19.1 5.2 %collective-permute-start = (f32[3,40,8,1]{3,1,2,0:T(8,128)}, f32[3,40,8,1]{3,1,2,0:T(8,128)}, u32[]{:S(2)}, u32[]{:S(2)}) collective-permute-start(f32[3,40,8,1]{3,1,2,0:T(8,128)} %copy.73), channel_id=1, source_target_pairs={{16,0},{32,16},{48,32},{64,48},{80,64},{96,80},{112,96},{128,112},... | collective-permute-start | bytes 11528 | tf_op jit(solution)/shard_map/ppermute | solution.py:31
  24.3 0.9 copy.74
  25.2 1.9 collective-permute-start.1
  27.4 1.0 gather_fusion
  29.0 0.4 slice_reduce_fusion
  29.5 1.0 fusion.154
  30.5 0.9 fusion.156
  31.6 0.6 iota_compare_fusion.2
  32.3 0.9 copy.55
  33.2 2.6 %gather_fusion.1 = f32[512,2]{1,0:T(8,128)} fusion(f32[2,512]{0,1:T(8,128)} %copy.55, s32[1024]{0:T(1024)S(1)} %pad_clamp_fusion), kind=kCustom, calls=%fused_computation.1 | custom fusion | bytes 10240 | tf_op jit(solution)/shard_map/gather | solution.py:187
  35.8 1.4 slice_reduce_fusion.2
  37.2 1.8 multiply_multiply_fusion
  39.6 1.6 fusion.70
  41.7 6.4 %collective-permute-start.9 = (f32[3,40,1,128]{3,1,2,0:T(8,128)S(1)}, f32[3,40,1,128]{3,1,2,0:T(8,128)S(1)}, u32[]{:S(2)}, u32[]{:S(2)}) collective-permute-start(f32[3,40,1,128]{3,1,2,0:T(8,128)S(1)} %get-tuple-element.62), channel_id=1, source_target_pairs={{0,1},{1,2},{2,3},{3,4},{4,5},{5,6},{6,7},{7,8},{8,9},{9,10},{10,1... | collective-permute-start | bytes 184328 | tf_op jit(solution)/shard_map/ppermute | solution.py:39
  48.1 4.2 %collective-permute-start.8 = (f32[3,40,1,128]{3,1,2,0:T(8,128)S(1)}, f32[3,40,1,128]{3,1,2,0:T(8,128)S(1)}, u32[]{:S(2)}, u32[]{:S(2)}) collective-permute-start(f32[3,40,1,128]{3,1,2,0:T(8,128)S(1)} %get-tuple-element.63), channel_id=1, source_target_pairs={{1,0},{2,1},{3,2},{4,3},{5,4},{6,5},{7,6},{8,7},{9,8},{10,9},{11,1... | collective-permute-start | bytes 184328 | tf_op jit(solution)/shard_map/ppermute | solution.py:40
  52.3 6.9 %collective-permute-start.4 = (f32[3,40,8,1]{3,1,2,0:T(8,128)S(1)}, f32[3,40,8,1]{3,1,2,0:T(8,128)S(1)}, u32[]{:S(2)}, u32[]{:S(2)}) collective-permute-start(f32[3,40,8,1]{3,1,2,0:T(8,128)S(1)} %get-tuple-element.60), channel_id=1, source_target_pairs={{16,0},{32,16},{48,32},{64,48},{80,64},{96,80},{112,96},{128,112},... | collective-permute-start | bytes 11528 | tf_op jit(solution)/shard_map/ppermute | solution.py:31
  59.2 1.9 collective-permute-start.5
  61.2 4.3 %collective-permute-done.4 = f32[3,40,8,1]{3,1,2,0:T(8,128)S(1)} collective-permute-done((f32[3,40,8,1]{3,1,2,0:T(8,128)S(1)}, f32[3,40,8,1]{3,1,2,0:T(8,128)S(1)}, u32[]{:S(2)}, u32[]{:S(2)}) %collective-permute-start.4) | collective-permute-done | bytes 3872 | tf_op jit(solution)/shard_map/ppermute | solution.py:31
  65.5 7.7 %collective-permute-done.5 = f32[3,40,8,1]{3,1,2,0:T(8,128)S(1)} collective-permute-done((f32[3,40,8,1]{3,1,2,0:T(8,128)S(1)}, f32[3,40,8,1]{3,1,2,0:T(8,128)S(1)}, u32[]{:S(2)}, u32[]{:S(2)}) %collective-permute-start.5) | collective-permute-done | bytes 3872 | tf_op jit(solution)/shard_map/ppermute | solution.py:30
  73.3 0.5 fusion.77
  74.2 7.6 %collective-permute-start.10 = (f32[3,40,1,128]{3,1,2,0:T(8,128)S(1)}, f32[3,40,1,128]{3,1,2,0:T(8,128)S(1)}, u32[]{:S(2)}, u32[]{:S(2)}) collective-permute-start(f32[3,40,1,128]{3,1,2,0:T(8,128)S(1)} %get-tuple-element.56), channel_id=1, source_target_pairs={{1,0},{2,1},{3,2},{4,3},{5,4},{6,5},{7,6},{8,7},{9,8},{10,9},{11,1... | collective-permute-start | bytes 184328 | tf_op jit(solution)/shard_map/ppermute | solution.py:40
  81.8 2.1 %collective-permute-start.11 = (f32[3,40,1,128]{3,1,2,0:T(8,128)S(1)}, f32[3,40,1,128]{3,1,2,0:T(8,128)S(1)}, u32[]{:S(2)}, u32[]{:S(2)}) collective-permute-start(f32[3,40,1,128]{3,1,2,0:T(8,128)S(1)} %get-tuple-element.57), channel_id=1, source_target_pairs={{0,1},{1,2},{2,3},{3,4},{4,5},{5,6},{6,7},{7,8},{8,9},{9,10},{10,1... | collective-permute-start | bytes 184328 | tf_op jit(solution)/shard_map/ppermute | solution.py:39
  84.0 1.9 collective-permute-start.6
  85.9 2.4 %collective-permute-start.7 = (f32[3,40,8,1]{3,1,2,0:T(8,128)S(1)}, f32[3,40,8,1]{3,1,2,0:T(8,128)S(1)}, u32[]{:S(2)}, u32[]{:S(2)}) collective-permute-start(f32[3,40,8,1]{3,1,2,0:T(8,128)S(1)} %get-tuple-element.53), channel_id=1, source_target_pairs={{0,16},{16,32},{32,48},{48,64},{64,80},{80,96},{96,112},{112,128},... | collective-permute-start | bytes 11528 | tf_op jit(solution)/shard_map/ppermute | solution.py:30
  88.4 3.8 %collective-permute-done.6 = f32[3,40,8,1]{3,1,2,0:T(8,128)S(1)} collective-permute-done((f32[3,40,8,1]{3,1,2,0:T(8,128)S(1)}, f32[3,40,8,1]{3,1,2,0:T(8,128)S(1)}, u32[]{:S(2)}, u32[]{:S(2)}) %collective-permute-start.6) | collective-permute-done | bytes 3872 | tf_op jit(solution)/shard_map/ppermute | solution.py:31
  92.2 7.7 %collective-permute-done.7 = f32[3,40,8,1]{3,1,2,0:T(8,128)S(1)} collective-permute-done((f32[3,40,8,1]{3,1,2,0:T(8,128)S(1)}, f32[3,40,8,1]{3,1,2,0:T(8,128)S(1)}, u32[]{:S(2)}, u32[]{:S(2)}) %collective-permute-start.7) | collective-permute-done | bytes 3872 | tf_op jit(solution)/shard_map/ppermute | solution.py:30
  100.0 0.4 fusion.143
  101.0 1.9 collective-permute-start.12
  102.9 2.4 %collective-permute-start.13 = (f32[3,40,8,1]{3,1,2,0:T(8,128)S(1)}, f32[3,40,8,1]{3,1,2,0:T(8,128)S(1)}, u32[]{:S(2)}, u32[]{:S(2)}) collective-permute-start(f32[3,40,8,1]{3,1,2,0:T(8,128)S(1)} %get-tuple-element.42), channel_id=1, source_target_pairs={{0,16},{16,32},{32,48},{48,64},{64,80},{80,96},{96,112},{112,128},... | collective-permute-start | bytes 11528 | tf_op jit(solution)/shard_map/ppermute | solution.py:30
  105.4 8.5 %collective-permute-start.14 = (f32[3,40,1,128]{3,1,2,0:T(8,128)S(1)}, f32[3,40,1,128]{3,1,2,0:T(8,128)S(1)}, u32[]{:S(2)}, u32[]{:S(2)}) collective-permute-start(f32[3,40,1,128]{3,1,2,0:T(8,128)S(1)} %get-tuple-element.45), channel_id=1, source_target_pairs={{1,0},{2,1},{3,2},{4,3},{5,4},{6,5},{7,6},{8,7},{9,8},{10,9},{11,1... | collective-permute-start | bytes 184328 | tf_op jit(solution)/shard_map/ppermute | solution.py:40
  113.9 1.9 collective-permute-start.15
  115.8 2.5 %collective-permute-done.13 = f32[3,40,8,1]{3,1,2,0:T(8,128)S(1)} collective-permute-done((f32[3,40,8,1]{3,1,2,0:T(8,128)S(1)}, f32[3,40,8,1]{3,1,2,0:T(8,128)S(1)}, u32[]{:S(2)}, u32[]{:S(2)}) %collective-permute-start.13) | collective-permute-done | bytes 3872 | tf_op jit(solution)/shard_map/ppermute | solution.py:30
  118.7 6.1 %collective-permute-done.15 = f32[3,40,1,128]{3,1,2,0:T(8,128)S(1)} collective-permute-done((f32[3,40,1,128]{3,1,2,0:T(8,128)S(1)}, f32[3,40,1,128]{3,1,2,0:T(8,128)S(1)}, u32[]{:S(2)}, u32[]{:S(2)}) %collective-permute-start.15) | collective-permute-done | bytes 61472 | tf_op jit(solution)/shard_map/ppermute | solution.py:39
  125.1 1.7 fusion.45
  126.8 5.6 %collective-permute-start.17 = (f32[512,40]{0,1:T(8,128)S(1)}, f32[512,40]{0,1:T(8,128)S(1)}, u32[]{:S(2)}, u32[]{:S(2)}) collective-permute-start(f32[512,40]{0,1:T(8,128)S(1)} %fusion.45), channel_id=1, source_target_pairs={{0,496},{16,0},{32,16},{48,32},{64,48},{80,64},{96,80},{112,96},{1... | collective-permute-start | bytes 245768 | tf_op jit(solution)/shard_map/ppermute | solution.py:202
  132.4 1.9 collective-permute-start.16
  134.4 2.3 %collective-permute-start.19 = (f32[256,40]{0,1:T(8,128)S(1)}, f32[256,40]{0,1:T(8,128)S(1)}, u32[]{:S(2)}, u32[]{:S(2)}) collective-permute-start(f32[256,40]{0,1:T(8,128)S(1)} %split.5), channel_id=1, source_target_pairs={{0,480},{16,496},{32,0},{48,16},{64,32},{80,48},{96,64},{112,80},{... | collective-permute-start | bytes 122888 | tf_op jit(solution)/shard_map/ppermute | solution.py:207
  136.7 3.5 %collective-permute-start.18 = (f32[256,40]{0,1:T(8,128)S(1)}, f32[256,40]{0,1:T(8,128)S(1)}, u32[]{:S(2)}, u32[]{:S(2)}) collective-permute-start(f32[256,40]{0,1:T(8,128)S(1)} %split.5), channel_id=1, source_target_pairs={{0,32},{16,48},{32,64},{48,80},{64,96},{80,112},{96,128},{112,144}... | collective-permute-start | bytes 122888 | tf_op jit(solution)/shard_map/ppermute | solution.py:206
  140.3 1.8 collective-permute-done.16
  142.1 7.6 %collective-permute-done.18 = f32[256,40]{0,1:T(8,128)S(1)} collective-permute-done((f32[256,40]{0,1:T(8,128)S(1)}, f32[256,40]{0,1:T(8,128)S(1)}, u32[]{:S(2)}, u32[]{:S(2)}) %collective-permute-start.18) | collective-permute-done | bytes 40992 | tf_op jit(solution)/shard_map/ppermute | solution.py:206
  149.8 1.9 collective-permute-start.21
  151.7 7.8 %collective-permute-start.20 = (f32[512,40]{0,1:T(8,128)S(1)}, f32[512,40]{0,1:T(8,128)S(1)}, u32[]{:S(2)}, u32[]{:S(2)}) collective-permute-start(f32[512,40]{0,1:T(8,128)S(1)} %pad_maximum_fusion.3), channel_id=1, source_target_pairs={{0,1},{1,2},{2,3},{3,4},{4,5},{5,6},{6,7},{7,8},{8,9},{9,10},{10,1... | collective-permute-start | bytes 245768 | tf_op jit(solution)/shard_map/ppermute | solution.py:212
  159.5 2.9 %collective-permute-start.23 = (f32[256,40]{0,1:T(8,128)S(1)}, f32[256,40]{0,1:T(8,128)S(1)}, u32[]{:S(2)}, u32[]{:S(2)}) collective-permute-start(f32[256,40]{0,1:T(8,128)S(1)} %get-tuple-element.71), channel_id=1, source_target_pairs={{2,0},{3,1},{4,2},{5,3},{6,4},{7,5},{8,6},{9,7},{10,8},{11,9},{12,... | collective-permute-start | bytes 122888 | tf_op jit(solution)/shard_map/ppermute | solution.py:218
  162.4 11.9 %collective-permute-start.22 = (f32[256,40]{0,1:T(8,128)S(1)}, f32[256,40]{0,1:T(8,128)S(1)}, u32[]{:S(2)}, u32[]{:S(2)}) collective-permute-start(f32[256,40]{0,1:T(8,128)S(1)} %get-tuple-element.71), channel_id=1, source_target_pairs={{0,2},{1,3},{2,4},{3,5},{4,6},{5,7},{6,8},{7,9},{8,10},{9,11},{10,... | collective-permute-start | bytes 122888 | tf_op jit(solution)/shard_map/ppermute | solution.py:217
  174.6 3.5 %collective-permute-done.22 = f32[256,40]{0,1:T(8,128)S(1)} collective-permute-done((f32[256,40]{0,1:T(8,128)S(1)}, f32[256,40]{0,1:T(8,128)S(1)}, u32[]{:S(2)}, u32[]{:S(2)}) %collective-permute-start.22) | collective-permute-done | bytes 40992 | tf_op jit(solution)/shard_map/ppermute | solution.py:217
  178.1 0.5 fusion.50
  178.6 1.4 fusion.65
  180.3 1.5 fusion.170
  181.9 1.4 fusion.82
  183.3 1.5 fusion.44
  184.9 1.4 fusion.66
  186.3 1.5 fusion.172
  187.8 1.4 fusion.84
  189.3 1.5 fusion.43
  190.9 1.7 fusion.67
  192.5 1.5 fusion.173
  194.1 1.4 fusion.86
  195.5 1.5 fusion.42
  197.1 0.9 pad_maximum_fusion
  (100 shorter events, 4.6 us)
Async XLA Ops:
  0.0 29.5 %copy-start = (f32[9,40,8,128]{3,2,1,0:T(8,128)S(1)}, f32[9,40,8,128]{3,2,1,0:T(8,128)}, u32[]{:S(2)}) copy-start(f32[9,40,8,128]{3,2,1,0:T(8,128)} %param.10) | copy-start | bytes 4423684
  0.0 27.1 %copy-start.6 = (s32[512]{0:T(512)S(1)}, s32[512]{0:T(512)}, u32[]{:S(2)}) copy-start(s32[512]{0:T(512)} %param.15) | copy-start | bytes 6148
  0.0 27.2 %copy-start.9 = (s32[512]{0:T(512)S(1)}, s32[512]{0:T(512)}, u32[]{:S(2)}) copy-start(s32[512]{0:T(512)} %param.14) | copy-start | bytes 6148
  0.0 27.2 %copy-start.10 = (s32[512]{0:T(512)S(1)}, s32[512]{0:T(512)}, u32[]{:S(2)}) copy-start(s32[512]{0:T(512)} %param.13) | copy-start | bytes 6148
  0.0 27.2 %copy-start.11 = (s32[512]{0:T(512)S(1)}, s32[512]{0:T(512)}, u32[]{:S(2)}) copy-start(s32[512]{0:T(512)} %param.12) | copy-start | bytes 6148
  0.0 27.2 %copy-start.12 = (s32[512]{0:T(512)S(1)}, s32[512]{0:T(512)}, u32[]{:S(2)}) copy-start(s32[512]{0:T(512)} %param.11) | copy-start | bytes 6148
  2.0 37.5 %collective-permute-start.2 = (f32[3,40,1,128]{3,1,2,0:T(8,128)}, f32[3,40,1,128]{3,1,2,0:T(8,128)}, u32[]{:S(2)}, u32[]{:S(2)}) collective-permute-start(f32[3,40,1,128]{3,1,2,0:T(8,128)} %bitcast.29), channel_id=1, source_target_pairs={{1,0},{2,1},{3,2},{4,3},{5,4},{6,5},{7,6},{8,7},{9,8},{10,9},{11,1... | collective-permute-start | bytes 184328 | tf_op jit(solution)/shard_map/ppermute | solution.py:40
  15.0 24.6 %collective-permute-start.3 = (f32[3,40,1,128]{3,1,2,0:T(8,128)}, f32[3,40,1,128]{3,1,2,0:T(8,128)}, u32[]{:S(2)}, u32[]{:S(2)}) collective-permute-start(f32[3,40,1,128]{3,1,2,0:T(8,128)} %bitcast.30), channel_id=1, source_target_pairs={{0,1},{1,2},{2,3},{3,4},{4,5},{5,6},{6,7},{7,8},{8,9},{9,10},{10,1... | collective-permute-start | bytes 184328 | tf_op jit(solution)/shard_map/ppermute | solution.py:39
  19.1 20.3 %collective-permute-start = (f32[3,40,8,1]{3,1,2,0:T(8,128)}, f32[3,40,8,1]{3,1,2,0:T(8,128)}, u32[]{:S(2)}, u32[]{:S(2)}) collective-permute-start(f32[3,40,8,1]{3,1,2,0:T(8,128)} %copy.73), channel_id=1, source_target_pairs={{16,0},{32,16},{48,32},{64,48},{80,64},{96,80},{112,96},{128,112},... | collective-permute-start | bytes 11528 | tf_op jit(solution)/shard_map/ppermute | solution.py:31
  25.2 14.4 %collective-permute-start.1 = (f32[3,40,8,1]{3,1,2,0:T(8,128)}, f32[3,40,8,1]{3,1,2,0:T(8,128)}, u32[]{:S(2)}, u32[]{:S(2)}) collective-permute-start(f32[3,40,8,1]{3,1,2,0:T(8,128)} %copy.74), channel_id=1, source_target_pairs={{0,16},{16,32},{32,48},{48,64},{64,80},{80,96},{96,112},{112,128},... | collective-permute-start | bytes 11528 | tf_op jit(solution)/shard_map/ppermute | solution.py:30
  29.5 2.8 %copy-start.7 = (f32[512]{0:T(512)S(1)}, f32[512]{0:T(512)}, u32[]{:S(2)}) copy-start(f32[512]{0:T(512)} %param.17) | copy-start | bytes 6148
  29.5 2.8 %copy-start.8 = (f32[512]{0:T(512)S(1)}, f32[512]{0:T(512)}, u32[]{:S(2)}) copy-start(f32[512]{0:T(512)} %param.16) | copy-start | bytes 6148
  31.5 7.5 %copy-start.3 = (f32[3,40,7,128]{3,2,1,0:T(8,128)S(1)}, f32[3,40,7,128]{3,2,1,0:T(8,128)}, u32[]{:S(2)}) copy-start(f32[3,40,7,128]{3,2,1,0:T(8,128)} %get-tuple-element.33) | copy-start | bytes 1290244
  31.5 7.6 %copy-start.2 = (f32[3,40,7,128]{3,2,1,0:T(8,128)S(1)}, f32[3,40,7,128]{3,2,1,0:T(8,128)}, u32[]{:S(2)}) copy-start(f32[3,40,7,128]{3,2,1,0:T(8,128)} %get-tuple-element.34) | copy-start | bytes 1290244
  31.5 7.7 %copy-start.1 = (f32[3,40,8,127]{3,2,1,0:T(8,128)S(1)}, f32[3,40,8,127]{3,2,1,0:T(8,128)}, u32[]{:S(2)}) copy-start(f32[3,40,8,127]{3,2,1,0:T(8,128)} %get-tuple-element.37) | copy-start | bytes 1463044
  35.8 3.8 %copy-start.5 = (f32[3]{0:T(128)S(1)}, f32[3]{0:T(128)}, u32[]{:S(2)}) copy-start(f32[3]{0:T(128)} %constant.109) | copy-start | bytes 40
  41.7 31.6 %collective-permute-start.9 = (f32[3,40,1,128]{3,1,2,0:T(8,128)S(1)}, f32[3,40,1,128]{3,1,2,0:T(8,128)S(1)}, u32[]{:S(2)}, u32[]{:S(2)}) collective-permute-start(f32[3,40,1,128]{3,1,2,0:T(8,128)S(1)} %get-tuple-element.62), channel_id=1, source_target_pairs={{0,1},{1,2},{2,3},{3,4},{4,5},{5,6},{6,7},{7,8},{8,9},{9,10},{10,1... | collective-permute-start | bytes 184328 | tf_op jit(solution)/shard_map/ppermute | solution.py:39
  48.1 25.2 %collective-permute-start.8 = (f32[3,40,1,128]{3,1,2,0:T(8,128)S(1)}, f32[3,40,1,128]{3,1,2,0:T(8,128)S(1)}, u32[]{:S(2)}, u32[]{:S(2)}) collective-permute-start(f32[3,40,1,128]{3,1,2,0:T(8,128)S(1)} %get-tuple-element.63), channel_id=1, source_target_pairs={{1,0},{2,1},{3,2},{4,3},{5,4},{6,5},{7,6},{8,7},{9,8},{10,9},{11,1... | collective-permute-start | bytes 184328 | tf_op jit(solution)/shard_map/ppermute | solution.py:40
  52.3 13.2 %collective-permute-start.4 = (f32[3,40,8,1]{3,1,2,0:T(8,128)S(1)}, f32[3,40,8,1]{3,1,2,0:T(8,128)S(1)}, u32[]{:S(2)}, u32[]{:S(2)}) collective-permute-start(f32[3,40,8,1]{3,1,2,0:T(8,128)S(1)} %get-tuple-element.60), channel_id=1, source_target_pairs={{16,0},{32,16},{48,32},{64,48},{80,64},{96,80},{112,96},{128,112},... | collective-permute-start | bytes 11528 | tf_op jit(solution)/shard_map/ppermute | solution.py:31
  59.2 14.1 %collective-permute-start.5 = (f32[3,40,8,1]{3,1,2,0:T(8,128)S(1)}, f32[3,40,8,1]{3,1,2,0:T(8,128)S(1)}, u32[]{:S(2)}, u32[]{:S(2)}) collective-permute-start(f32[3,40,8,1]{3,1,2,0:T(8,128)S(1)} %get-tuple-element.61), channel_id=1, source_target_pairs={{0,16},{16,32},{32,48},{48,64},{64,80},{80,96},{96,112},{112,128},... | collective-permute-start | bytes 11528 | tf_op jit(solution)/shard_map/ppermute | solution.py:30
  74.2 25.8 %collective-permute-start.10 = (f32[3,40,1,128]{3,1,2,0:T(8,128)S(1)}, f32[3,40,1,128]{3,1,2,0:T(8,128)S(1)}, u32[]{:S(2)}, u32[]{:S(2)}) collective-permute-start(f32[3,40,1,128]{3,1,2,0:T(8,128)S(1)} %get-tuple-element.56), channel_id=1, source_target_pairs={{1,0},{2,1},{3,2},{4,3},{5,4},{6,5},{7,6},{8,7},{9,8},{10,9},{11,1... | collective-permute-start | bytes 184328 | tf_op jit(solution)/shard_map/ppermute | solution.py:40
  81.8 18.1 %collective-permute-start.11 = (f32[3,40,1,128]{3,1,2,0:T(8,128)S(1)}, f32[3,40,1,128]{3,1,2,0:T(8,128)S(1)}, u32[]{:S(2)}, u32[]{:S(2)}) collective-permute-start(f32[3,40,1,128]{3,1,2,0:T(8,128)S(1)} %get-tuple-element.57), channel_id=1, source_target_pairs={{0,1},{1,2},{2,3},{3,4},{4,5},{5,6},{6,7},{7,8},{8,9},{9,10},{10,1... | collective-permute-start | bytes 184328 | tf_op jit(solution)/shard_map/ppermute | solution.py:39
  84.0 8.3 %collective-permute-start.6 = (f32[3,40,8,1]{3,1,2,0:T(8,128)S(1)}, f32[3,40,8,1]{3,1,2,0:T(8,128)S(1)}, u32[]{:S(2)}, u32[]{:S(2)}) collective-permute-start(f32[3,40,8,1]{3,1,2,0:T(8,128)S(1)} %get-tuple-element.52), channel_id=1, source_target_pairs={{16,0},{32,16},{48,32},{64,48},{80,64},{96,80},{112,96},{128,112},... | collective-permute-start | bytes 11528 | tf_op jit(solution)/shard_map/ppermute | solution.py:31
  85.9 14.1 %collective-permute-start.7 = (f32[3,40,8,1]{3,1,2,0:T(8,128)S(1)}, f32[3,40,8,1]{3,1,2,0:T(8,128)S(1)}, u32[]{:S(2)}, u32[]{:S(2)}) collective-permute-start(f32[3,40,8,1]{3,1,2,0:T(8,128)S(1)} %get-tuple-element.53), channel_id=1, source_target_pairs={{0,16},{16,32},{32,48},{48,64},{64,80},{80,96},{96,112},{112,128},... | collective-permute-start | bytes 11528 | tf_op jit(solution)/shard_map/ppermute | solution.py:30
  101.0 24.1 %copy-start.4 = (pred[512,8]{0,1:T(8,128)(4,1)S(1)}, pred[512,8]{0,1:T(8,128)(4,1)}, u32[]{:S(2)}) copy-start(pred[512,8]{0,1:T(8,128)(4,1)} %iota_compare_fusion.2) | copy-start | bytes 12292
  101.0 14.8 %collective-permute-start.12 = (f32[3,40,8,1]{3,1,2,0:T(8,128)S(1)}, f32[3,40,8,1]{3,1,2,0:T(8,128)S(1)}, u32[]{:S(2)}, u32[]{:S(2)}) collective-permute-start(f32[3,40,8,1]{3,1,2,0:T(8,128)S(1)} %get-tuple-element.41), channel_id=1, source_target_pairs={{16,0},{32,16},{48,32},{64,48},{80,64},{96,80},{112,96},{128,112},... | collective-permute-start | bytes 11528 | tf_op jit(solution)/shard_map/ppermute | solution.py:31
  102.9 15.4 %collective-permute-start.13 = (f32[3,40,8,1]{3,1,2,0:T(8,128)S(1)}, f32[3,40,8,1]{3,1,2,0:T(8,128)S(1)}, u32[]{:S(2)}, u32[]{:S(2)}) collective-permute-start(f32[3,40,8,1]{3,1,2,0:T(8,128)S(1)} %get-tuple-element.42), channel_id=1, source_target_pairs={{0,16},{16,32},{32,48},{48,64},{64,80},{80,96},{96,112},{112,128},... | collective-permute-start | bytes 11528 | tf_op jit(solution)/shard_map/ppermute | solution.py:30
  105.4 13.3 %collective-permute-start.14 = (f32[3,40,1,128]{3,1,2,0:T(8,128)S(1)}, f32[3,40,1,128]{3,1,2,0:T(8,128)S(1)}, u32[]{:S(2)}, u32[]{:S(2)}) collective-permute-start(f32[3,40,1,128]{3,1,2,0:T(8,128)S(1)} %get-tuple-element.45), channel_id=1, source_target_pairs={{1,0},{2,1},{3,2},{4,3},{5,4},{6,5},{7,6},{8,7},{9,8},{10,9},{11,1... | collective-permute-start | bytes 184328 | tf_op jit(solution)/shard_map/ppermute | solution.py:40
  113.9 10.9 %collective-permute-start.15 = (f32[3,40,1,128]{3,1,2,0:T(8,128)S(1)}, f32[3,40,1,128]{3,1,2,0:T(8,128)S(1)}, u32[]{:S(2)}, u32[]{:S(2)}) collective-permute-start(f32[3,40,1,128]{3,1,2,0:T(8,128)S(1)} %get-tuple-element.46), channel_id=1, source_target_pairs={{0,1},{1,2},{2,3},{3,4},{4,5},{5,6},{6,7},{7,8},{8,9},{9,10},{10,1... | collective-permute-start | bytes 184328 | tf_op jit(solution)/shard_map/ppermute | solution.py:39
  126.8 13.5 %collective-permute-start.17 = (f32[512,40]{0,1:T(8,128)S(1)}, f32[512,40]{0,1:T(8,128)S(1)}, u32[]{:S(2)}, u32[]{:S(2)}) collective-permute-start(f32[512,40]{0,1:T(8,128)S(1)} %fusion.45), channel_id=1, source_target_pairs={{0,496},{16,0},{32,16},{48,32},{64,48},{80,64},{96,80},{112,96},{1... | collective-permute-start | bytes 245768 | tf_op jit(solution)/shard_map/ppermute | solution.py:202
  132.4 9.7 %collective-permute-start.16 = (f32[512,40]{0,1:T(8,128)S(1)}, f32[512,40]{0,1:T(8,128)S(1)}, u32[]{:S(2)}, u32[]{:S(2)}) collective-permute-start(f32[512,40]{0,1:T(8,128)S(1)} %fusion.45), channel_id=1, source_target_pairs={{0,16},{16,32},{32,48},{48,64},{64,80},{80,96},{96,112},{112,128},... | collective-permute-start | bytes 245768 | tf_op jit(solution)/shard_map/ppermute | solution.py:201
  134.4 7.7 %collective-permute-start.19 = (f32[256,40]{0,1:T(8,128)S(1)}, f32[256,40]{0,1:T(8,128)S(1)}, u32[]{:S(2)}, u32[]{:S(2)}) collective-permute-start(f32[256,40]{0,1:T(8,128)S(1)} %split.5), channel_id=1, source_target_pairs={{0,480},{16,496},{32,0},{48,16},{64,32},{80,48},{96,64},{112,80},{... | collective-permute-start | bytes 122888 | tf_op jit(solution)/shard_map/ppermute | solution.py:207
  136.7 13.0 %collective-permute-start.18 = (f32[256,40]{0,1:T(8,128)S(1)}, f32[256,40]{0,1:T(8,128)S(1)}, u32[]{:S(2)}, u32[]{:S(2)}) collective-permute-start(f32[256,40]{0,1:T(8,128)S(1)} %split.5), channel_id=1, source_target_pairs={{0,32},{16,48},{32,64},{48,80},{64,96},{80,112},{96,128},{112,144}... | collective-permute-start | bytes 122888 | tf_op jit(solution)/shard_map/ppermute | solution.py:206
  149.8 24.5 %collective-permute-start.21 = (f32[512,40]{0,1:T(8,128)S(1)}, f32[512,40]{0,1:T(8,128)S(1)}, u32[]{:S(2)}, u32[]{:S(2)}) collective-permute-start(f32[512,40]{0,1:T(8,128)S(1)} %pad_maximum_fusion.3), channel_id=1, source_target_pairs={{1,0},{2,1},{3,2},{4,3},{5,4},{6,5},{7,6},{8,7},{9,8},{10,9},{11,1... | collective-permute-start | bytes 245768 | tf_op jit(solution)/shard_map/ppermute | solution.py:213
  151.7 22.6 %collective-permute-start.20 = (f32[512,40]{0,1:T(8,128)S(1)}, f32[512,40]{0,1:T(8,128)S(1)}, u32[]{:S(2)}, u32[]{:S(2)}) collective-permute-start(f32[512,40]{0,1:T(8,128)S(1)} %pad_maximum_fusion.3), channel_id=1, source_target_pairs={{0,1},{1,2},{2,3},{3,4},{4,5},{5,6},{6,7},{7,8},{8,9},{9,10},{10,1... | collective-permute-start | bytes 245768 | tf_op jit(solution)/shard_map/ppermute | solution.py:212
  159.5 15.0 %collective-permute-start.23 = (f32[256,40]{0,1:T(8,128)S(1)}, f32[256,40]{0,1:T(8,128)S(1)}, u32[]{:S(2)}, u32[]{:S(2)}) collective-permute-start(f32[256,40]{0,1:T(8,128)S(1)} %get-tuple-element.71), channel_id=1, source_target_pairs={{2,0},{3,1},{4,2},{5,3},{6,4},{7,5},{8,6},{9,7},{10,8},{11,9},{12,... | collective-permute-start | bytes 122888 | tf_op jit(solution)/shard_map/ppermute | solution.py:218
  162.4 15.6 %collective-permute-start.22 = (f32[256,40]{0,1:T(8,128)S(1)}, f32[256,40]{0,1:T(8,128)S(1)}, u32[]{:S(2)}, u32[]{:S(2)}) collective-permute-start(f32[256,40]{0,1:T(8,128)S(1)} %get-tuple-element.71), channel_id=1, source_target_pairs={{0,2},{1,3},{2,4},{3,5},{4,6},{5,7},{6,8},{7,9},{8,10},{9,11},{10,... | collective-permute-start | bytes 122888 | tf_op jit(solution)/shard_map/ppermute | solution.py:217

commit v3 on v2

--- a/solution.py
+++ b/solution.py
@@ -17,10 +17,6 @@
 
 def ring_pairs(size, step):
     return [(i, (i + step) % size) for i in range(size)]
-
-
-def line_pairs(size, step):
-    return [(i, i + step) for i in range(size) if 0 <= i + step < size]
 
 
 def lon_edges(array):
@@ -32,12 +28,16 @@
     return left, right
 
 
+def lat_shift(array, step):
+    size = lax.axis_size("lat")
+    source = lax.axis_index("lat") - step
+    moved = lax.ppermute(array, "lat", ring_pairs(size, step))
+    return jnp.where((source >= 0) & (source < size), moved, 0.0)
+
+
 def lat_edges(array):
-    size = lax.axis_size("lat")
-    up = [(i, i + 1) for i in range(size - 1)]
-    down = [(i + 1, i) for i in range(size - 1)]
-    before = lax.ppermute(array[:, :, -1:, :], "lat", up)
-    after = lax.ppermute(array[:, :, :1, :], "lat", down)
+    before = lat_shift(array[:, :, -1:, :], 1)
+    after = lat_shift(array[:, :, :1, :], -1)
     return before, after
 
 
@@ -106,21 +106,6 @@
     distance_sq = (lon_gap * lon_gap + lat_gap * lat_gap).astype(jnp.float32)
     radius_sq = (radius_obs * radius_obs).astype(jnp.float32)[:, None]
     return jnp.square(jnp.maximum(1.0 - distance_sq / radius_sq, 0.0))
-
-
-def neighbourhood_sum(table):
-    lon_n = lax.axis_size("lon")
-    lat_n = lax.axis_size("lat")
-    row = (
-        table
-        + lax.ppermute(table, "lon", ring_pairs(lon_n, 1))
-        + lax.ppermute(table, "lon", ring_pairs(lon_n, -1))
-    )
-    return (
-        row
-        + lax.ppermute(row, "lat", line_pairs(lat_n, 1))
-        + lax.ppermute(row, "lat", line_pairs(lat_n, -1))
-    )
 
 
 def tile_origin(state):
@@ -209,13 +194,13 @@
     both = jnp.concatenate([wide0, both[NB:]])
     both = (
         both
-        + lax.ppermute(both, "lat", line_pairs(lat_size, 1))
-        + lax.ppermute(both, "lat", line_pairs(lat_size, -1))
+        + lat_shift(both, 1)
+        + lat_shift(both, -1)
     )
     priors = (
         both[:NB]
-        + lax.ppermute(wide0, "lat", line_pairs(lat_size, 2))
-        + lax.ppermute(wide0, "lat", line_pairs(lat_size, -2))
+        + lat_shift(wide0, 2)
+        + lat_shift(wide0, -2)
     )
     raw1 = both[NB:]
     gains, anomaly = statistics(priors, value0, error0, member_count)

time: 202 us -> 210 us (1.040)
  the two profiles are of different devices: /device:TPU:24 before, /device:TPU:1 now
where the time goes in v3:
time: 210 us; the launch traced here: 209 us
  starting transfers between devices  129 us (61%)
  waiting for transfers between devices  33.1 us (16%)
  matrix products  20.3 us (10%)
  local copies, waits for them, and re-layouts  16.5 us (8%)
  other arithmetic  8.76 us (4%)
    ppermute x12, starting transfers between devices, lat_shift(): moved = lax.ppermute(array, 'lat', ring_pairs(size, step))  73.2 us
    ppermute x4, starting transfers between devices, lon_edges(): right = lax.ppermute(array[..., :1], 'lon', down)  28.8 us
    ppermute x12, waiting for transfers between devices, lat_shift(): moved = lax.ppermute(array, 'lat', ring_pairs(size, step))  12.3 us
    ppermute x1, starting transfers between devices, shards(): lax.ppermute(table0, 'lon', ring_pairs(lon_size, -2))  10.9 us
    dot_general x6, matrix products, update_group(): jnp.einsum('om,foc->fmc', gains, covariance * weights[None], precision=la...  9.1 us
    dot_general x6, matrix products, update_group(): jnp.einsum('om,fmc->foc', anomaly, deviation, precision=lax.Precision.HIGH)  8.85 us
    ppermute x4, starting transfers between devices, lon_edges(): left = lax.ppermute(array[..., -1:], 'lon', up)  8.77 us
    ppermute x1, waiting for transfers between devices, shards(): lax.ppermute(table0, 'lon', ring_pairs(lon_size, 2))  8.67 us
  transfers between devices with their start and end apart: 24, of which 6 were waited for; matrix products, arithmetic and copies ran while one was open for 8% of the time, Pallas kernels for 0%

profile of v3, /device:TPU:1, one launch (start us, length us, event | category | flops | bytes accessed | tf_op | source)
XLA Modules:
  0.0 209.0 jit_solution(4609040293344997593)
XLA Ops:
  0.0 2.0 fusion.153
  2.1 15.7 %collective-permute-start.2 = (f32[3,40,1,128]{3,1,2,0:T(8,128)}, f32[3,40,1,128]{3,1,2,0:T(8,128)}, u32[]{:S(2)}, u32[]{:S(2)}) collective-permute-start(f32[3,40,1,128]{3,1,2,0:T(8,128)} %bitcast.29), channel_id=1, source_target_pairs={{0,15},{1,0},{2,1},{3,2},{4,3},{5,4},{6,5},{7,6},{8,7},{9,8},{10,9... | collective-permute-start | bytes 184328 | tf_op jit(solution)/shard_map/ppermute | solution.py:34
  17.8 1.9 collective-permute-start.3
  19.7 1.4 fusion.155
  21.1 0.9 copy.73
  22.0 2.9 %collective-permute-start = (f32[3,40,8,1]{3,1,2,0:T(8,128)}, f32[3,40,8,1]{3,1,2,0:T(8,128)}, u32[]{:S(2)}, u32[]{:S(2)}) collective-permute-start(f32[3,40,8,1]{3,1,2,0:T(8,128)} %copy.73), channel_id=1, source_target_pairs={{16,0},{32,16},{48,32},{64,48},{80,64},{96,80},{112,96},{128,112},... | collective-permute-start | bytes 11528 | tf_op jit(solution)/shard_map/ppermute | solution.py:27
  24.8 0.9 copy.74
  25.7 3.0 %collective-permute-start.1 = (f32[3,40,8,1]{3,1,2,0:T(8,128)}, f32[3,40,8,1]{3,1,2,0:T(8,128)}, u32[]{:S(2)}, u32[]{:S(2)}) collective-permute-start(f32[3,40,8,1]{3,1,2,0:T(8,128)} %copy.74), channel_id=1, source_target_pairs={{0,16},{16,32},{32,48},{48,64},{64,80},{80,96},{96,112},{112,128},... | collective-permute-start | bytes 11528 | tf_op jit(solution)/shard_map/ppermute | solution.py:26
  29.0 1.0 gather_fusion
  30.6 0.4 slice_reduce_fusion
  31.1 1.0 fusion.154
  32.1 0.9 fusion.156
  33.2 0.6 iota_compare_fusion.2
  34.1 1.0 gather_fusion.1
  35.1 0.9 slice_reduce_fusion.2
  36.0 1.1 copy.79
  37.1 1.9 copy.76
  39.0 1.1 copy.75
  40.2 1.8 multiply_multiply_fusion
  42.0 0.8 broadcast_select_fusion.7
  42.9 1.6 fusion.70
  45.1 3.5 %collective-permute-start.9 = (f32[3,40,1,128]{3,1,2,0:T(8,128)S(1)}, f32[3,40,1,128]{3,1,2,0:T(8,128)S(1)}, u32[]{:S(2)}, u32[]{:S(2)}) collective-permute-start(f32[3,40,1,128]{3,1,2,0:T(8,128)S(1)} %get-tuple-element.62), channel_id=1, source_target_pairs={{0,1},{1,2},{2,3},{3,4},{4,5},{5,6},{6,7},{7,8},{8,9},{9,10},{10,1... | collective-permute-start | bytes 184328 | tf_op jit(solution)/shard_map/ppermute | solution.py:34
  48.7 8.0 %collective-permute-start.8 = (f32[3,40,1,128]{3,1,2,0:T(8,128)S(1)}, f32[3,40,1,128]{3,1,2,0:T(8,128)S(1)}, u32[]{:S(2)}, u32[]{:S(2)}) collective-permute-start(f32[3,40,1,128]{3,1,2,0:T(8,128)S(1)} %get-tuple-element.63), channel_id=1, source_target_pairs={{0,15},{1,0},{2,1},{3,2},{4,3},{5,4},{6,5},{7,6},{8,7},{9,8},{10,9... | collective-permute-start | bytes 184328 | tf_op jit(solution)/shard_map/ppermute | solution.py:34
  56.8 4.4 %collective-permute-start.4 = (f32[3,40,8,1]{3,1,2,0:T(8,128)S(1)}, f32[3,40,8,1]{3,1,2,0:T(8,128)S(1)}, u32[]{:S(2)}, u32[]{:S(2)}) collective-permute-start(f32[3,40,8,1]{3,1,2,0:T(8,128)S(1)} %get-tuple-element.60), channel_id=1, source_target_pairs={{16,0},{32,16},{48,32},{64,48},{80,64},{96,80},{112,96},{128,112},... | collective-permute-start | bytes 11528 | tf_op jit(solution)/shard_map/ppermute | solution.py:27
  61.1 1.9 collective-permute-start.5
  63.1 3.8 %collective-permute-done.4 = f32[3,40,8,1]{3,1,2,0:T(8,128)S(1)} collective-permute-done((f32[3,40,8,1]{3,1,2,0:T(8,128)S(1)}, f32[3,40,8,1]{3,1,2,0:T(8,128)S(1)}, u32[]{:S(2)}, u32[]{:S(2)}) %collective-permute-start.4) | collective-permute-done | bytes 3872 | tf_op jit(solution)/shard_map/ppermute | solution.py:27
  66.9 2.6 %collective-permute-done.5 = f32[3,40,8,1]{3,1,2,0:T(8,128)S(1)} collective-permute-done((f32[3,40,8,1]{3,1,2,0:T(8,128)S(1)}, f32[3,40,8,1]{3,1,2,0:T(8,128)S(1)}, u32[]{:S(2)}, u32[]{:S(2)}) %collective-permute-start.5) | collective-permute-done | bytes 3872 | tf_op jit(solution)/shard_map/ppermute | solution.py:26
  69.5 0.5 fusion.77
  70.4 7.3 %collective-permute-start.10 = (f32[3,40,1,128]{3,1,2,0:T(8,128)S(1)}, f32[3,40,1,128]{3,1,2,0:T(8,128)S(1)}, u32[]{:S(2)}, u32[]{:S(2)}) collective-permute-start(f32[3,40,1,128]{3,1,2,0:T(8,128)S(1)} %get-tuple-element.56), channel_id=1, source_target_pairs={{0,15},{1,0},{2,1},{3,2},{4,3},{5,4},{6,5},{7,6},{8,7},{9,8},{10,9... | collective-permute-start | bytes 184328 | tf_op jit(solution)/shard_map/ppermute | solution.py:34
  77.8 1.9 collective-permute-start.11
  79.7 13.3 %collective-permute-start.6 = (f32[3,40,8,1]{3,1,2,0:T(8,128)S(1)}, f32[3,40,8,1]{3,1,2,0:T(8,128)S(1)}, u32[]{:S(2)}, u32[]{:S(2)}) collective-permute-start(f32[3,40,8,1]{3,1,2,0:T(8,128)S(1)} %get-tuple-element.52), channel_id=1, source_target_pairs={{16,0},{32,16},{48,32},{64,48},{80,64},{96,80},{112,96},{128,112},... | collective-permute-start | bytes 11528 | tf_op jit(solution)/shard_map/ppermute | solution.py:27
  93.0 1.9 collective-permute-start.7
  95.0 5.7 %collective-permute-done.7 = f32[3,40,8,1]{3,1,2,0:T(8,128)S(1)} collective-permute-done((f32[3,40,8,1]{3,1,2,0:T(8,128)S(1)}, f32[3,40,8,1]{3,1,2,0:T(8,128)S(1)}, u32[]{:S(2)}, u32[]{:S(2)}) %collective-permute-start.7) | collective-permute-done | bytes 3872 | tf_op jit(solution)/shard_map/ppermute | solution.py:26
  100.6 0.4 fusion.143
  101.7 8.3 %collective-permute-start.12 = (f32[3,40,8,1]{3,1,2,0:T(8,128)S(1)}, f32[3,40,8,1]{3,1,2,0:T(8,128)S(1)}, u32[]{:S(2)}, u32[]{:S(2)}) collective-permute-start(f32[3,40,8,1]{3,1,2,0:T(8,128)S(1)} %get-tuple-element.41), channel_id=1, source_target_pairs={{16,0},{32,16},{48,32},{64,48},{80,64},{96,80},{112,96},{128,112},... | collective-permute-start | bytes 11528 | tf_op jit(solution)/shard_map/ppermute | solution.py:27
  110.0 1.9 collective-permute-start.13
  112.0 9.5 %collective-permute-start.14 = (f32[3,40,1,128]{3,1,2,0:T(8,128)S(1)}, f32[3,40,1,128]{3,1,2,0:T(8,128)S(1)}, u32[]{:S(2)}, u32[]{:S(2)}) collective-permute-start(f32[3,40,1,128]{3,1,2,0:T(8,128)S(1)} %get-tuple-element.45), channel_id=1, source_target_pairs={{0,15},{1,0},{2,1},{3,2},{4,3},{5,4},{6,5},{7,6},{8,7},{9,8},{10,9... | collective-permute-start | bytes 184328 | tf_op jit(solution)/shard_map/ppermute | solution.py:34
  121.5 1.9 collective-permute-start.15
  123.9 8.6 %collective-permute-done.15 = f32[3,40,1,128]{3,1,2,0:T(8,128)S(1)} collective-permute-done((f32[3,40,1,128]{3,1,2,0:T(8,128)S(1)}, f32[3,40,1,128]{3,1,2,0:T(8,128)S(1)}, u32[]{:S(2)}, u32[]{:S(2)}) %collective-permute-start.15) | collective-permute-done | bytes 61472 | tf_op jit(solution)/shard_map/ppermute | solution.py:34
  132.7 1.7 fusion.45
  134.4 3.8 %collective-permute-start.17 = (f32[512,40]{0,1:T(8,128)S(1)}, f32[512,40]{0,1:T(8,128)S(1)}, u32[]{:S(2)}, u32[]{:S(2)}) collective-permute-start(f32[512,40]{0,1:T(8,128)S(1)} %fusion.45), channel_id=1, source_target_pairs={{0,496},{16,0},{32,16},{48,32},{64,48},{80,64},{96,80},{112,96},{1... | collective-permute-start | bytes 245768 | tf_op jit(solution)/shard_map/ppermute | solution.py:187
  138.3 1.9 collective-permute-start.16
  140.3 10.9 %collective-permute-start.19 = (f32[256,40]{0,1:T(8,128)S(1)}, f32[256,40]{0,1:T(8,128)S(1)}, u32[]{:S(2)}, u32[]{:S(2)}) collective-permute-start(f32[256,40]{0,1:T(8,128)S(1)} %split.5), channel_id=1, source_target_pairs={{0,480},{16,496},{32,0},{48,16},{64,32},{80,48},{96,64},{112,80},{... | collective-permute-start | bytes 122888 | tf_op jit(solution)/shard_map/ppermute | solution.py:192
  151.1 1.9 collective-permute-start.18
  153.1 8.7 %collective-permute-done.18 = f32[256,40]{0,1:T(8,128)S(1)} collective-permute-done((f32[256,40]{0,1:T(8,128)S(1)}, f32[256,40]{0,1:T(8,128)S(1)}, u32[]{:S(2)}, u32[]{:S(2)}) %collective-permute-start.18) | collective-permute-done | bytes 40992 | tf_op jit(solution)/shard_map/ppermute | solution.py:191
  161.8 1.9 collective-permute-start.21
  163.8 7.3 %collective-permute-start.20 = (f32[512,40]{0,1:T(8,128)S(1)}, f32[512,40]{0,1:T(8,128)S(1)}, u32[]{:S(2)}, u32[]{:S(2)}) collective-permute-start(f32[512,40]{0,1:T(8,128)S(1)} %pad_maximum_fusion.3), channel_id=1, source_target_pairs={{0,1},{1,2},{2,3},{3,4},{4,5},{5,6},{6,7},{7,8},{8,9},{9,10},{10,1... | collective-permute-start | bytes 245768 | tf_op jit(solution)/shard_map/ppermute | solution.py:34
  171.1 1.9 collective-permute-start.23
  173.0 12.3 %collective-permute-start.22 = (f32[256,40]{0,1:T(8,128)S(1)}, f32[256,40]{0,1:T(8,128)S(1)}, u32[]{:S(2)}, u32[]{:S(2)}) collective-permute-start(f32[256,40]{0,1:T(8,128)S(1)} %get-tuple-element.71), channel_id=1, source_target_pairs={{0,2},{1,3},{2,4},{3,5},{4,6},{5,7},{6,8},{7,9},{8,10},{9,11},{10,... | collective-permute-start | bytes 122888 | tf_op jit(solution)/shard_map/ppermute | solution.py:34
  185.3 3.7 %collective-permute-done.22 = f32[256,40]{0,1:T(8,128)S(1)} collective-permute-done((f32[256,40]{0,1:T(8,128)S(1)}, f32[256,40]{0,1:T(8,128)S(1)}, u32[]{:S(2)}, u32[]{:S(2)}) %collective-permute-start.22) | collective-permute-done | bytes 40992 | tf_op jit(solution)/shard_map/ppermute | solution.py:34
  189.1 0.5 fusion.50
  189.6 1.4 fusion.65
  191.3 1.5 fusion.170
  192.9 1.4 fusion.82
  194.3 1.5 fusion.44
  195.9 1.4 fusion.66
  197.3 1.5 fusion.172
  198.9 1.4 fusion.84
  200.3 1.5 fusion.43
  201.9 1.7 fusion.67
  203.5 1.5 fusion.173
  205.1 1.4 fusion.86
  206.5 1.5 fusion.42
  208.1 0.9 pad_maximum_fusion
  (106 shorter events, 4.2 us)
Async XLA Ops:
  0.0 31.1 %copy-start = (f32[9,40,8,128]{3,2,1,0:T(8,128)S(1)}, f32[9,40,8,128]{3,2,1,0:T(8,128)}, u32[]{:S(2)}) copy-start(f32[9,40,8,128]{3,2,1,0:T(8,128)} %param.10) | copy-start | bytes 4423684
  0.0 28.7 %copy-start.5 = (s32[512]{0:T(512)S(1)}, s32[512]{0:T(512)}, u32[]{:S(2)}) copy-start(s32[512]{0:T(512)} %param.15) | copy-start | bytes 6148
  0.0 28.8 %copy-start.8 = (s32[512]{0:T(512)S(1)}, s32[512]{0:T(512)}, u32[]{:S(2)}) copy-start(s32[512]{0:T(512)} %param.14) | copy-start | bytes 6148
  0.0 28.8 %copy-start.9 = (s32[512]{0:T(512)S(1)}, s32[512]{0:T(512)}, u32[]{:S(2)}) copy-start(s32[512]{0:T(512)} %param.13) | copy-start | bytes 6148
  0.0 28.8 %copy-start.10 = (s32[512]{0:T(512)S(1)}, s32[512]{0:T(512)}, u32[]{:S(2)}) copy-start(s32[512]{0:T(512)} %param.12) | copy-start | bytes 6148
  0.0 28.8 %copy-start.11 = (s32[512]{0:T(512)S(1)}, s32[512]{0:T(512)}, u32[]{:S(2)}) copy-start(s32[512]{0:T(512)} %param.11) | copy-start | bytes 6148
  2.1 40.0 %collective-permute-start.2 = (f32[3,40,1,128]{3,1,2,0:T(8,128)}, f32[3,40,1,128]{3,1,2,0:T(8,128)}, u32[]{:S(2)}, u32[]{:S(2)}) collective-permute-start(f32[3,40,1,128]{3,1,2,0:T(8,128)} %bitcast.29), channel_id=1, source_target_pairs={{0,15},{1,0},{2,1},{3,2},{4,3},{5,4},{6,5},{7,6},{8,7},{9,8},{10,9... | collective-permute-start | bytes 184328 | tf_op jit(solution)/shard_map/ppermute | solution.py:34
  17.8 25.1 %collective-permute-start.3 = (f32[3,40,1,128]{3,1,2,0:T(8,128)}, f32[3,40,1,128]{3,1,2,0:T(8,128)}, u32[]{:S(2)}, u32[]{:S(2)}) collective-permute-start(f32[3,40,1,128]{3,1,2,0:T(8,128)} %bitcast.30), channel_id=1, source_target_pairs={{0,1},{1,2},{2,3},{3,4},{4,5},{5,6},{6,7},{7,8},{8,9},{9,10},{10,1... | collective-permute-start | bytes 184328 | tf_op jit(solution)/shard_map/ppermute | solution.py:34
  22.0 20.9 %collective-permute-start = (f32[3,40,8,1]{3,1,2,0:T(8,128)}, f32[3,40,8,1]{3,1,2,0:T(8,128)}, u32[]{:S(2)}, u32[]{:S(2)}) collective-permute-start(f32[3,40,8,1]{3,1,2,0:T(8,128)} %copy.73), channel_id=1, source_target_pairs={{16,0},{32,16},{48,32},{64,48},{80,64},{96,80},{112,96},{128,112},... | collective-permute-start | bytes 11528 | tf_op jit(solution)/shard_map/ppermute | solution.py:27
  25.7 17.2 %collective-permute-start.1 = (f32[3,40,8,1]{3,1,2,0:T(8,128)}, f32[3,40,8,1]{3,1,2,0:T(8,128)}, u32[]{:S(2)}, u32[]{:S(2)}) collective-permute-start(f32[3,40,8,1]{3,1,2,0:T(8,128)} %copy.74), channel_id=1, source_target_pairs={{0,16},{16,32},{32,48},{48,64},{64,80},{80,96},{96,112},{112,128},... | collective-permute-start | bytes 11528 | tf_op jit(solution)/shard_map/ppermute | solution.py:26
  31.1 2.8 %copy-start.6 = (f32[512]{0:T(512)S(1)}, f32[512]{0:T(512)}, u32[]{:S(2)}) copy-start(f32[512]{0:T(512)} %param.17) | copy-start | bytes 6148
  31.1 2.8 %copy-start.7 = (f32[512]{0:T(512)S(1)}, f32[512]{0:T(512)}, u32[]{:S(2)}) copy-start(f32[512]{0:T(512)} %param.16) | copy-start | bytes 6148
  45.1 18.0 %collective-permute-start.9 = (f32[3,40,1,128]{3,1,2,0:T(8,128)S(1)}, f32[3,40,1,128]{3,1,2,0:T(8,128)S(1)}, u32[]{:S(2)}, u32[]{:S(2)}) collective-permute-start(f32[3,40,1,128]{3,1,2,0:T(8,128)S(1)} %get-tuple-element.62), channel_id=1, source_target_pairs={{0,1},{1,2},{2,3},{3,4},{4,5},{5,6},{6,7},{7,8},{8,9},{9,10},{10,1... | collective-permute-start | bytes 184328 | tf_op jit(solution)/shard_map/ppermute | solution.py:34
  48.7 14.4 %collective-permute-start.8 = (f32[3,40,1,128]{3,1,2,0:T(8,128)S(1)}, f32[3,40,1,128]{3,1,2,0:T(8,128)S(1)}, u32[]{:S(2)}, u32[]{:S(2)}) collective-permute-start(f32[3,40,1,128]{3,1,2,0:T(8,128)S(1)} %get-tuple-element.63), channel_id=1, source_target_pairs={{0,15},{1,0},{2,1},{3,2},{4,3},{5,4},{6,5},{7,6},{8,7},{9,8},{10,9... | collective-permute-start | bytes 184328 | tf_op jit(solution)/shard_map/ppermute | solution.py:34
  56.8 10.1 %collective-permute-start.4 = (f32[3,40,8,1]{3,1,2,0:T(8,128)S(1)}, f32[3,40,8,1]{3,1,2,0:T(8,128)S(1)}, u32[]{:S(2)}, u32[]{:S(2)}) collective-permute-start(f32[3,40,8,1]{3,1,2,0:T(8,128)S(1)} %get-tuple-element.60), channel_id=1, source_target_pairs={{16,0},{32,16},{48,32},{64,48},{80,64},{96,80},{112,96},{128,112},... | collective-permute-start | bytes 11528 | tf_op jit(solution)/shard_map/ppermute | solution.py:27
  61.1 8.3 %collective-permute-start.5 = (f32[3,40,8,1]{3,1,2,0:T(8,128)S(1)}, f32[3,40,8,1]{3,1,2,0:T(8,128)S(1)}, u32[]{:S(2)}, u32[]{:S(2)}) collective-permute-start(f32[3,40,8,1]{3,1,2,0:T(8,128)S(1)} %get-tuple-element.61), channel_id=1, source_target_pairs={{0,16},{16,32},{32,48},{48,64},{64,80},{80,96},{96,112},{112,128},... | collective-permute-start | bytes 11528 | tf_op jit(solution)/shard_map/ppermute | solution.py:26
  70.0 30.6 %copy-start.4 = (f32[3]{0:T(128)S(1)}, f32[3]{0:T(128)}, u32[]{:S(2)}) copy-start(f32[3]{0:T(128)} %constant.124) | copy-start | bytes 40
  70.4 24.5 %collective-permute-start.10 = (f32[3,40,1,128]{3,1,2,0:T(8,128)S(1)}, f32[3,40,1,128]{3,1,2,0:T(8,128)S(1)}, u32[]{:S(2)}, u32[]{:S(2)}) collective-permute-start(f32[3,40,1,128]{3,1,2,0:T(8,128)S(1)} %get-tuple-element.56), channel_id=1, source_target_pairs={{0,15},{1,0},{2,1},{3,2},{4,3},{5,4},{6,5},{7,6},{8,7},{9,8},{10,9... | collective-permute-start | bytes 184328 | tf_op jit(solution)/shard_map/ppermute | solution.py:34
  77.8 17.2 %collective-permute-start.11 = (f32[3,40,1,128]{3,1,2,0:T(8,128)S(1)}, f32[3,40,1,128]{3,1,2,0:T(8,128)S(1)}, u32[]{:S(2)}, u32[]{:S(2)}) collective-permute-start(f32[3,40,1,128]{3,1,2,0:T(8,128)S(1)} %get-tuple-element.57), channel_id=1, source_target_pairs={{0,1},{1,2},{2,3},{3,4},{4,5},{5,6},{6,7},{7,8},{8,9},{9,10},{10,1... | collective-permute-start | bytes 184328 | tf_op jit(solution)/shard_map/ppermute | solution.py:34
  79.7 15.3 %collective-permute-start.6 = (f32[3,40,8,1]{3,1,2,0:T(8,128)S(1)}, f32[3,40,8,1]{3,1,2,0:T(8,128)S(1)}, u32[]{:S(2)}, u32[]{:S(2)}) collective-permute-start(f32[3,40,8,1]{3,1,2,0:T(8,128)S(1)} %get-tuple-element.52), channel_id=1, source_target_pairs={{16,0},{32,16},{48,32},{64,48},{80,64},{96,80},{112,96},{128,112},... | collective-permute-start | bytes 11528 | tf_op jit(solution)/shard_map/ppermute | solution.py:27
  93.0 7.7 %collective-permute-start.7 = (f32[3,40,8,1]{3,1,2,0:T(8,128)S(1)}, f32[3,40,8,1]{3,1,2,0:T(8,128)S(1)}, u32[]{:S(2)}, u32[]{:S(2)}) collective-permute-start(f32[3,40,8,1]{3,1,2,0:T(8,128)S(1)} %get-tuple-element.53), channel_id=1, source_target_pairs={{0,16},{16,32},{32,48},{48,64},{64,80},{80,96},{96,112},{112,128},... | collective-permute-start | bytes 11528 | tf_op jit(solution)/shard_map/ppermute | solution.py:26
  101.7 31.1 %copy-start.3 = (pred[512,8]{0,1:T(8,128)(4,1)S(1)}, pred[512,8]{0,1:T(8,128)(4,1)}, u32[]{:S(2)}) copy-start(pred[512,8]{0,1:T(8,128)(4,1)} %iota_compare_fusion.2) | copy-start | bytes 12292
  101.7 21.7 %collective-permute-start.12 = (f32[3,40,8,1]{3,1,2,0:T(8,128)S(1)}, f32[3,40,8,1]{3,1,2,0:T(8,128)S(1)}, u32[]{:S(2)}, u32[]{:S(2)}) collective-permute-start(f32[3,40,8,1]{3,1,2,0:T(8,128)S(1)} %get-tuple-element.41), channel_id=1, source_target_pairs={{16,0},{32,16},{48,32},{64,48},{80,64},{96,80},{112,96},{128,112},... | collective-permute-start | bytes 11528 | tf_op jit(solution)/shard_map/ppermute | solution.py:27
  110.0 13.4 %collective-permute-start.13 = (f32[3,40,8,1]{3,1,2,0:T(8,128)S(1)}, f32[3,40,8,1]{3,1,2,0:T(8,128)S(1)}, u32[]{:S(2)}, u32[]{:S(2)}) collective-permute-start(f32[3,40,8,1]{3,1,2,0:T(8,128)S(1)} %get-tuple-element.42), channel_id=1, source_target_pairs={{0,16},{16,32},{32,48},{48,64},{64,80},{80,96},{96,112},{112,128},... | collective-permute-start | bytes 11528 | tf_op jit(solution)/shard_map/ppermute | solution.py:26
  112.0 11.9 %collective-permute-start.14 = (f32[3,40,1,128]{3,1,2,0:T(8,128)S(1)}, f32[3,40,1,128]{3,1,2,0:T(8,128)S(1)}, u32[]{:S(2)}, u32[]{:S(2)}) collective-permute-start(f32[3,40,1,128]{3,1,2,0:T(8,128)S(1)} %get-tuple-element.45), channel_id=1, source_target_pairs={{0,15},{1,0},{2,1},{3,2},{4,3},{5,4},{6,5},{7,6},{8,7},{9,8},{10,9... | collective-permute-start | bytes 184328 | tf_op jit(solution)/shard_map/ppermute | solution.py:34
  121.5 11.0 %collective-permute-start.15 = (f32[3,40,1,128]{3,1,2,0:T(8,128)S(1)}, f32[3,40,1,128]{3,1,2,0:T(8,128)S(1)}, u32[]{:S(2)}, u32[]{:S(2)}) collective-permute-start(f32[3,40,1,128]{3,1,2,0:T(8,128)S(1)} %get-tuple-element.46), channel_id=1, source_target_pairs={{0,1},{1,2},{2,3},{3,4},{4,5},{5,6},{6,7},{7,8},{8,9},{9,10},{10,1... | collective-permute-start | bytes 184328 | tf_op jit(solution)/shard_map/ppermute | solution.py:34
  132.7 56.3 %copy-start.2 = (f32[256]{0:T(256)S(1)}, f32[256]{0:T(256)}, u32[]{:S(2)}) copy-start(f32[256]{0:T(256)} %get-tuple-element.7) | copy-start | bytes 3076
  134.4 18.6 %collective-permute-start.17 = (f32[512,40]{0,1:T(8,128)S(1)}, f32[512,40]{0,1:T(8,128)S(1)}, u32[]{:S(2)}, u32[]{:S(2)}) collective-permute-start(f32[512,40]{0,1:T(8,128)S(1)} %fusion.45), channel_id=1, source_target_pairs={{0,496},{16,0},{32,16},{48,32},{64,48},{80,64},{96,80},{112,96},{1... | collective-permute-start | bytes 245768 | tf_op jit(solution)/shard_map/ppermute | solution.py:187
  138.3 14.8 %collective-permute-start.16 = (f32[512,40]{0,1:T(8,128)S(1)}, f32[512,40]{0,1:T(8,128)S(1)}, u32[]{:S(2)}, u32[]{:S(2)}) collective-permute-start(f32[512,40]{0,1:T(8,128)S(1)} %fusion.45), channel_id=1, source_target_pairs={{0,16},{16,32},{32,48},{48,64},{64,80},{80,96},{96,112},{112,128},... | collective-permute-start | bytes 245768 | tf_op jit(solution)/shard_map/ppermute | solution.py:186
  140.3 12.9 %collective-permute-start.19 = (f32[256,40]{0,1:T(8,128)S(1)}, f32[256,40]{0,1:T(8,128)S(1)}, u32[]{:S(2)}, u32[]{:S(2)}) collective-permute-start(f32[256,40]{0,1:T(8,128)S(1)} %split.5), channel_id=1, source_target_pairs={{0,480},{16,496},{32,0},{48,16},{64,32},{80,48},{96,64},{112,80},{... | collective-permute-start | bytes 122888 | tf_op jit(solution)/shard_map/ppermute | solution.py:192
  151.1 10.7 %collective-permute-start.18 = (f32[256,40]{0,1:T(8,128)S(1)}, f32[256,40]{0,1:T(8,128)S(1)}, u32[]{:S(2)}, u32[]{:S(2)}) collective-permute-start(f32[256,40]{0,1:T(8,128)S(1)} %split.5), channel_id=1, source_target_pairs={{0,32},{16,48},{32,64},{48,80},{64,96},{80,112},{96,128},{112,144}... | collective-permute-start | bytes 122888 | tf_op jit(solution)/shard_map/ppermute | solution.py:191
  161.8 23.4 %collective-permute-start.21 = (f32[512,40]{0,1:T(8,128)S(1)}, f32[512,40]{0,1:T(8,128)S(1)}, u32[]{:S(2)}, u32[]{:S(2)}) collective-permute-start(f32[512,40]{0,1:T(8,128)S(1)} %pad_maximum_fusion.3), channel_id=1, source_target_pairs={{0,15},{1,0},{2,1},{3,2},{4,3},{5,4},{6,5},{7,6},{8,7},{9,8},{10,9... | collective-permute-start | bytes 245768 | tf_op jit(solution)/shard_map/ppermute | solution.py:34
  163.8 21.5 %collective-permute-start.20 = (f32[512,40]{0,1:T(8,128)S(1)}, f32[512,40]{0,1:T(8,128)S(1)}, u32[]{:S(2)}, u32[]{:S(2)}) collective-permute-start(f32[512,40]{0,1:T(8,128)S(1)} %pad_maximum_fusion.3), channel_id=1, source_target_pairs={{0,1},{1,2},{2,3},{3,4},{4,5},{5,6},{6,7},{7,8},{8,9},{9,10},{10,1... | collective-permute-start | bytes 245768 | tf_op jit(solution)/shard_map/ppermute | solution.py:34
  171.1 14.2 %collective-permute-start.23 = (f32[256,40]{0,1:T(8,128)S(1)}, f32[256,40]{0,1:T(8,128)S(1)}, u32[]{:S(2)}, u32[]{:S(2)}) collective-permute-start(f32[256,40]{0,1:T(8,128)S(1)} %get-tuple-element.71), channel_id=1, source_target_pairs={{0,14},{1,15},{2,0},{3,1},{4,2},{5,3},{6,4},{7,5},{8,6},{9,7},{10,... | collective-permute-start | bytes 122888 | tf_op jit(solution)/shard_map/ppermute | solution.py:34
  173.0 16.0 %collective-permute-start.22 = (f32[256,40]{0,1:T(8,128)S(1)}, f32[256,40]{0,1:T(8,128)S(1)}, u32[]{:S(2)}, u32[]{:S(2)}) collective-permute-start(f32[256,40]{0,1:T(8,128)S(1)} %get-tuple-element.71), channel_id=1, source_target_pairs={{0,2},{1,3},{2,4},{3,5},{4,6},{5,7},{6,8},{7,9},{8,10},{9,11},{10,... | collective-permute-start | bytes 122888 | tf_op jit(solution)/shard_map/ppermute | solution.py:34
  189.1 2.0 copy-start.1

commit v4 on v2

--- a/solution.py
+++ b/solution.py
@@ -67,18 +67,14 @@
     eastward_speed = running_member_set[3:6]
     merid_vel = running_member_set[6:9]
     depths = jnp.array(DEPTHS, jnp.float32)[:, None, None, None]
-    u_left, u_right = lon_edges(eastward_speed)
     v_before, v_after = lat_edges(merid_vel)
     height = height - RATE * depths * (
-        zonal(eastward_speed, u_left, u_right) + meridional(merid_vel, v_before, v_after)
+        zonal_inside(eastward_speed) + meridional(merid_vel, v_before, v_after)
     )
     pressure = couple(height)
-    p_left, p_right = lon_edges(pressure)
     p_before, p_after = lat_edges(pressure)
     eastward_speed = (
-        eastward_speed
-        + RATE * rotation_frequency * merid_vel
-        - RATE * zonal(pressure, p_left, p_right)
+        eastward_speed + RATE * rotation_frequency * merid_vel - RATE * zonal_inside(pressure)
     )
     merid_vel = (
         merid_vel
@@ -86,6 +82,17 @@
         - RATE * meridional(pressure, p_before, p_after)
     )
     return jnp.concatenate([height, eastward_speed, merid_vel])
+
+
+def zonal_inside(values):
+    return zonal(values, values[..., :1], values[..., -1:])
+
+
+def lon_widened(state, width):
+    size = lax.axis_size("lon")
+    left = lax.ppermute(state[..., -width:], "lon", ring_pairs(size, 1))
+    right = lax.ppermute(state[..., :width], "lon", ring_pairs(size, -1))
+    return jnp.concatenate([left, state, right], axis=3)
 
 
 def statistics(priors, values, errors, member_count):
@@ -188,9 +195,11 @@
     batches = [
         (ints[:, b * NB : (b + 1) * NB], floats[:, b * NB : (b + 1) * NB]) for b in range(BATCHES)
     ]
-    state = ensemble
+    width = 2 * STEPS
+    state = lon_widened(ensemble, width)
     for step_index in range(STEPS):
         state = march_prediction(state, rotation_frequency)
+    state = state[..., width : width + cols_tile]
 
     (lon0, lat0, kind0, radius0), (value0, error0) = batches[0]
     (lon1, lat1, kind1, radius1), (value1, error1) = batches[1]

time: 202 us -> 202 us (level)
  the two profiles are of different devices: /device:TPU:24 before, /device:TPU:17 now
where the time goes in v4:
time: 202 us; the launch traced here: 201 us
  starting transfers between devices  104 us (51%)
  waiting for transfers between devices  40.6 us (20%)
  matrix products  20.6 us (10%)
  local copies, waits for them, and re-layouts  19.6 us (10%)
  other arithmetic  16.1 us (8%)
    ppermute x4, starting transfers between devices, lat_edges(): after = lax.ppermute(array[:, :, :1, :], 'lat', down)  21.3 us
    ppermute x4, starting transfers between devices, lat_edges(): before = lax.ppermute(array[:, :, -1:, :], 'lat', up)  20.7 us
    ppermute x4, waiting for transfers between devices, lat_edges(): before = lax.ppermute(array[:, :, -1:, :], 'lat', up)  20.6 us
    ppermute x1, starting transfers between devices, shards(): lax.ppermute(both, 'lon', ring_pairs(lon_size, -1))  11 us
    ppermute x1, starting transfers between devices, shards(): lax.ppermute(table0, 'lon', ring_pairs(lon_size, -2))  9.6 us
    dot_general x6, matrix products, update_group(): jnp.einsum('om,foc->fmc', gains, covariance * weights[None], precision=la...  9.11 us
    ppermute x1, starting transfers between devices, shards(): lax.ppermute(both, 'lon', ring_pairs(lon_size, 1))  9.02 us
    dot_general x6, matrix products, update_group(): jnp.einsum('om,fmc->foc', anomaly, deviation, precision=lax.Precision.HIGH)  8.85 us
  transfers between devices with their start and end apart: 18, of which 10 were waited for; matrix products, arithmetic and copies ran while one was open for 8% of the time, Pallas kernels for 0%

profile of v4, /device:TPU:17, one launch (start us, length us, event | category | flops | bytes accessed | tf_op | source)
XLA Modules:
  0.0 201.3 jit_solution(6617230741893601439)
XLA Ops:
  0.0 2.3 %fusion.138 = (f32[9,40,8,4]{3,2,1,0:T(8,128)S(1)}, f32[9,40,8,4]{3,2,1,0:T(8,128)S(1)}) fusion(f32[9,40,8,128]{3,2,1,0:T(8,128)} %param.10), kind=kLoop, calls=%fused_computation.243 | loop fusion | bytes 184320 | tf_op jit(solution)/shard_map/slice | solution.py:93
  2.4 0.6 copy.52
  3.0 2.6 %collective-permute-start.1 = (f32[9,40,8,4]{1,2,3,0:T(8,128)S(1)}, f32[9,40,8,4]{1,2,3,0:T(8,128)S(1)}, u32[]{:S(2)}, u32[]{:S(2)}) collective-permute-start(f32[9,40,8,4]{1,2,3,0:T(8,128)S(1)} %copy.52), channel_id=1, source_target_pairs={{0,496},{16,0},{32,16},{48,32},{64,48},{80,64},{96,80},{112,96},{1... | collective-permute-start | bytes 138248 | tf_op jit(solution)/shard_map/ppermute | solution.py:94
  5.6 0.6 copy.51
  6.1 3.0 %collective-permute-start = (f32[9,40,8,4]{1,2,3,0:T(8,128)S(1)}, f32[9,40,8,4]{1,2,3,0:T(8,128)S(1)}, u32[]{:S(2)}, u32[]{:S(2)}) collective-permute-start(f32[9,40,8,4]{1,2,3,0:T(8,128)S(1)} %copy.51), channel_id=1, source_target_pairs={{0,16},{16,32},{32,48},{48,64},{64,80},{80,96},{96,112},{112,128},... | collective-permute-start | bytes 138248 | tf_op jit(solution)/shard_map/ppermute | solution.py:93
  9.4 1.0 gather_fusion
  11.7 1.0 gather_fusion.1
  12.7 0.8 slice_reduce_fusion.5
  13.7 0.6 iota_compare_fusion.2
  14.3 2.9 %multiply_multiply_fusion = (f32[256,1024]{0,1:T(8,128)}, f32[256,1024]{0,1:T(8,128)}) fusion(f32[256]{0:T(256)S(1)} %get-tuple-element.9, s32[256]{0:T(256)S(1)} %get-tuple-element.12, s32[256]{0:T(256)S(1)} %get-tuple-element.11, s32[1024]{0:T(1024)S(1)} %get-tuple-element.92, s32[1024]{0:T(1024)S(1)} %get-tuple-element.93, f32[256]{0:T(256)S(1)} %get-tuple-element.10, ...), kind=kLoop, calls=%fused_computation.72 | loop fusion | flops 12582912 | bytes 2111488 | tf_op jit(solution)/shard_map/mul | solution.py:163
  17.2 0.6 sine_multiply_fusion
  17.8 1.4 copy.29
  19.2 1.7 copy.30
  20.9 0.7 copy-done.6
  21.6 1.7 copy.28
  23.3 3.6 %pad_maximum_fusion = f32[9,40,8,136]{3,1,2,0:T(8,128)S(1)} fusion(f32[9,40,8,4]{3,1,2,0:T(8,128)} %copy.30, f32[9,40,8,128]{3,1,2,0:T(8,128)} %copy.29, f32[9,40,8,4]{3,1,2,0:T(8,128)} %copy.28), kind=kLoop, calls=%fused_computation.14 | loop fusion | flops 783360 | bytes 3133440 | tf_op jit(solution)/shard_map/concatenate | solution.py:95
  26.9 0.9 pad_maximum_fusion.14
  27.8 1.6 fusion.137
  29.4 12.3 %collective-permute-start.2 = (f32[3,40,1,136]{3,1,2,0:T(8,128)}, f32[3,40,1,136]{3,1,2,0:T(8,128)}, u32[]{:S(2)}, u32[]{:S(2)}) collective-permute-start(f32[3,40,1,136]{3,1,2,0:T(8,128)} %get-tuple-element.25), channel_id=1, source_target_pairs={{1,0},{2,1},{3,2},{4,3},{5,4},{6,5},{7,6},{8,7},{9,8},{10,9},{11,1... | collective-permute-start | bytes 195848 | tf_op jit(solution)/shard_map/ppermute | solution.py:40
  41.7 1.9 collective-permute-start.3
  43.6 1.3 fusion.136
  45.2 0.7 slice.266
  45.9 1.0 copy.32
  47.0 2.5 %collective-permute-done.2 = f32[3,40,1,136]{3,1,2,0:T(8,128)} collective-permute-done((f32[3,40,1,136]{3,1,2,0:T(8,128)}, f32[3,40,1,136]{3,1,2,0:T(8,128)}, u32[]{:S(2)}, u32[]{:S(2)}) %collective-permute-start.2) | collective-permute-done | bytes 65312 | tf_op jit(solution)/shard_map/ppermute | solution.py:40
  49.5 6.7 %collective-permute-done.3 = f32[3,40,1,136]{3,1,2,0:T(8,128)} collective-permute-done((f32[3,40,1,136]{3,1,2,0:T(8,128)}, f32[3,40,1,136]{3,1,2,0:T(8,128)}, u32[]{:S(2)}, u32[]{:S(2)}) %collective-permute-start.3) | collective-permute-done | bytes 65312 | tf_op jit(solution)/shard_map/ppermute | solution.py:39
  56.2 2.7 %slice_subtract_fusion = f32[3,40,8,136]{3,1,2,0:T(8,128)S(1)} fusion(f32[9,40,8,136]{3,1,2,0:T(8,128)S(1)} %pad_maximum_fusion, f32[3,40,8,1]{3,1,2,0:T(8,128)S(1)} %copy.31, f32[3,40,8,135]{3,1,2,0:T(8,128)} %get-tuple-element.29, f32[3,40,8,135]{3,1,2,0:T(8,128)} %get-tuple-element.28, f32[3,40,8,1]{3,1,2,0:T(8,128)} %copy.32, ...), kind=kLoop, calls=%fused_computation.78 | loop fusion | flops 1175040 | bytes 3133452 | tf_op jit(solution)/shard_map/sub | solution.py:71
  59.6 5.1 %collective-permute-start.4 = (f32[3,40,1,136]{3,1,2,0:T(8,128)S(1)}, f32[3,40,1,136]{3,1,2,0:T(8,128)S(1)}, u32[]{:S(2)}, u32[]{:S(2)}) collective-permute-start(f32[3,40,1,136]{3,1,2,0:T(8,128)S(1)} %get-tuple-element.62), channel_id=1, source_target_pairs={{1,0},{2,1},{3,2},{4,3},{5,4},{6,5},{7,6},{8,7},{9,8},{10,9},{11,1... | collective-permute-start | bytes 195848 | tf_op jit(solution)/shard_map/ppermute | solution.py:40
  64.7 4.0 %collective-permute-start.5 = (f32[3,40,1,136]{3,1,2,0:T(8,128)S(1)}, f32[3,40,1,136]{3,1,2,0:T(8,128)S(1)}, u32[]{:S(2)}, u32[]{:S(2)}) collective-permute-start(f32[3,40,1,136]{3,1,2,0:T(8,128)S(1)} %get-tuple-element.61), channel_id=1, source_target_pairs={{0,1},{1,2},{2,3},{3,4},{4,5},{5,6},{6,7},{7,8},{8,9},{9,10},{10,1... | collective-permute-start | bytes 195848 | tf_op jit(solution)/shard_map/ppermute | solution.py:39
  69.1 10.1 %collective-permute-done.5 = f32[3,40,1,136]{3,1,2,0:T(8,128)S(1)} collective-permute-done((f32[3,40,1,136]{3,1,2,0:T(8,128)S(1)}, f32[3,40,1,136]{3,1,2,0:T(8,128)S(1)}, u32[]{:S(2)}, u32[]{:S(2)}) %collective-permute-start.5) | collective-permute-done | bytes 65312 | tf_op jit(solution)/shard_map/ppermute | solution.py:39
  79.2 0.7 fusion.63
  80.4 1.9 collective-permute-start.6
  82.3 7.5 %collective-permute-start.7 = (f32[3,40,1,136]{3,1,2,0:T(8,128)S(1)}, f32[3,40,1,136]{3,1,2,0:T(8,128)S(1)}, u32[]{:S(2)}, u32[]{:S(2)}) collective-permute-start(f32[3,40,1,136]{3,1,2,0:T(8,128)S(1)} %get-tuple-element.49), channel_id=1, source_target_pairs={{0,1},{1,2},{2,3},{3,4},{4,5},{5,6},{6,7},{7,8},{8,9},{9,10},{10,1... | collective-permute-start | bytes 195848 | tf_op jit(solution)/shard_map/ppermute | solution.py:39
  90.0 1.1 collective-permute-done.6
  91.1 2.2 %collective-permute-done.7 = f32[3,40,1,136]{3,1,2,0:T(8,128)S(1)} collective-permute-done((f32[3,40,1,136]{3,1,2,0:T(8,128)S(1)}, f32[3,40,1,136]{3,1,2,0:T(8,128)S(1)}, u32[]{:S(2)}, u32[]{:S(2)}) %collective-permute-start.7) | collective-permute-done | bytes 65312 | tf_op jit(solution)/shard_map/ppermute | solution.py:39
  93.3 0.6 fusion.61
  95.0 1.9 collective-permute-start.8
  96.9 7.3 %collective-permute-start.9 = (f32[3,40,1,136]{3,1,2,0:T(8,128)S(1)}, f32[3,40,1,136]{3,1,2,0:T(8,128)S(1)}, u32[]{:S(2)}, u32[]{:S(2)}) collective-permute-start(f32[3,40,1,136]{3,1,2,0:T(8,128)S(1)} %get-tuple-element.42), channel_id=1, source_target_pairs={{0,1},{1,2},{2,3},{3,4},{4,5},{5,6},{6,7},{7,8},{8,9},{9,10},{10,1... | collective-permute-start | bytes 195848 | tf_op jit(solution)/shard_map/ppermute | solution.py:39
  104.2 1.6 collective-permute-done.8
  105.9 1.6 collective-permute-done.9
  107.5 0.6 fusion.67
  108.2 1.9 fusion.37
  110.1 11.0 %collective-permute-start.11 = (f32[512,40]{0,1:T(8,128)S(1)}, f32[512,40]{0,1:T(8,128)S(1)}, u32[]{:S(2)}, u32[]{:S(2)}) collective-permute-start(f32[512,40]{0,1:T(8,128)S(1)} %fusion.37), channel_id=1, source_target_pairs={{0,496},{16,0},{32,16},{48,32},{64,48},{80,64},{96,80},{112,96},{1... | collective-permute-start | bytes 245768 | tf_op jit(solution)/shard_map/ppermute | solution.py:211
  121.1 9.0 %collective-permute-start.10 = (f32[512,40]{0,1:T(8,128)S(1)}, f32[512,40]{0,1:T(8,128)S(1)}, u32[]{:S(2)}, u32[]{:S(2)}) collective-permute-start(f32[512,40]{0,1:T(8,128)S(1)} %fusion.37), channel_id=1, source_target_pairs={{0,16},{16,32},{32,48},{48,64},{64,80},{80,96},{96,112},{112,128},... | collective-permute-start | bytes 245768 | tf_op jit(solution)/shard_map/ppermute | solution.py:210
  130.2 9.6 %collective-permute-start.13 = (f32[256,40]{0,1:T(8,128)S(1)}, f32[256,40]{0,1:T(8,128)S(1)}, u32[]{:S(2)}, u32[]{:S(2)}) collective-permute-start(f32[256,40]{0,1:T(8,128)S(1)} %split.5), channel_id=1, source_target_pairs={{0,480},{16,496},{32,0},{48,16},{64,32},{80,48},{96,64},{112,80},{... | collective-permute-start | bytes 122888 | tf_op jit(solution)/shard_map/ppermute | solution.py:216
  139.8 1.9 collective-permute-start.12
  142.1 6.4 %collective-permute-done.12 = f32[256,40]{0,1:T(8,128)S(1)} collective-permute-done((f32[256,40]{0,1:T(8,128)S(1)}, f32[256,40]{0,1:T(8,128)S(1)}, u32[]{:S(2)}, u32[]{:S(2)}) %collective-permute-start.12) | collective-permute-done | bytes 40992 | tf_op jit(solution)/shard_map/ppermute | solution.py:215
  148.6 8.4 %collective-permute-start.15 = (f32[512,40]{0,1:T(8,128)S(1)}, f32[512,40]{0,1:T(8,128)S(1)}, u32[]{:S(2)}, u32[]{:S(2)}) collective-permute-start(f32[512,40]{0,1:T(8,128)S(1)} %pad_maximum_fusion.16), channel_id=1, source_target_pairs={{1,0},{2,1},{3,2},{4,3},{5,4},{6,5},{7,6},{8,7},{9,8},{10,9},{11,1... | collective-permute-start | bytes 245768 | tf_op jit(solution)/shard_map/ppermute | solution.py:222
  157.0 1.9 collective-permute-start.14
  159.0 7.9 %collective-permute-start.17 = (f32[256,40]{0,1:T(8,128)S(1)}, f32[256,40]{0,1:T(8,128)S(1)}, u32[]{:S(2)}, u32[]{:S(2)}) collective-permute-start(f32[256,40]{0,1:T(8,128)S(1)} %get-tuple-element.70), channel_id=1, source_target_pairs={{2,0},{3,1},{4,2},{5,3},{6,4},{7,5},{8,6},{9,7},{10,8},{11,9},{12,... | collective-permute-start | bytes 122888 | tf_op jit(solution)/shard_map/ppermute | solution.py:227
  166.9 6.1 %collective-permute-start.16 = (f32[256,40]{0,1:T(8,128)S(1)}, f32[256,40]{0,1:T(8,128)S(1)}, u32[]{:S(2)}, u32[]{:S(2)}) collective-permute-start(f32[256,40]{0,1:T(8,128)S(1)} %get-tuple-element.70), channel_id=1, source_target_pairs={{0,2},{1,3},{2,4},{3,5},{4,6},{5,7},{6,8},{7,9},{8,10},{9,11},{10,... | collective-permute-start | bytes 122888 | tf_op jit(solution)/shard_map/ppermute | solution.py:226
  173.1 8.2 %collective-permute-done.16 = f32[256,40]{0,1:T(8,128)S(1)} collective-permute-done((f32[256,40]{0,1:T(8,128)S(1)}, f32[256,40]{0,1:T(8,128)S(1)}, u32[]{:S(2)}, u32[]{:S(2)}) %collective-permute-start.16) | collective-permute-done | bytes 40992 | tf_op jit(solution)/shard_map/ppermute | solution.py:226
  181.3 1.4 fusion.68
  182.8 1.5 fusion.152
  185.1 1.4 fusion.71
  186.5 1.5 fusion.36
  188.1 1.4 fusion.69
  189.6 1.5 fusion.154
  191.1 1.4 fusion.73
  192.5 1.5 fusion.35
  194.1 1.7 fusion.70
  195.8 1.5 fusion.155
  197.3 1.4 fusion.75
  198.8 1.5 fusion.34
  200.3 0.9 pad_maximum_fusion.13
  (104 shorter events, 5.9 us)
Async XLA Ops:
  0.0 9.2 %copy-start.12 = (s32[512]{0:T(512)S(1)}, s32[512]{0:T(512)}, u32[]{:S(2)}) copy-start(s32[512]{0:T(512)} %param.15) | copy-start | bytes 6148
  0.0 9.2 %copy-start.15 = (s32[512]{0:T(512)S(1)}, s32[512]{0:T(512)}, u32[]{:S(2)}) copy-start(s32[512]{0:T(512)} %param.14) | copy-start | bytes 6148
  0.0 9.2 %copy-start.16 = (s32[512]{0:T(512)S(1)}, s32[512]{0:T(512)}, u32[]{:S(2)}) copy-start(s32[512]{0:T(512)} %param.13) | copy-start | bytes 6148
  0.0 9.2 %copy-start.17 = (s32[512]{0:T(512)S(1)}, s32[512]{0:T(512)}, u32[]{:S(2)}) copy-start(s32[512]{0:T(512)} %param.12) | copy-start | bytes 6148
  0.0 9.2 %copy-start.18 = (s32[512]{0:T(512)S(1)}, s32[512]{0:T(512)}, u32[]{:S(2)}) copy-start(s32[512]{0:T(512)} %param.11) | copy-start | bytes 6148
  2.4 9.1 %copy-start.13 = (f32[512]{0:T(512)S(1)}, f32[512]{0:T(512)}, u32[]{:S(2)}) copy-start(f32[512]{0:T(512)} %param.17) | copy-start | bytes 6148
  2.4 9.1 %copy-start.14 = (f32[512]{0:T(512)S(1)}, f32[512]{0:T(512)}, u32[]{:S(2)}) copy-start(f32[512]{0:T(512)} %param.16) | copy-start | bytes 6148
  3.0 16.2 %collective-permute-start.1 = (f32[9,40,8,4]{1,2,3,0:T(8,128)S(1)}, f32[9,40,8,4]{1,2,3,0:T(8,128)S(1)}, u32[]{:S(2)}, u32[]{:S(2)}) collective-permute-start(f32[9,40,8,4]{1,2,3,0:T(8,128)S(1)} %copy.52), channel_id=1, source_target_pairs={{0,496},{16,0},{32,16},{48,32},{64,48},{80,64},{96,80},{112,96},{1... | collective-permute-start | bytes 138248 | tf_op jit(solution)/shard_map/ppermute | solution.py:94
  5.6 12.2 %copy-start.5 = (f32[9,40,8,128]{3,2,1,0:T(8,128)S(1)}, f32[9,40,8,128]{3,2,1,0:T(8,128)}, u32[]{:S(2)}) copy-start(f32[9,40,8,128]{3,2,1,0:T(8,128)} %param.10) | copy-start | bytes 4423684
  6.1 14.7 %collective-permute-start = (f32[9,40,8,4]{1,2,3,0:T(8,128)S(1)}, f32[9,40,8,4]{1,2,3,0:T(8,128)S(1)}, u32[]{:S(2)}, u32[]{:S(2)}) collective-permute-start(f32[9,40,8,4]{1,2,3,0:T(8,128)S(1)} %copy.51), channel_id=1, source_target_pairs={{0,16},{16,32},{32,48},{48,64},{64,80},{80,96},{96,112},{112,128},... | collective-permute-start | bytes 138248 | tf_op jit(solution)/shard_map/ppermute | solution.py:93
  20.9 0.7 copy-start.6
  23.3 3.6 %copy-start.2 = (f32[9,40,8,128]{3,1,2,0:T(8,128)S(1)}, f32[9,40,8,128]{3,1,2,0:T(8,128)}, u32[]{:S(2)}) copy-start(f32[9,40,8,128]{3,1,2,0:T(8,128)} %copy.29) | copy-start | bytes 4423684
  23.3 3.6 %copy-start.3 = (f32[9,40,8,4]{3,1,2,0:T(8,128)S(1)}, f32[9,40,8,4]{3,1,2,0:T(8,128)}, u32[]{:S(2)}) copy-start(f32[9,40,8,4]{3,1,2,0:T(8,128)} %copy.30) | copy-start | bytes 138244
  23.3 3.6 %copy-start.4 = (f32[9,40,8,4]{3,1,2,0:T(8,128)S(1)}, f32[9,40,8,4]{3,1,2,0:T(8,128)}, u32[]{:S(2)}) copy-start(f32[9,40,8,4]{3,1,2,0:T(8,128)} %copy.28) | copy-start | bytes 138244
  29.4 20.1 %collective-permute-start.2 = (f32[3,40,1,136]{3,1,2,0:T(8,128)}, f32[3,40,1,136]{3,1,2,0:T(8,128)}, u32[]{:S(2)}, u32[]{:S(2)}) collective-permute-start(f32[3,40,1,136]{3,1,2,0:T(8,128)} %get-tuple-element.25), channel_id=1, source_target_pairs={{1,0},{2,1},{3,2},{4,3},{5,4},{6,5},{7,6},{8,7},{9,8},{10,9},{11,1... | collective-permute-start | bytes 195848 | tf_op jit(solution)/shard_map/ppermute | solution.py:40
  41.7 14.4 %collective-permute-start.3 = (f32[3,40,1,136]{3,1,2,0:T(8,128)}, f32[3,40,1,136]{3,1,2,0:T(8,128)}, u32[]{:S(2)}, u32[]{:S(2)}) collective-permute-start(f32[3,40,1,136]{3,1,2,0:T(8,128)} %get-tuple-element.24), channel_id=1, source_target_pairs={{0,1},{1,2},{2,3},{3,4},{4,5},{5,6},{6,7},{7,8},{8,9},{9,10},{10,1... | collective-permute-start | bytes 195848 | tf_op jit(solution)/shard_map/ppermute | solution.py:39
  59.2 20.0 %copy-start.11 = (f32[8]{0:T(128)S(1)}, f32[8]{0:T(128)}, u32[]{:S(2)}) copy-start(f32[8]{0:T(128)} %sine_multiply_fusion) | copy-start | bytes 100
  59.6 9.5 %collective-permute-start.4 = (f32[3,40,1,136]{3,1,2,0:T(8,128)S(1)}, f32[3,40,1,136]{3,1,2,0:T(8,128)S(1)}, u32[]{:S(2)}, u32[]{:S(2)}) collective-permute-start(f32[3,40,1,136]{3,1,2,0:T(8,128)S(1)} %get-tuple-element.62), channel_id=1, source_target_pairs={{1,0},{2,1},{3,2},{4,3},{5,4},{6,5},{7,6},{8,7},{9,8},{10,9},{11,1... | collective-permute-start | bytes 195848 | tf_op jit(solution)/shard_map/ppermute | solution.py:40
  64.7 14.5 %collective-permute-start.5 = (f32[3,40,1,136]{3,1,2,0:T(8,128)S(1)}, f32[3,40,1,136]{3,1,2,0:T(8,128)S(1)}, u32[]{:S(2)}, u32[]{:S(2)}) collective-permute-start(f32[3,40,1,136]{3,1,2,0:T(8,128)S(1)} %get-tuple-element.61), channel_id=1, source_target_pairs={{0,1},{1,2},{2,3},{3,4},{4,5},{5,6},{6,7},{7,8},{8,9},{9,10},{10,1... | collective-permute-start | bytes 195848 | tf_op jit(solution)/shard_map/ppermute | solution.py:39
  80.1 13.2 %copy-start.10 = (f32[3]{0:T(128)S(1)}, f32[3]{0:T(128)}, u32[]{:S(2)}) copy-start(f32[3]{0:T(128)} %constant.109) | copy-start | bytes 40
  80.4 10.7 %collective-permute-start.6 = (f32[3,40,1,136]{3,1,2,0:T(8,128)S(1)}, f32[3,40,1,136]{3,1,2,0:T(8,128)S(1)}, u32[]{:S(2)}, u32[]{:S(2)}) collective-permute-start(f32[3,40,1,136]{3,1,2,0:T(8,128)S(1)} %get-tuple-element.50), channel_id=1, source_target_pairs={{1,0},{2,1},{3,2},{4,3},{5,4},{6,5},{7,6},{8,7},{9,8},{10,9},{11,1... | collective-permute-start | bytes 195848 | tf_op jit(solution)/shard_map/ppermute | solution.py:40
  82.3 10.9 %collective-permute-start.7 = (f32[3,40,1,136]{3,1,2,0:T(8,128)S(1)}, f32[3,40,1,136]{3,1,2,0:T(8,128)S(1)}, u32[]{:S(2)}, u32[]{:S(2)}) collective-permute-start(f32[3,40,1,136]{3,1,2,0:T(8,128)S(1)} %get-tuple-element.49), channel_id=1, source_target_pairs={{0,1},{1,2},{2,3},{3,4},{4,5},{5,6},{6,7},{7,8},{8,9},{9,10},{10,1... | collective-permute-start | bytes 195848 | tf_op jit(solution)/shard_map/ppermute | solution.py:39
  95.0 10.8 %collective-permute-start.8 = (f32[3,40,1,136]{3,1,2,0:T(8,128)S(1)}, f32[3,40,1,136]{3,1,2,0:T(8,128)S(1)}, u32[]{:S(2)}, u32[]{:S(2)}) collective-permute-start(f32[3,40,1,136]{3,1,2,0:T(8,128)S(1)} %get-tuple-element.43), channel_id=1, source_target_pairs={{1,0},{2,1},{3,2},{4,3},{5,4},{6,5},{7,6},{8,7},{9,8},{10,9},{11,1... | collective-permute-start | bytes 195848 | tf_op jit(solution)/shard_map/ppermute | solution.py:40
  96.9 10.5 %collective-permute-start.9 = (f32[3,40,1,136]{3,1,2,0:T(8,128)S(1)}, f32[3,40,1,136]{3,1,2,0:T(8,128)S(1)}, u32[]{:S(2)}, u32[]{:S(2)}) collective-permute-start(f32[3,40,1,136]{3,1,2,0:T(8,128)S(1)} %get-tuple-element.42), channel_id=1, source_target_pairs={{0,1},{1,2},{2,3},{3,4},{4,5},{5,6},{6,7},{7,8},{8,9},{9,10},{10,1... | collective-permute-start | bytes 195848 | tf_op jit(solution)/shard_map/ppermute | solution.py:39
  107.5 0.7 copy-start.9
  108.2 73.1 %copy-start.8 = (f32[256]{0:T(256)S(1)}, f32[256]{0:T(256)}, u32[]{:S(2)}) copy-start(f32[256]{0:T(256)} %get-tuple-element.7) | copy-start | bytes 3076
  108.2 73.1 %copy-start.7 = (f32[256]{0:T(256)S(1)}, f32[256]{0:T(256)}, u32[]{:S(2)}) copy-start(f32[256]{0:T(256)} %get-tuple-element.6) | copy-start | bytes 3076
  110.1 32.0 %collective-permute-start.11 = (f32[512,40]{0,1:T(8,128)S(1)}, f32[512,40]{0,1:T(8,128)S(1)}, u32[]{:S(2)}, u32[]{:S(2)}) collective-permute-start(f32[512,40]{0,1:T(8,128)S(1)} %fusion.37), channel_id=1, source_target_pairs={{0,496},{16,0},{32,16},{48,32},{64,48},{80,64},{96,80},{112,96},{1... | collective-permute-start | bytes 245768 | tf_op jit(solution)/shard_map/ppermute | solution.py:211
  121.1 20.9 %collective-permute-start.10 = (f32[512,40]{0,1:T(8,128)S(1)}, f32[512,40]{0,1:T(8,128)S(1)}, u32[]{:S(2)}, u32[]{:S(2)}) collective-permute-start(f32[512,40]{0,1:T(8,128)S(1)} %fusion.37), channel_id=1, source_target_pairs={{0,16},{16,32},{32,48},{48,64},{64,80},{80,96},{96,112},{112,128},... | collective-permute-start | bytes 245768 | tf_op jit(solution)/shard_map/ppermute | solution.py:210
  130.2 52.6 %copy-start.1 = (f32[256,1024]{0,1:T(8,128)S(1)}, f32[256,1024]{0,1:T(8,128)}, u32[]{:S(2)}) copy-start(f32[256,1024]{0,1:T(8,128)} %get-tuple-element.72) | copy-start | bytes 3145732
  130.2 11.9 %collective-permute-start.13 = (f32[256,40]{0,1:T(8,128)S(1)}, f32[256,40]{0,1:T(8,128)S(1)}, u32[]{:S(2)}, u32[]{:S(2)}) collective-permute-start(f32[256,40]{0,1:T(8,128)S(1)} %split.5), channel_id=1, source_target_pairs={{0,480},{16,496},{32,0},{48,16},{64,32},{80,48},{96,64},{112,80},{... | collective-permute-start | bytes 122888 | tf_op jit(solution)/shard_map/ppermute | solution.py:216
  139.8 8.8 %collective-permute-start.12 = (f32[256,40]{0,1:T(8,128)S(1)}, f32[256,40]{0,1:T(8,128)S(1)}, u32[]{:S(2)}, u32[]{:S(2)}) collective-permute-start(f32[256,40]{0,1:T(8,128)S(1)} %split.5), channel_id=1, source_target_pairs={{0,32},{16,48},{32,64},{48,80},{64,96},{80,112},{96,128},{112,144}... | collective-permute-start | bytes 122888 | tf_op jit(solution)/shard_map/ppermute | solution.py:215
  148.6 24.4 %collective-permute-start.15 = (f32[512,40]{0,1:T(8,128)S(1)}, f32[512,40]{0,1:T(8,128)S(1)}, u32[]{:S(2)}, u32[]{:S(2)}) collective-permute-start(f32[512,40]{0,1:T(8,128)S(1)} %pad_maximum_fusion.16), channel_id=1, source_target_pairs={{1,0},{2,1},{3,2},{4,3},{5,4},{6,5},{7,6},{8,7},{9,8},{10,9},{11,1... | collective-permute-start | bytes 245768 | tf_op jit(solution)/shard_map/ppermute | solution.py:222
  157.0 16.0 %collective-permute-start.14 = (f32[512,40]{0,1:T(8,128)S(1)}, f32[512,40]{0,1:T(8,128)S(1)}, u32[]{:S(2)}, u32[]{:S(2)}) collective-permute-start(f32[512,40]{0,1:T(8,128)S(1)} %pad_maximum_fusion.16), channel_id=1, source_target_pairs={{0,1},{1,2},{2,3},{3,4},{4,5},{5,6},{6,7},{7,8},{8,9},{9,10},{10,1... | collective-permute-start | bytes 245768 | tf_op jit(solution)/shard_map/ppermute | solution.py:221
  159.0 14.1 %collective-permute-start.17 = (f32[256,40]{0,1:T(8,128)S(1)}, f32[256,40]{0,1:T(8,128)S(1)}, u32[]{:S(2)}, u32[]{:S(2)}) collective-permute-start(f32[256,40]{0,1:T(8,128)S(1)} %get-tuple-element.70), channel_id=1, source_target_pairs={{2,0},{3,1},{4,2},{5,3},{6,4},{7,5},{8,6},{9,7},{10,8},{11,9},{12,... | collective-permute-start | bytes 122888 | tf_op jit(solution)/shard_map/ppermute | solution.py:227
  166.9 14.4 %collective-permute-start.16 = (f32[256,40]{0,1:T(8,128)S(1)}, f32[256,40]{0,1:T(8,128)S(1)}, u32[]{:S(2)}, u32[]{:S(2)}) collective-permute-start(f32[256,40]{0,1:T(8,128)S(1)} %get-tuple-element.70), channel_id=1, source_target_pairs={{0,2},{1,3},{2,4},{3,5},{4,6},{5,7},{6,8},{7,9},{8,10},{9,11},{10,... | collective-permute-start | bytes 122888 | tf_op jit(solution)/shard_map/ppermute | solution.py:226
  184.3 2.2 %copy-start = (f32[256,1024]{0,1:T(8,128)S(1)}, f32[256,1024]{0,1:T(8,128)}, u32[]{:S(2)}) copy-start(f32[256,1024]{0,1:T(8,128)} %get-tuple-element.71) | copy-start | bytes 3145732

commit v5 on v4

--- a/solution.py
+++ b/solution.py
@@ -133,6 +133,31 @@
 def tile_origin(state):
     _, _, rows_tile, cols_tile = state.shape
     return lax.axis_index("lon") * cols_tile, lax.axis_index("lat") * rows_tile
+
+
+REACH = BATCHES * (8 - 1)
+
+
+def lat_shift(array, step):
+    size = lax.axis_size("lat")
+    pairs = [(i, i + step) for i in range(size) if 0 <= i + step < size]
+    return lax.ppermute(array, "lat", pairs)
+
+
+def band_table(wide, lon_obs, lat_obs, kind_obs, width):
+    fields_count, _, rows_tile, wide_cols = wide.shape
+    cols_tile = wide_cols - 2 * width
+    grid_lon = cols_tile * lax.axis_size("lon")
+    lon_base = lax.axis_index("lon") * cols_tile
+    lat_base = lax.axis_index("lat") * rows_tile
+    column = (lon_obs - lon_base + width) % grid_lon
+    inside = (column >= width - REACH) & (column < width + cols_tile + REACH)
+    row_hit = jnp.arange(rows_tile, dtype=jnp.int32)[None, :] == (lat_obs - lat_base)[:, None]
+    col_hit = (jnp.arange(wide_cols, dtype=jnp.int32)[None, :] == column[:, None]) & inside[:, None]
+    cell = (row_hit[:, :, None] & col_hit[:, None, :]).astype(jnp.float32)
+    picked = jnp.einsum("jrc,fmrc->jfm", cell, wide, precision=lax.Precision.HIGHEST)
+    field_hit = jnp.arange(fields_count, dtype=jnp.int32)[None, :] == kind_obs[:, None]
+    return jnp.sum(jnp.where(field_hit[:, :, None], picked, 0.0), axis=1)
 
 
 def owner_table(state, lon_obs, lat_obs, kind_obs):
@@ -195,37 +220,18 @@
     batches = [
         (ints[:, b * NB : (b + 1) * NB], floats[:, b * NB : (b + 1) * NB]) for b in range(BATCHES)
     ]
-    width = 2 * STEPS
+    width = 2 * STEPS + REACH
     state = lon_widened(ensemble, width)
     for step_index in range(STEPS):
         state = march_prediction(state, rotation_frequency)
+    band = band_table(state, ints[0], ints[1], ints[2], width)
     state = state[..., width : width + cols_tile]
 
     (lon0, lat0, kind0, radius0), (value0, error0) = batches[0]
     (lon1, lat1, kind1, radius1), (value1, error1) = batches[1]
-    table0, table1 = jnp.split(owner_table(state, ints[0], ints[1], ints[2]), 2)
-    both = jnp.concatenate([table0, table1])
-    both = (
-        both
-        + lax.ppermute(both, "lon", ring_pairs(lon_size, 1))
-        + lax.ppermute(both, "lon", ring_pairs(lon_size, -1))
-    )
-    wide0 = (
-        both[:NB]
-        + lax.ppermute(table0, "lon", ring_pairs(lon_size, 2))
-        + lax.ppermute(table0, "lon", ring_pairs(lon_size, -2))
-    )
-    both = jnp.concatenate([wide0, both[NB:]])
-    both = (
-        both
-        + lax.ppermute(both, "lat", line_pairs(lat_size, 1))
-        + lax.ppermute(both, "lat", line_pairs(lat_size, -1))
-    )
-    priors = (
-        both[:NB]
-        + lax.ppermute(wide0, "lat", line_pairs(lat_size, 2))
-        + lax.ppermute(wide0, "lat", line_pairs(lat_size, -2))
-    )
+    table0 = band[:NB]
+    both = band + lat_shift(band, 1) + lat_shift(band, -1)
+    priors = both[:NB] + lat_shift(table0, 2) + lat_shift(table0, -2)
     raw1 = both[NB:]
     gains, anomaly = statistics(priors, value0, error0, member_count)
     deviation = raw1 - jnp.mean(raw1, axis=1, keepdims=True)

time: 202 us -> 189 us (0.936)
  the two profiles are of different devices: /device:TPU:17 before, /device:TPU:22 now
where the time goes in v5:
time: 189 us; the launch traced here: 188 us
  starting transfers between devices  72.7 us (38%)
  waiting for transfers between devices  51.5 us (27%)
  local copies, waits for them, and re-layouts  26 us (14%)
  matrix products  21.2 us (11%)
  other arithmetic  16.1 us (9%)
    ppermute x4, waiting for transfers between devices, lat_edges(): before = lax.ppermute(array[:, :, -1:, :], 'lat', up)  30 us
    ppermute x4, starting transfers between devices, lat_edges(): after = lax.ppermute(array[:, :, :1, :], 'lat', down)  24.9 us
    ppermute x4, starting transfers between devices, lat_shift(): return lax.ppermute(array, 'lat', pairs)  24.4 us
    ppermute x4, starting transfers between devices, lat_edges(): before = lax.ppermute(array[:, :, -1:, :], 'lat', up)  19 us
    ppermute x4, waiting for transfers between devices, lat_edges(): after = lax.ppermute(array[:, :, :1, :], 'lat', down)  11.9 us
    ppermute x4, waiting for transfers between devices, lat_shift(): return lax.ppermute(array, 'lat', pairs)  9.6 us
    dot_general x6, matrix products, update_group(): jnp.einsum('om,foc->fmc', gains, covariance * weights[None], precision=la...  9.1 us
    dot_general x6, matrix products, update_group(): jnp.einsum('om,fmc->foc', anomaly, deviation, precision=lax.Precision.HIGH)  8.84 us
  transfers between devices with their start and end apart: 14, of which 10 were waited for; matrix products, arithmetic and copies ran while one was open for 10% of the time, Pallas kernels for 0%

profile of v5, /device:TPU:22, one launch (start us, length us, event | category | flops | bytes accessed | tf_op | source)
XLA Modules:
  0.0 188.4 jit_solution(13723245142655300673)
XLA Ops:
  0.0 3.6 %fusion.150 = (f32[9,40,8,18]{3,2,1,0:T(8,128)S(1)}, f32[9,40,8,18]{3,2,1,0:T(8,128)}) fusion(f32[9,40,8,128]{3,2,1,0:T(8,128)} %param.10), kind=kLoop, calls=%fused_computation.248 | loop fusion | bytes 829440 | tf_op jit(solution)/shard_map/slice | solution.py:93
  3.6 2.9 %copy.52 = f32[9,40,8,18]{1,2,3,0:T(8,128)} copy(f32[9,40,8,18]{3,2,1,0:T(8,128)} %get-tuple-element.33) | data formatting | bytes 414720
  6.5 2.2 %collective-permute-start.1 = (f32[9,40,8,18]{1,2,3,0:T(8,128)}, f32[9,40,8,18]{1,2,3,0:T(8,128)}, u32[]{:S(2)}, u32[]{:S(2)}) collective-permute-start(f32[9,40,8,18]{1,2,3,0:T(8,128)} %copy.52), channel_id=1, source_target_pairs={{0,496},{16,0},{32,16},{48,32},{64,48},{80,64},{96,80},{112,96},{1... | collective-permute-start | bytes 622088 | tf_op jit(solution)/shard_map/ppermute | solution.py:94
  8.7 1.4 copy.51
  10.1 2.1 %collective-permute-start = (f32[9,40,8,18]{1,2,3,0:T(8,128)}, f32[9,40,8,18]{1,2,3,0:T(8,128)S(1)}, u32[]{:S(2)}, u32[]{:S(2)}) collective-permute-start(f32[9,40,8,18]{1,2,3,0:T(8,128)} %copy.51), channel_id=1, source_target_pairs={{0,16},{16,32},{32,48},{48,64},{64,80},{80,96},{96,112},{112,128},... | collective-permute-start | bytes 622088 | tf_op jit(solution)/shard_map/ppermute | solution.py:93
  12.3 1.4 copy.29
  13.9 1.0 gather_fusion
  15.5 0.6 sine_multiply_fusion
  16.2 0.4 slice_reduce_fusion.3
  16.8 1.0 gather_fusion.1
  17.8 0.9 slice_reduce_fusion.5
  18.8 2.9 %multiply_multiply_fusion = (f32[256,1024]{0,1:T(8,128)}, f32[256,1024]{0,1:T(8,128)}) fusion(f32[256]{0:T(256)S(1)} %get-tuple-element.9, s32[256]{0:T(256)S(1)} %get-tuple-element.12, s32[256]{0:T(256)S(1)} %get-tuple-element.11, s32[1024]{0:T(1024)S(1)} %get-tuple-element.92, s32[1024]{0:T(1024)S(1)} %get-tuple-element.93, f32[256]{0:T(256)S(1)} %get-tuple-element.10, ...), kind=kLoop, calls=%fused_computation.76 | loop fusion | flops 12582912 | bytes 2111488 | tf_op jit(solution)/shard_map/mul | solution.py:188
  21.7 0.6 iota_compare_fusion.2
  22.3 2.8 %copy.30 = f32[9,40,8,18]{3,1,2,0:T(8,128)} copy(f32[9,40,8,18]{1,2,3,0:T(8,128)} %collective-permute-done.1) | data formatting | bytes 414720 | tf_op jit(solution)/shard_map/ppermute | solution.py:94
  25.1 0.8 copy-done.6
  25.9 1.7 copy.28
  27.7 3.6 %pad_maximum_fusion = f32[9,40,8,164]{3,1,2,0:T(8,128)S(1)} fusion(f32[9,40,8,18]{3,1,2,0:T(8,128)} %copy.30, f32[9,40,8,128]{3,1,2,0:T(8,128)} %copy.29, f32[9,40,8,18]{3,1,2,0:T(8,128)} %copy.28), kind=kLoop, calls=%fused_computation.14 | loop fusion | flops 944640 | bytes 3778560 | tf_op jit(solution)/shard_map/concatenate | solution.py:95
  31.3 0.9 pad_maximum_fusion.4
  32.2 1.6 fusion.149
  33.8 12.6 %collective-permute-start.2 = (f32[3,40,1,164]{3,1,2,0:T(8,128)}, f32[3,40,1,164]{3,1,2,0:T(8,128)}, u32[]{:S(2)}, u32[]{:S(2)}) collective-permute-start(f32[3,40,1,164]{3,1,2,0:T(8,128)} %get-tuple-element.27), channel_id=1, source_target_pairs={{1,0},{2,1},{3,2},{4,3},{5,4},{6,5},{7,6},{8,7},{9,8},{10,9},{11,1... | collective-permute-start | bytes 236168 | tf_op jit(solution)/shard_map/ppermute | solution.py:40
  46.4 1.9 %collective-permute-start.3 = (f32[3,40,1,164]{3,1,2,0:T(8,128)}, f32[3,40,1,164]{3,1,2,0:T(8,128)}, u32[]{:S(2)}, u32[]{:S(2)}) collective-permute-start(f32[3,40,1,164]{3,1,2,0:T(8,128)} %get-tuple-element.26), channel_id=1, source_target_pairs={{0,1},{1,2},{2,3},{3,4},{4,5},{5,6},{6,7},{7,8},{8,9},{9,10},{10,1... | collective-permute-start | bytes 236168 | tf_op jit(solution)/shard_map/ppermute | solution.py:39
  48.3 1.3 fusion.148
  49.6 0.7 slice.257
  50.6 0.7 slice.258
  51.3 1.0 copy.32
  52.3 1.1 collective-permute-done.2
  53.4 8.5 %collective-permute-done.3 = f32[3,40,1,164]{3,1,2,0:T(8,128)} collective-permute-done((f32[3,40,1,164]{3,1,2,0:T(8,128)}, f32[3,40,1,164]{3,1,2,0:T(8,128)}, u32[]{:S(2)}, u32[]{:S(2)}) %collective-permute-start.3) | collective-permute-done | bytes 78752 | tf_op jit(solution)/shard_map/ppermute | solution.py:39
  61.9 2.7 %slice_subtract_fusion = f32[3,40,8,164]{3,1,2,0:T(8,128)S(1)} fusion(f32[9,40,8,164]{3,1,2,0:T(8,128)S(1)} %pad_maximum_fusion, f32[3,40,8,1]{3,1,2,0:T(8,128)S(1)} %copy.31, f32[3,40,8,163]{3,1,2,0:T(8,128)} %get-tuple-element.31, f32[3,40,8,163]{3,1,2,0:T(8,128)} %get-tuple-element.30, f32[3,40,8,1]{3,1,2,0:T(8,128)} %copy.32, ...), kind=kLoop, calls=%fused_computation.80 | loop fusion | flops 1416960 | bytes 3778572 | tf_op jit(solution)/shard_map/sub | solution.py:71
  65.3 5.0 %collective-permute-start.4 = (f32[3,40,1,164]{3,1,2,0:T(8,128)S(1)}, f32[3,40,1,164]{3,1,2,0:T(8,128)S(1)}, u32[]{:S(2)}, u32[]{:S(2)}) collective-permute-start(f32[3,40,1,164]{3,1,2,0:T(8,128)S(1)} %get-tuple-element.64), channel_id=1, source_target_pairs={{1,0},{2,1},{3,2},{4,3},{5,4},{6,5},{7,6},{8,7},{9,8},{10,9},{11,1... | collective-permute-start | bytes 236168 | tf_op jit(solution)/shard_map/ppermute | solution.py:40
  70.3 4.8 %collective-permute-start.5 = (f32[3,40,1,164]{3,1,2,0:T(8,128)S(1)}, f32[3,40,1,164]{3,1,2,0:T(8,128)S(1)}, u32[]{:S(2)}, u32[]{:S(2)}) collective-permute-start(f32[3,40,1,164]{3,1,2,0:T(8,128)S(1)} %get-tuple-element.63), channel_id=1, source_target_pairs={{0,1},{1,2},{2,3},{3,4},{4,5},{5,6},{6,7},{7,8},{8,9},{9,10},{10,1... | collective-permute-start | bytes 236168 | tf_op jit(solution)/shard_map/ppermute | solution.py:39
  75.3 1.5 collective-permute-done.4
  76.8 14.0 %collective-permute-done.5 = f32[3,40,1,164]{3,1,2,0:T(8,128)S(1)} collective-permute-done((f32[3,40,1,164]{3,1,2,0:T(8,128)S(1)}, f32[3,40,1,164]{3,1,2,0:T(8,128)S(1)}, u32[]{:S(2)}, u32[]{:S(2)}) %collective-permute-start.5) | collective-permute-done | bytes 78752 | tf_op jit(solution)/shard_map/ppermute | solution.py:39
  90.7 0.7 fusion.73
  91.9 1.9 %collective-permute-start.6 = (f32[3,40,1,164]{3,1,2,0:T(8,128)S(1)}, f32[3,40,1,164]{3,1,2,0:T(8,128)S(1)}, u32[]{:S(2)}, u32[]{:S(2)}) collective-permute-start(f32[3,40,1,164]{3,1,2,0:T(8,128)S(1)} %get-tuple-element.52), channel_id=1, source_target_pairs={{1,0},{2,1},{3,2},{4,3},{5,4},{6,5},{7,6},{8,7},{9,8},{10,9},{11,1... | collective-permute-start | bytes 236168 | tf_op jit(solution)/shard_map/ppermute | solution.py:40
  93.8 8.0 %collective-permute-start.7 = (f32[3,40,1,164]{3,1,2,0:T(8,128)S(1)}, f32[3,40,1,164]{3,1,2,0:T(8,128)S(1)}, u32[]{:S(2)}, u32[]{:S(2)}) collective-permute-start(f32[3,40,1,164]{3,1,2,0:T(8,128)S(1)} %get-tuple-element.51), channel_id=1, source_target_pairs={{0,1},{1,2},{2,3},{3,4},{4,5},{5,6},{6,7},{7,8},{8,9},{9,10},{10,1... | collective-permute-start | bytes 236168 | tf_op jit(solution)/shard_map/ppermute | solution.py:39
  102.0 5.4 %collective-permute-done.6 = f32[3,40,1,164]{3,1,2,0:T(8,128)S(1)} collective-permute-done((f32[3,40,1,164]{3,1,2,0:T(8,128)S(1)}, f32[3,40,1,164]{3,1,2,0:T(8,128)S(1)}, u32[]{:S(2)}, u32[]{:S(2)}) %collective-permute-start.6) | collective-permute-done | bytes 78752 | tf_op jit(solution)/shard_map/ppermute | solution.py:40
  107.4 2.0 %collective-permute-done.7 = f32[3,40,1,164]{3,1,2,0:T(8,128)S(1)} collective-permute-done((f32[3,40,1,164]{3,1,2,0:T(8,128)S(1)}, f32[3,40,1,164]{3,1,2,0:T(8,128)S(1)}, u32[]{:S(2)}, u32[]{:S(2)}) %collective-permute-start.7) | collective-permute-done | bytes 78752 | tf_op jit(solution)/shard_map/ppermute | solution.py:39
  109.5 0.6 fusion.71
  111.3 5.4 %collective-permute-start.8 = (f32[3,40,1,164]{3,1,2,0:T(8,128)S(1)}, f32[3,40,1,164]{3,1,2,0:T(8,128)S(1)}, u32[]{:S(2)}, u32[]{:S(2)}) collective-permute-start(f32[3,40,1,164]{3,1,2,0:T(8,128)S(1)} %get-tuple-element.45), channel_id=1, source_target_pairs={{1,0},{2,1},{3,2},{4,3},{5,4},{6,5},{7,6},{8,7},{9,8},{10,9},{11,1... | collective-permute-start | bytes 236168 | tf_op jit(solution)/shard_map/ppermute | solution.py:40
  116.7 4.3 %collective-permute-start.9 = (f32[3,40,1,164]{3,1,2,0:T(8,128)S(1)}, f32[3,40,1,164]{3,1,2,0:T(8,128)S(1)}, u32[]{:S(2)}, u32[]{:S(2)}) collective-permute-start(f32[3,40,1,164]{3,1,2,0:T(8,128)S(1)} %get-tuple-element.44), channel_id=1, source_target_pairs={{0,1},{1,2},{2,3},{3,4},{4,5},{5,6},{6,7},{7,8},{8,9},{9,10},{10,1... | collective-permute-start | bytes 236168 | tf_op jit(solution)/shard_map/ppermute | solution.py:39
  121.1 3.9 %collective-permute-done.8 = f32[3,40,1,164]{3,1,2,0:T(8,128)S(1)} collective-permute-done((f32[3,40,1,164]{3,1,2,0:T(8,128)S(1)}, f32[3,40,1,164]{3,1,2,0:T(8,128)S(1)}, u32[]{:S(2)}, u32[]{:S(2)}) %collective-permute-start.8) | collective-permute-done | bytes 78752 | tf_op jit(solution)/shard_map/ppermute | solution.py:40
  125.0 5.5 %collective-permute-done.9 = f32[3,40,1,164]{3,1,2,0:T(8,128)S(1)} collective-permute-done((f32[3,40,1,164]{3,1,2,0:T(8,128)S(1)}, f32[3,40,1,164]{3,1,2,0:T(8,128)S(1)}, u32[]{:S(2)}, u32[]{:S(2)}) %collective-permute-start.9) | collective-permute-done | bytes 78752 | tf_op jit(solution)/shard_map/ppermute | solution.py:39
  130.5 0.6 fusion.77
  131.2 2.5 %fusion.47 = f32[512,40]{0,1:T(8,128)S(1)} fusion(f32[3,40,8,164]{3,1,2,0:T(8,128)S(1)} %get-tuple-element.22, f32[3,40,8,164]{3,1,2,0:T(8,128)S(1)} %get-tuple-element.23, f32[3,40,8,164]{3,1,2,0:T(8,128)S(1)} %fusion.71, pred[512,164]{0,1:T(8,128)(4,1)S(1)} %fusion.90, pred[512,8]{0,1:T(8,128)(4,1)S(1)} %copy-done.17, ...), kind=kOutput, calls=%fused_computation.60 | convolution fusion | flops 2903898624 | bytes 2063872 | tf_op jit(solution)/shard_map/jrc,fmrc->jfm/dot_general | solution.py:158
  133.8 5.7 %collective-permute-start.13 = (f32[256,40]{0,1:T(8,128)S(1)}, f32[256,40]{0,1:T(8,128)S(1)}, u32[]{:S(2)}, u32[]{:S(2)}) collective-permute-start(f32[256,40]{0,1:T(8,128)S(1)} %slice.299), channel_id=1, source_target_pairs={{2,0},{3,1},{4,2},{5,3},{6,4},{7,5},{8,6},{9,7},{10,8},{11,9},{12,... | collective-permute-start | bytes 122888 | tf_op jit(solution)/shard_map/ppermute | solution.py:144
  139.5 9.0 %collective-permute-start.12 = (f32[256,40]{0,1:T(8,128)S(1)}, f32[256,40]{0,1:T(8,128)S(1)}, u32[]{:S(2)}, u32[]{:S(2)}) collective-permute-start(f32[256,40]{0,1:T(8,128)S(1)} %slice.299), channel_id=1, source_target_pairs={{0,2},{1,3},{2,4},{3,5},{4,6},{5,7},{6,8},{7,9},{8,10},{9,11},{10,... | collective-permute-start | bytes 122888 | tf_op jit(solution)/shard_map/ppermute | solution.py:144
  148.5 7.6 %collective-permute-start.11 = (f32[512,40]{0,1:T(8,128)S(1)}, f32[512,40]{0,1:T(8,128)S(1)}, u32[]{:S(2)}, u32[]{:S(2)}) collective-permute-start(f32[512,40]{0,1:T(8,128)S(1)} %fusion.47), channel_id=1, source_target_pairs={{1,0},{2,1},{3,2},{4,3},{5,4},{6,5},{7,6},{8,7},{9,8},{10,9},{11,1... | collective-permute-start | bytes 245768 | tf_op jit(solution)/shard_map/ppermute | solution.py:144
  156.1 2.1 %collective-permute-start.10 = (f32[512,40]{0,1:T(8,128)S(1)}, f32[512,40]{0,1:T(8,128)S(1)}, u32[]{:S(2)}, u32[]{:S(2)}) collective-permute-start(f32[512,40]{0,1:T(8,128)S(1)} %fusion.47), channel_id=1, source_target_pairs={{0,1},{1,2},{2,3},{3,4},{4,5},{5,6},{6,7},{7,8},{8,9},{9,10},{10,1... | collective-permute-start | bytes 245768 | tf_op jit(solution)/shard_map/ppermute | solution.py:144
  158.6 2.0 %collective-permute-done.11 = f32[512,40]{0,1:T(8,128)S(1)} collective-permute-done((f32[512,40]{0,1:T(8,128)S(1)}, f32[512,40]{0,1:T(8,128)S(1)}, u32[]{:S(2)}, u32[]{:S(2)}) %collective-permute-start.11) | collective-permute-done | bytes 81952 | tf_op jit(solution)/shard_map/ppermute | solution.py:144
  160.7 7.6 %collective-permute-done.10 = f32[512,40]{0,1:T(8,128)S(1)} collective-permute-done((f32[512,40]{0,1:T(8,128)S(1)}, f32[512,40]{0,1:T(8,128)S(1)}, u32[]{:S(2)}, u32[]{:S(2)}) %collective-permute-start.10) | collective-permute-done | bytes 81952 | tf_op jit(solution)/shard_map/ppermute | solution.py:144
  168.4 1.4 fusion.78
  169.9 1.5 fusion.163
  171.5 0.5 fusion.52
  172.2 1.4 fusion.81
  173.7 1.5 fusion.46
  175.2 1.4 fusion.79
  176.7 1.5 fusion.165
  178.2 1.4 fusion.83
  179.7 1.5 fusion.45
  181.2 1.7 fusion.80
  182.9 1.5 fusion.166
  184.4 1.4 fusion.85
  185.9 1.5 fusion.44
  187.5 0.9 pad_maximum_fusion.3
  (110 shorter events, 4.8 us)
Async XLA Ops:
  3.6 8.7 %copy-start.5 = (f32[9,40,8,128]{3,2,1,0:T(8,128)S(1)}, f32[9,40,8,128]{3,2,1,0:T(8,128)}, u32[]{:S(2)}) copy-start(f32[9,40,8,128]{3,2,1,0:T(8,128)} %param.10) | copy-start | bytes 4423684
  3.6 10.1 %copy-start.20 = (s32[512]{0:T(512)S(1)}, s32[512]{0:T(512)}, u32[]{:S(2)}) copy-start(s32[512]{0:T(512)} %param.15) | copy-start | bytes 6148
  3.6 10.1 %copy-start.23 = (s32[512]{0:T(512)S(1)}, s32[512]{0:T(512)}, u32[]{:S(2)}) copy-start(s32[512]{0:T(512)} %param.14) | copy-start | bytes 6148
  3.6 10.1 %copy-start.24 = (s32[512]{0:T(512)S(1)}, s32[512]{0:T(512)}, u32[]{:S(2)}) copy-start(s32[512]{0:T(512)} %param.13) | copy-start | bytes 6148
  3.6 10.1 %copy-start.25 = (s32[512]{0:T(512)S(1)}, s32[512]{0:T(512)}, u32[]{:S(2)}) copy-start(s32[512]{0:T(512)} %param.12) | copy-start | bytes 6148
  3.6 10.1 %copy-start.26 = (s32[512]{0:T(512)S(1)}, s32[512]{0:T(512)}, u32[]{:S(2)}) copy-start(s32[512]{0:T(512)} %param.11) | copy-start | bytes 6148
  6.5 15.8 %collective-permute-start.1 = (f32[9,40,8,18]{1,2,3,0:T(8,128)}, f32[9,40,8,18]{1,2,3,0:T(8,128)}, u32[]{:S(2)}, u32[]{:S(2)}) collective-permute-start(f32[9,40,8,18]{1,2,3,0:T(8,128)} %copy.52), channel_id=1, source_target_pairs={{0,496},{16,0},{32,16},{48,32},{64,48},{80,64},{96,80},{112,96},{1... | collective-permute-start | bytes 622088 | tf_op jit(solution)/shard_map/ppermute | solution.py:94
  8.7 8.0 %copy-start.21 = (f32[512]{0:T(512)S(1)}, f32[512]{0:T(512)}, u32[]{:S(2)}) copy-start(f32[512]{0:T(512)} %param.17) | copy-start | bytes 6148
  8.7 8.0 %copy-start.22 = (f32[512]{0:T(512)S(1)}, f32[512]{0:T(512)}, u32[]{:S(2)}) copy-start(f32[512]{0:T(512)} %param.16) | copy-start | bytes 6148
  10.1 15.0 %collective-permute-start = (f32[9,40,8,18]{1,2,3,0:T(8,128)}, f32[9,40,8,18]{1,2,3,0:T(8,128)S(1)}, u32[]{:S(2)}, u32[]{:S(2)}) collective-permute-start(f32[9,40,8,18]{1,2,3,0:T(8,128)} %copy.51), channel_id=1, source_target_pairs={{0,16},{16,32},{32,48},{48,64},{64,80},{80,96},{96,112},{112,128},... | collective-permute-start | bytes 622088 | tf_op jit(solution)/shard_map/ppermute | solution.py:93
  15.5 12.1 %copy-start.7 = (s32[256]{0:T(256)}, s32[256]{0:T(256)S(1)}, u32[]{:S(2)}) copy-start(s32[256]{0:T(256)S(1)} %get-tuple-element.12) | copy-start | bytes 3076
  15.5 12.1 %copy-start.9 = (s32[256]{0:T(256)}, s32[256]{0:T(256)S(1)}, u32[]{:S(2)}) copy-start(s32[256]{0:T(256)S(1)} %get-tuple-element.13) | copy-start | bytes 3076
  15.5 12.1 %copy-start.11 = (s32[256]{0:T(256)}, s32[256]{0:T(256)S(1)}, u32[]{:S(2)}) copy-start(s32[256]{0:T(256)S(1)} %get-tuple-element.14) | copy-start | bytes 3076
  25.1 0.8 copy-start.6
  27.6 3.6 %copy-start.2 = (f32[9,40,8,128]{3,1,2,0:T(8,128)S(1)}, f32[9,40,8,128]{3,1,2,0:T(8,128)}, u32[]{:S(2)}) copy-start(f32[9,40,8,128]{3,1,2,0:T(8,128)} %copy.29) | copy-start | bytes 4423684
  27.6 3.7 %copy-start.3 = (f32[9,40,8,18]{3,1,2,0:T(8,128)S(1)}, f32[9,40,8,18]{3,1,2,0:T(8,128)}, u32[]{:S(2)}) copy-start(f32[9,40,8,18]{3,1,2,0:T(8,128)} %copy.30) | copy-start | bytes 622084
  27.7 3.7 %copy-start.4 = (f32[9,40,8,18]{3,1,2,0:T(8,128)S(1)}, f32[9,40,8,18]{3,1,2,0:T(8,128)}, u32[]{:S(2)}) copy-start(f32[9,40,8,18]{3,1,2,0:T(8,128)} %copy.28) | copy-start | bytes 622084
  33.8 19.6 %collective-permute-start.2 = (f32[3,40,1,164]{3,1,2,0:T(8,128)}, f32[3,40,1,164]{3,1,2,0:T(8,128)}, u32[]{:S(2)}, u32[]{:S(2)}) collective-permute-start(f32[3,40,1,164]{3,1,2,0:T(8,128)} %get-tuple-element.27), channel_id=1, source_target_pairs={{1,0},{2,1},{3,2},{4,3},{5,4},{6,5},{7,6},{8,7},{9,8},{10,9},{11,1... | collective-permute-start | bytes 236168 | tf_op jit(solution)/shard_map/ppermute | solution.py:40
  46.4 15.5 %collective-permute-start.3 = (f32[3,40,1,164]{3,1,2,0:T(8,128)}, f32[3,40,1,164]{3,1,2,0:T(8,128)}, u32[]{:S(2)}, u32[]{:S(2)}) collective-permute-start(f32[3,40,1,164]{3,1,2,0:T(8,128)} %get-tuple-element.26), channel_id=1, source_target_pairs={{0,1},{1,2},{2,3},{3,4},{4,5},{5,6},{6,7},{7,8},{8,9},{9,10},{10,1... | collective-permute-start | bytes 236168 | tf_op jit(solution)/shard_map/ppermute | solution.py:39
  65.0 25.7 %copy-start.18 = (f32[8]{0:T(128)S(1)}, f32[8]{0:T(128)}, u32[]{:S(2)}) copy-start(f32[8]{0:T(128)} %sine_multiply_fusion) | copy-start | bytes 100
  65.3 11.4 %collective-permute-start.4 = (f32[3,40,1,164]{3,1,2,0:T(8,128)S(1)}, f32[3,40,1,164]{3,1,2,0:T(8,128)S(1)}, u32[]{:S(2)}, u32[]{:S(2)}) collective-permute-start(f32[3,40,1,164]{3,1,2,0:T(8,128)S(1)} %get-tuple-element.64), channel_id=1, source_target_pairs={{1,0},{2,1},{3,2},{4,3},{5,4},{6,5},{7,6},{8,7},{9,8},{10,9},{11,1... | collective-permute-start | bytes 236168 | tf_op jit(solution)/shard_map/ppermute | solution.py:40
  70.3 20.4 %collective-permute-start.5 = (f32[3,40,1,164]{3,1,2,0:T(8,128)S(1)}, f32[3,40,1,164]{3,1,2,0:T(8,128)S(1)}, u32[]{:S(2)}, u32[]{:S(2)}) collective-permute-start(f32[3,40,1,164]{3,1,2,0:T(8,128)S(1)} %get-tuple-element.63), channel_id=1, source_target_pairs={{0,1},{1,2},{2,3},{3,4},{4,5},{5,6},{6,7},{7,8},{8,9},{9,10},{10,1... | collective-permute-start | bytes 236168 | tf_op jit(solution)/shard_map/ppermute | solution.py:39
  91.5 18.0 %copy-start.19 = (f32[3]{0:T(128)S(1)}, f32[3]{0:T(128)}, u32[]{:S(2)}) copy-start(f32[3]{0:T(128)} %constant.123) | copy-start | bytes 40
  91.9 15.6 %collective-permute-start.6 = (f32[3,40,1,164]{3,1,2,0:T(8,128)S(1)}, f32[3,40,1,164]{3,1,2,0:T(8,128)S(1)}, u32[]{:S(2)}, u32[]{:S(2)}) collective-permute-start(f32[3,40,1,164]{3,1,2,0:T(8,128)S(1)} %get-tuple-element.52), channel_id=1, source_target_pairs={{1,0},{2,1},{3,2},{4,3},{5,4},{6,5},{7,6},{8,7},{9,8},{10,9},{11,1... | collective-permute-start | bytes 236168 | tf_op jit(solution)/shard_map/ppermute | solution.py:40
  93.8 15.7 %collective-permute-start.7 = (f32[3,40,1,164]{3,1,2,0:T(8,128)S(1)}, f32[3,40,1,164]{3,1,2,0:T(8,128)S(1)}, u32[]{:S(2)}, u32[]{:S(2)}) collective-permute-start(f32[3,40,1,164]{3,1,2,0:T(8,128)S(1)} %get-tuple-element.51), channel_id=1, source_target_pairs={{0,1},{1,2},{2,3},{3,4},{4,5},{5,6},{6,7},{7,8},{8,9},{9,10},{10,1... | collective-permute-start | bytes 236168 | tf_op jit(solution)/shard_map/ppermute | solution.py:39
  111.3 13.7 %collective-permute-start.8 = (f32[3,40,1,164]{3,1,2,0:T(8,128)S(1)}, f32[3,40,1,164]{3,1,2,0:T(8,128)S(1)}, u32[]{:S(2)}, u32[]{:S(2)}) collective-permute-start(f32[3,40,1,164]{3,1,2,0:T(8,128)S(1)} %get-tuple-element.45), channel_id=1, source_target_pairs={{1,0},{2,1},{3,2},{4,3},{5,4},{6,5},{7,6},{8,7},{9,8},{10,9},{11,1... | collective-permute-start | bytes 236168 | tf_op jit(solution)/shard_map/ppermute | solution.py:40
  116.7 13.8 %collective-permute-start.9 = (f32[3,40,1,164]{3,1,2,0:T(8,128)S(1)}, f32[3,40,1,164]{3,1,2,0:T(8,128)S(1)}, u32[]{:S(2)}, u32[]{:S(2)}) collective-permute-start(f32[3,40,1,164]{3,1,2,0:T(8,128)S(1)} %get-tuple-element.44), channel_id=1, source_target_pairs={{0,1},{1,2},{2,3},{3,4},{4,5},{5,6},{6,7},{7,8},{8,9},{9,10},{10,1... | collective-permute-start | bytes 236168 | tf_op jit(solution)/shard_map/ppermute | solution.py:39
  130.5 0.7 copy-start.17
  131.2 37.1 %copy-start.16 = (f32[256]{0:T(256)S(1)}, f32[256]{0:T(256)}, u32[]{:S(2)}) copy-start(f32[256]{0:T(256)} %get-tuple-element.7) | copy-start | bytes 3076
  131.2 37.2 %copy-start.15 = (f32[256]{0:T(256)S(1)}, f32[256]{0:T(256)}, u32[]{:S(2)}) copy-start(f32[256]{0:T(256)} %get-tuple-element.6) | copy-start | bytes 3076
  133.8 36.1 %copy-start.1 = (f32[256,1024]{0,1:T(8,128)S(1)}, f32[256,1024]{0,1:T(8,128)}, u32[]{:S(2)}) copy-start(f32[256,1024]{0,1:T(8,128)} %get-tuple-element.72) | copy-start | bytes 3145732
  133.8 34.5 %collective-permute-start.13 = (f32[256,40]{0,1:T(8,128)S(1)}, f32[256,40]{0,1:T(8,128)S(1)}, u32[]{:S(2)}, u32[]{:S(2)}) collective-permute-start(f32[256,40]{0,1:T(8,128)S(1)} %slice.299), channel_id=1, source_target_pairs={{2,0},{3,1},{4,2},{5,3},{6,4},{7,5},{8,6},{9,7},{10,8},{11,9},{12,... | collective-permute-start | bytes 122888 | tf_op jit(solution)/shard_map/ppermute | solution.py:144
  139.5 28.8 %collective-permute-start.12 = (f32[256,40]{0,1:T(8,128)S(1)}, f32[256,40]{0,1:T(8,128)S(1)}, u32[]{:S(2)}, u32[]{:S(2)}) collective-permute-start(f32[256,40]{0,1:T(8,128)S(1)} %slice.299), channel_id=1, source_target_pairs={{0,2},{1,3},{2,4},{3,5},{4,6},{5,7},{6,8},{7,9},{8,10},{9,11},{10,... | collective-permute-start | bytes 122888 | tf_op jit(solution)/shard_map/ppermute | solution.py:144
  148.5 12.2 %collective-permute-start.11 = (f32[512,40]{0,1:T(8,128)S(1)}, f32[512,40]{0,1:T(8,128)S(1)}, u32[]{:S(2)}, u32[]{:S(2)}) collective-permute-start(f32[512,40]{0,1:T(8,128)S(1)} %fusion.47), channel_id=1, source_target_pairs={{1,0},{2,1},{3,2},{4,3},{5,4},{6,5},{7,6},{8,7},{9,8},{10,9},{11,1... | collective-permute-start | bytes 245768 | tf_op jit(solution)/shard_map/ppermute | solution.py:144
  156.1 12.1 %collective-permute-start.10 = (f32[512,40]{0,1:T(8,128)S(1)}, f32[512,40]{0,1:T(8,128)S(1)}, u32[]{:S(2)}, u32[]{:S(2)}) collective-permute-start(f32[512,40]{0,1:T(8,128)S(1)} %fusion.47), channel_id=1, source_target_pairs={{0,1},{1,2},{2,3},{3,4},{4,5},{5,6},{6,7},{7,8},{8,9},{9,10},{10,1... | collective-permute-start | bytes 245768 | tf_op jit(solution)/shard_map/ppermute | solution.py:144
  169.8 1.6 copy-start.8
  169.8 1.6 copy-start.10
  169.8 1.6 copy-start.12
  169.9 2.3 %copy-start.14 = (f32[256]{0:T(256)S(1)}, f32[256]{0:T(256)}, u32[]{:S(2)}) copy-start(f32[256]{0:T(256)} %get-tuple-element.5) | copy-start | bytes 3076
  171.4 2.2 %copy-start.13 = (f32[256]{0:T(256)S(1)}, f32[256]{0:T(256)}, u32[]{:S(2)}) copy-start(f32[256]{0:T(256)} %get-tuple-element.8) | copy-start | bytes 3076
  171.4 2.2 %copy-start = (f32[256,1024]{0,1:T(8,128)S(1)}, f32[256,1024]{0,1:T(8,128)}, u32[]{:S(2)}) copy-start(f32[256,1024]{0,1:T(8,128)} %get-tuple-element.71) | copy-start | bytes 3145732

commit v6 on v5

--- a/solution.py
+++ b/solution.py
@@ -172,12 +172,6 @@
 
 
 def update(state, gains, anomaly, weights):
-    return jnp.concatenate(
-        [update_group(state[f : f + 3], gains, anomaly, weights) for f in range(0, state.shape[0], 3)]
-    )
-
-
-def update_group(state, gains, anomaly, weights):
     fields_count, member_count, rows_tile, cols_tile = state.shape
     flattened = state.reshape(fields_count, member_count, rows_tile * cols_tile)
     deviation = flattened - jnp.mean(flattened, axis=1, keepdims=True)

time: 189 us -> 184 us (0.974)
  the two profiles are of different devices: /device:TPU:22 before, /device:TPU:30 now
where the time goes in v6:
time: 184 us; the launch traced here: 183 us
  starting transfers between devices  78.1 us (42%)
  waiting for transfers between devices  45.1 us (25%)
  local copies, waits for them, and re-layouts  23.3 us (13%)
  matrix products  19.9 us (11%)
  other arithmetic  15.6 us (8%)
    ppermute x4, starting transfers between devices, lat_shift(): return lax.ppermute(array, 'lat', pairs)  26.5 us
    ppermute x4, starting transfers between devices, lat_edges(): before = lax.ppermute(array[:, :, -1:, :], 'lat', up)  25.6 us
    ppermute x4, starting transfers between devices, lat_edges(): after = lax.ppermute(array[:, :, :1, :], 'lat', down)  21.4 us
    ppermute x4, waiting for transfers between devices, lat_edges(): after = lax.ppermute(array[:, :, :1, :], 'lat', down)  19.1 us
    ppermute x4, waiting for transfers between devices, lat_edges(): before = lax.ppermute(array[:, :, -1:, :], 'lat', up)  16 us
    ppermute x4, waiting for transfers between devices, lat_shift(): return lax.ppermute(array, 'lat', pairs)  9.17 us
    dot_general x2, matrix products, update(): jnp.einsum('om,foc->fmc', gains, covariance * weights[None], precision=la...  8.6 us
    dot_general x2, matrix products, update(): jnp.einsum('om,fmc->foc', anomaly, deviation, precision=lax.Precision.HIGH)  8 us
  transfers between devices with their start and end apart: 14, of which 10 were waited for; matrix products, arithmetic and copies ran while one was open for 10% of the time, Pallas kernels for 0%

profile of v6, /device:TPU:30, one launch (start us, length us, event | category | flops | bytes accessed | tf_op | source)
XLA Modules:
  0.0 182.7 jit_solution(15209356875831540179)
XLA Ops:
  0.0 2.4 %fusion.110 = (f32[9,40,8,18]{3,2,1,0:T(8,128)S(1)}, f32[9,40,8,18]{3,2,1,0:T(8,128)S(1)}) fusion(f32[9,40,8,128]{3,2,1,0:T(8,128)} %param.10), kind=kLoop, calls=%fused_computation.190 | loop fusion | bytes 829440 | tf_op jit(solution)/shard_map/slice | solution.py:93
  2.4 1.4 copy.40
  3.9 2.3 %collective-permute-start.1 = (f32[9,40,8,18]{1,2,3,0:T(8,128)}, f32[9,40,8,18]{1,2,3,0:T(8,128)}, u32[]{:S(2)}, u32[]{:S(2)}) collective-permute-start(f32[9,40,8,18]{1,2,3,0:T(8,128)} %copy.40), channel_id=1, source_target_pairs={{0,496},{16,0},{32,16},{48,32},{64,48},{80,64},{96,80},{112,96},{1... | collective-permute-start | bytes 622088 | tf_op jit(solution)/shard_map/ppermute | solution.py:94
  6.2 1.4 copy.39
  7.6 2.3 %collective-permute-start = (f32[9,40,8,18]{1,2,3,0:T(8,128)}, f32[9,40,8,18]{1,2,3,0:T(8,128)}, u32[]{:S(2)}, u32[]{:S(2)}) collective-permute-start(f32[9,40,8,18]{1,2,3,0:T(8,128)} %copy.39), channel_id=1, source_target_pairs={{0,16},{16,32},{32,48},{48,64},{64,80},{80,96},{96,112},{112,128},... | collective-permute-start | bytes 622088 | tf_op jit(solution)/shard_map/ppermute | solution.py:93
  10.2 1.0 gather_fusion
  11.2 0.3 fusion.75
  11.5 0.3 slice_reduce_fusion.4
  11.8 0.6 sine_multiply_fusion
  12.4 0.4 slice_reduce_fusion
  12.9 0.3 copy.27
  13.2 0.4 copy-done.20
  13.8 1.0 gather_fusion.1
  14.8 0.9 slice_reduce_fusion.2
  15.7 2.9 %multiply_multiply_fusion = (f32[256,1024]{0,1:T(8,128)}, f32[256,1024]{0,1:T(8,128)}) fusion(f32[256]{0:T(256)S(1)} %get-tuple-element.9, s32[256]{0:T(256)S(1)} %get-tuple-element.12, s32[256]{0:T(256)S(1)} %get-tuple-element.11, s32[1024]{0:T(1024)S(1)} %get-tuple-element.82, s32[1024]{0:T(1024)S(1)} %get-tuple-element.83, f32[256]{0:T(256)S(1)} %get-tuple-element.10, ...), kind=kLoop, calls=%fused_computation.58 | loop fusion | flops 12582912 | bytes 2111488 | tf_op jit(solution)/shard_map/mul | solution.py:182
  18.7 0.6 iota_compare_fusion.2
  19.3 0.8 collective-permute-done
  20.1 1.6 copy.26
  21.7 3.3 %copy.28 = f32[9,40,8,18]{3,1,2,0:T(8,128)} copy(f32[9,40,8,18]{1,2,3,0:T(8,128)} %collective-permute-done.1) | data formatting | bytes 414720 | tf_op jit(solution)/shard_map/ppermute | solution.py:94
  25.0 1.8 %pad_maximum_fusion.4 = (f32[3,40,1,164]{3,1,2,0:T(8,128)}, f32[3,40,1,164]{3,1,2,0:T(8,128)}) fusion(f32[9,40,8,18]{3,1,2,0:T(8,128)} %copy.28, f32[9,40,8,128]{3,1,2,0:T(8,128)S(1)} %copy.27, f32[9,40,8,18]{3,1,2,0:T(8,128)S(1)} %copy.26), kind=kLoop, calls=%fused_computation.131 | loop fusion | flops 78720 | bytes 2046720 | tf_op jit(solution)/shard_map/slice | solution.py:39
  26.8 3.1 %pad_maximum_fusion = f32[9,40,8,164]{3,1,2,0:T(8,128)S(1)} fusion(f32[9,40,8,18]{3,1,2,0:T(8,128)S(1)} %copy-done.2, f32[9,40,8,128]{3,1,2,0:T(8,128)} %copy-done, f32[9,40,8,18]{3,1,2,0:T(8,128)} %copy-done.1), kind=kLoop, calls=%fused_computation.8 | loop fusion | flops 944640 | bytes 3778560 | tf_op jit(solution)/shard_map/concatenate | solution.py:95
  30.0 9.1 %collective-permute-start.3 = (f32[3,40,1,164]{3,1,2,0:T(8,128)}, f32[3,40,1,164]{3,1,2,0:T(8,128)}, u32[]{:S(2)}, u32[]{:S(2)}) collective-permute-start(f32[3,40,1,164]{3,1,2,0:T(8,128)} %get-tuple-element.26), channel_id=1, source_target_pairs={{0,1},{1,2},{2,3},{3,4},{4,5},{5,6},{6,7},{7,8},{8,9},{9,10},{10,1... | collective-permute-start | bytes 236168 | tf_op jit(solution)/shard_map/ppermute | solution.py:39
  39.1 5.7 %collective-permute-start.2 = (f32[3,40,1,164]{3,1,2,0:T(8,128)}, f32[3,40,1,164]{3,1,2,0:T(8,128)}, u32[]{:S(2)}, u32[]{:S(2)}) collective-permute-start(f32[3,40,1,164]{3,1,2,0:T(8,128)} %get-tuple-element.27), channel_id=1, source_target_pairs={{1,0},{2,1},{3,2},{4,3},{5,4},{6,5},{7,6},{8,7},{9,8},{10,9},{11,1... | collective-permute-start | bytes 236168 | tf_op jit(solution)/shard_map/ppermute | solution.py:40
  44.8 1.6 fusion.109
  46.4 1.4 fusion.108
  47.8 0.7 slice.242
  48.5 0.3 copy.29
  48.7 0.7 slice.243
  49.4 1.0 copy.30
  50.5 8.7 %collective-permute-done.2 = f32[3,40,1,164]{3,1,2,0:T(8,128)} collective-permute-done((f32[3,40,1,164]{3,1,2,0:T(8,128)}, f32[3,40,1,164]{3,1,2,0:T(8,128)}, u32[]{:S(2)}, u32[]{:S(2)}) %collective-permute-start.2) | collective-permute-done | bytes 78752 | tf_op jit(solution)/shard_map/ppermute | solution.py:40
  59.2 2.7 %slice_subtract_fusion = f32[3,40,8,164]{3,1,2,0:T(8,128)S(1)} fusion(f32[9,40,8,164]{3,1,2,0:T(8,128)S(1)} %pad_maximum_fusion, f32[3,40,8,1]{3,1,2,0:T(8,128)S(1)} %copy.29, f32[3,40,8,163]{3,1,2,0:T(8,128)} %get-tuple-element.33, f32[3,40,8,163]{3,1,2,0:T(8,128)} %get-tuple-element.32, f32[3,40,8,1]{3,1,2,0:T(8,128)} %copy.30, ...), kind=kLoop, calls=%fused_computation.62 | loop fusion | flops 1416960 | bytes 3778572 | tf_op jit(solution)/shard_map/sub | solution.py:71
  62.3 0.3 fusion.119
  62.6 8.7 %collective-permute-start.5 = (f32[3,40,1,164]{3,1,2,0:T(8,128)S(1)}, f32[3,40,1,164]{3,1,2,0:T(8,128)S(1)}, u32[]{:S(2)}, u32[]{:S(2)}) collective-permute-start(f32[3,40,1,164]{3,1,2,0:T(8,128)S(1)} %get-tuple-element.59), channel_id=1, source_target_pairs={{0,1},{1,2},{2,3},{3,4},{4,5},{5,6},{6,7},{7,8},{8,9},{9,10},{10,1... | collective-permute-start | bytes 236168 | tf_op jit(solution)/shard_map/ppermute | solution.py:39
  71.3 2.0 %collective-permute-start.4 = (f32[3,40,1,164]{3,1,2,0:T(8,128)S(1)}, f32[3,40,1,164]{3,1,2,0:T(8,128)S(1)}, u32[]{:S(2)}, u32[]{:S(2)}) collective-permute-start(f32[3,40,1,164]{3,1,2,0:T(8,128)S(1)} %get-tuple-element.60), channel_id=1, source_target_pairs={{1,0},{2,1},{3,2},{4,3},{5,4},{6,5},{7,6},{8,7},{9,8},{10,9},{11,1... | collective-permute-start | bytes 236168 | tf_op jit(solution)/shard_map/ppermute | solution.py:40
  73.5 8.5 %collective-permute-done.5 = f32[3,40,1,164]{3,1,2,0:T(8,128)S(1)} collective-permute-done((f32[3,40,1,164]{3,1,2,0:T(8,128)S(1)}, f32[3,40,1,164]{3,1,2,0:T(8,128)S(1)}, u32[]{:S(2)}, u32[]{:S(2)}) %collective-permute-start.5) | collective-permute-done | bytes 78752 | tf_op jit(solution)/shard_map/ppermute | solution.py:39
  82.0 4.3 %collective-permute-done.4 = f32[3,40,1,164]{3,1,2,0:T(8,128)S(1)} collective-permute-done((f32[3,40,1,164]{3,1,2,0:T(8,128)S(1)}, f32[3,40,1,164]{3,1,2,0:T(8,128)S(1)}, u32[]{:S(2)}, u32[]{:S(2)}) %collective-permute-start.4) | collective-permute-done | bytes 78752 | tf_op jit(solution)/shard_map/ppermute | solution.py:40
  86.3 0.7 fusion.55
  87.1 5.4 %collective-permute-start.7 = (f32[3,40,1,164]{3,1,2,0:T(8,128)S(1)}, f32[3,40,1,164]{3,1,2,0:T(8,128)S(1)}, u32[]{:S(2)}, u32[]{:S(2)}) collective-permute-start(f32[3,40,1,164]{3,1,2,0:T(8,128)S(1)} %get-tuple-element.47), channel_id=1, source_target_pairs={{0,1},{1,2},{2,3},{3,4},{4,5},{5,6},{6,7},{7,8},{8,9},{9,10},{10,1... | collective-permute-start | bytes 236168 | tf_op jit(solution)/shard_map/ppermute | solution.py:39
  92.5 5.4 %collective-permute-start.6 = (f32[3,40,1,164]{3,1,2,0:T(8,128)S(1)}, f32[3,40,1,164]{3,1,2,0:T(8,128)S(1)}, u32[]{:S(2)}, u32[]{:S(2)}) collective-permute-start(f32[3,40,1,164]{3,1,2,0:T(8,128)S(1)} %get-tuple-element.48), channel_id=1, source_target_pairs={{1,0},{2,1},{3,2},{4,3},{5,4},{6,5},{7,6},{8,7},{9,8},{10,9},{11,1... | collective-permute-start | bytes 236168 | tf_op jit(solution)/shard_map/ppermute | solution.py:40
  97.9 0.3 fusion.118
  98.4 4.0 %collective-permute-done.7 = f32[3,40,1,164]{3,1,2,0:T(8,128)S(1)} collective-permute-done((f32[3,40,1,164]{3,1,2,0:T(8,128)S(1)}, f32[3,40,1,164]{3,1,2,0:T(8,128)S(1)}, u32[]{:S(2)}, u32[]{:S(2)}) %collective-permute-start.7) | collective-permute-done | bytes 78752 | tf_op jit(solution)/shard_map/ppermute | solution.py:39
  102.4 3.6 %collective-permute-done.6 = f32[3,40,1,164]{3,1,2,0:T(8,128)S(1)} collective-permute-done((f32[3,40,1,164]{3,1,2,0:T(8,128)S(1)}, f32[3,40,1,164]{3,1,2,0:T(8,128)S(1)}, u32[]{:S(2)}, u32[]{:S(2)}) %collective-permute-start.6) | collective-permute-done | bytes 78752 | tf_op jit(solution)/shard_map/ppermute | solution.py:40
  106.1 0.6 fusion.53
  107.1 0.3 fusion.111
  107.4 2.5 %collective-permute-start.9 = (f32[3,40,1,164]{3,1,2,0:T(8,128)S(1)}, f32[3,40,1,164]{3,1,2,0:T(8,128)S(1)}, u32[]{:S(2)}, u32[]{:S(2)}) collective-permute-start(f32[3,40,1,164]{3,1,2,0:T(8,128)S(1)} %get-tuple-element.40), channel_id=1, source_target_pairs={{0,1},{1,2},{2,3},{3,4},{4,5},{5,6},{6,7},{7,8},{8,9},{9,10},{10,1... | collective-permute-start | bytes 236168 | tf_op jit(solution)/shard_map/ppermute | solution.py:39
  109.9 8.2 %collective-permute-start.8 = (f32[3,40,1,164]{3,1,2,0:T(8,128)S(1)}, f32[3,40,1,164]{3,1,2,0:T(8,128)S(1)}, u32[]{:S(2)}, u32[]{:S(2)}) collective-permute-start(f32[3,40,1,164]{3,1,2,0:T(8,128)S(1)} %get-tuple-element.41), channel_id=1, source_target_pairs={{1,0},{2,1},{3,2},{4,3},{5,4},{6,5},{7,6},{8,7},{9,8},{10,9},{11,1... | collective-permute-start | bytes 236168 | tf_op jit(solution)/shard_map/ppermute | solution.py:40
  118.3 3.5 %collective-permute-done.9 = f32[3,40,1,164]{3,1,2,0:T(8,128)S(1)} collective-permute-done((f32[3,40,1,164]{3,1,2,0:T(8,128)S(1)}, f32[3,40,1,164]{3,1,2,0:T(8,128)S(1)}, u32[]{:S(2)}, u32[]{:S(2)}) %collective-permute-start.9) | collective-permute-done | bytes 78752 | tf_op jit(solution)/shard_map/ppermute | solution.py:39
  121.8 2.5 %collective-permute-done.8 = f32[3,40,1,164]{3,1,2,0:T(8,128)S(1)} collective-permute-done((f32[3,40,1,164]{3,1,2,0:T(8,128)S(1)}, f32[3,40,1,164]{3,1,2,0:T(8,128)S(1)}, u32[]{:S(2)}, u32[]{:S(2)}) %collective-permute-start.8) | collective-permute-done | bytes 78752 | tf_op jit(solution)/shard_map/ppermute | solution.py:40
  124.3 0.7 fusion.59
  125.0 0.5 fusion.63
  125.7 2.6 %fusion.29 = f32[512,40]{0,1:T(8,128)S(1)} fusion(f32[3,40,8,164]{3,1,2,0:T(8,128)S(1)} %get-tuple-element.22, f32[3,40,8,164]{3,1,2,0:T(8,128)S(1)} %get-tuple-element.23, f32[3,40,8,164]{3,1,2,0:T(8,128)S(1)} %fusion.53, pred[512,164]{0,1:T(8,128)(4,1)S(1)} %fusion.62, pred[512,8]{0,1:T(8,128)(4,1)S(1)} %copy-done.16, ...), kind=kOutput, calls=%fused_computation.42 | convolution fusion | flops 2903898624 | bytes 2063872 | tf_op jit(solution)/shard_map/jrc,fmrc->jfm/dot_general | solution.py:158
  128.3 7.5 %collective-permute-start.13 = (f32[256,40]{0,1:T(8,128)S(1)}, f32[256,40]{0,1:T(8,128)S(1)}, u32[]{:S(2)}, u32[]{:S(2)}) collective-permute-start(f32[256,40]{0,1:T(8,128)S(1)} %slice.283), channel_id=1, source_target_pairs={{2,0},{3,1},{4,2},{5,3},{6,4},{7,5},{8,6},{9,7},{10,8},{11,9},{12,... | collective-permute-start | bytes 122888 | tf_op jit(solution)/shard_map/ppermute | solution.py:144
  135.8 7.0 %collective-permute-start.12 = (f32[256,40]{0,1:T(8,128)S(1)}, f32[256,40]{0,1:T(8,128)S(1)}, u32[]{:S(2)}, u32[]{:S(2)}) collective-permute-start(f32[256,40]{0,1:T(8,128)S(1)} %slice.283), channel_id=1, source_target_pairs={{0,2},{1,3},{2,4},{3,5},{4,6},{5,7},{6,8},{7,9},{8,10},{9,11},{10,... | collective-permute-start | bytes 122888 | tf_op jit(solution)/shard_map/ppermute | solution.py:144
  142.8 10.1 %collective-permute-start.11 = (f32[512,40]{0,1:T(8,128)S(1)}, f32[512,40]{0,1:T(8,128)S(1)}, u32[]{:S(2)}, u32[]{:S(2)}) collective-permute-start(f32[512,40]{0,1:T(8,128)S(1)} %fusion.29), channel_id=1, source_target_pairs={{1,0},{2,1},{3,2},{4,3},{5,4},{6,5},{7,6},{8,7},{9,8},{10,9},{11,1... | collective-permute-start | bytes 245768 | tf_op jit(solution)/shard_map/ppermute | solution.py:144
  152.9 1.9 %collective-permute-start.10 = (f32[512,40]{0,1:T(8,128)S(1)}, f32[512,40]{0,1:T(8,128)S(1)}, u32[]{:S(2)}, u32[]{:S(2)}) collective-permute-start(f32[512,40]{0,1:T(8,128)S(1)} %fusion.29), channel_id=1, source_target_pairs={{0,1},{1,2},{2,3},{3,4},{4,5},{5,6},{6,7},{7,8},{8,9},{9,10},{10,1... | collective-permute-start | bytes 245768 | tf_op jit(solution)/shard_map/ppermute | solution.py:144
  154.9 1.5 collective-permute-done.11
  156.4 7.7 %collective-permute-done.10 = f32[512,40]{0,1:T(8,128)S(1)} collective-permute-done((f32[512,40]{0,1:T(8,128)S(1)}, f32[512,40]{0,1:T(8,128)S(1)}, u32[]{:S(2)}, u32[]{:S(2)}) %collective-permute-start.10) | collective-permute-done | bytes 81952 | tf_op jit(solution)/shard_map/ppermute | solution.py:144
  164.2 0.5 fusion.34
  164.7 3.9 %fusion.12 = f32[9,1024,256]{2,1,0:T(8,128)S(1)} fusion(f32[9,8,5,8,128]{4,3,2,1,0:T(8,128)S(1)} %get-tuple-element.29, f32[9,1024]{1,0:T(8,128)S(1)} %bitcast.79, f32[256,40]{0,1:T(8,128)S(1)} %get-tuple-element.19, f32[256]{0:T(256)S(1)} %get-tuple-element.76), kind=kOutput, calls=%fused_computation.31 | convolution fusion | flops 566609920 | bytes 10990592 | tf_op jit(solution)/shard_map/om,fmc->foc/dot_general | solution.py:178
  168.6 0.2 fusion.124
  168.9 4.3 %fusion.123 = (f32[9,1024]{1,0:T(8,128)S(1)}, f32[9,40,1024]{2,1,0:T(8,128)S(1)}) fusion(f32[256]{0:T(256)S(1)} %get-tuple-element.72, f32[256,40]{0,1:T(8,128)S(1)} %get-tuple-element.19, f32[256]{0:T(256)S(1)} %get-tuple-element.76, f32[256]{0:T(256)S(1)} %get-tuple-element.71, f32[256]{0:T(256)S(1)} %get-tuple-element.75, ...), kind=kOutput, calls=%fused_computation.203 | convolution fusion | flops 569359360 | bytes 13516800 | tf_op jit(solution)/shard_map/om,foc->fmc/dot_general | solution.py:181
  173.3 4.1 %fusion.14 = f32[9,1024,256]{2,1,0:T(8,128)S(1)} fusion(f32[9,40,1024]{2,1,0:T(8,128)S(1)} %get-tuple-element.78, f32[9,1024]{1,0:T(8,128)S(1)} %broadcast_multiply_fusion, f32[256,40]{0,1:T(8,128)S(1)} %get-tuple-element.80, f32[256]{0:T(256)S(1)} %get-tuple-element.74), kind=kOutput, calls=%fused_computation.35 | convolution fusion | flops 566609920 | bytes 10990592 | tf_op jit(solution)/shard_map/om,fmc->foc/dot_general | solution.py:178
  177.4 4.3 %fusion.13 = bf16[9,40,1024]{2,1,0:T(8,128)(2,1)S(1)} fusion(f32[9,40,1024]{2,1,0:T(8,128)S(1)} %get-tuple-element.78, f32[9,1024,256]{2,1,0:T(8,128)S(1)} %fusion.14, f32[256,1024]{0,1:T(8,128)S(1)} %copy-done.4, f32[256,40]{0,1:T(8,128)S(1)} %get-tuple-element.80, f32[256]{0:T(256)S(1)} %get-tuple-element.70, f32[256]{0:T(256)S(1)} %get-tuple-element.69, ...), kind=kOutput, calls=%fused_computation.34 | convolution fusion | flops 569368576 | bytes 12742656 | tf_op jit(solution)/shard_map/om,foc->fmc/dot_general | solution.py:181
  181.7 1.0 copy.43
  (91 shorter events, 2.3 us)
Async XLA Ops:
  3.9 6.1 %copy-start.19 = (s32[512]{0:T(512)S(1)}, s32[512]{0:T(512)}, u32[]{:S(2)}) copy-start(s32[512]{0:T(512)} %param.15) | copy-start | bytes 6148
  3.9 6.1 %copy-start.22 = (s32[512]{0:T(512)S(1)}, s32[512]{0:T(512)}, u32[]{:S(2)}) copy-start(s32[512]{0:T(512)} %param.14) | copy-start | bytes 6148
  3.9 6.1 %copy-start.23 = (s32[512]{0:T(512)S(1)}, s32[512]{0:T(512)}, u32[]{:S(2)}) copy-start(s32[512]{0:T(512)} %param.13) | copy-start | bytes 6148
  3.9 6.1 %copy-start.24 = (s32[512]{0:T(512)S(1)}, s32[512]{0:T(512)}, u32[]{:S(2)}) copy-start(s32[512]{0:T(512)} %param.12) | copy-start | bytes 6148
  3.9 6.1 %copy-start.25 = (s32[512]{0:T(512)S(1)}, s32[512]{0:T(512)}, u32[]{:S(2)}) copy-start(s32[512]{0:T(512)} %param.11) | copy-start | bytes 6148
  3.9 17.8 %collective-permute-start.1 = (f32[9,40,8,18]{1,2,3,0:T(8,128)}, f32[9,40,8,18]{1,2,3,0:T(8,128)}, u32[]{:S(2)}, u32[]{:S(2)}) collective-permute-start(f32[9,40,8,18]{1,2,3,0:T(8,128)} %copy.40), channel_id=1, source_target_pairs={{0,496},{16,0},{32,16},{48,32},{64,48},{80,64},{96,80},{112,96},{1... | collective-permute-start | bytes 622088 | tf_op jit(solution)/shard_map/ppermute | solution.py:94
  7.6 5.3 %copy-start.3 = (f32[9,40,8,128]{3,2,1,0:T(8,128)S(1)}, f32[9,40,8,128]{3,2,1,0:T(8,128)}, u32[]{:S(2)}) copy-start(f32[9,40,8,128]{3,2,1,0:T(8,128)} %param.10) | copy-start | bytes 4423684
  7.6 12.4 %collective-permute-start = (f32[9,40,8,18]{1,2,3,0:T(8,128)}, f32[9,40,8,18]{1,2,3,0:T(8,128)}, u32[]{:S(2)}, u32[]{:S(2)}) collective-permute-start(f32[9,40,8,18]{1,2,3,0:T(8,128)} %copy.39), channel_id=1, source_target_pairs={{0,16},{16,32},{32,48},{48,64},{64,80},{80,96},{96,112},{112,128},... | collective-permute-start | bytes 622088 | tf_op jit(solution)/shard_map/ppermute | solution.py:93
  11.8 4.0 %copy-start.6 = (s32[256]{0:T(256)}, s32[256]{0:T(256)S(1)}, u32[]{:S(2)}) copy-start(s32[256]{0:T(256)S(1)} %get-tuple-element.12) | copy-start | bytes 3076
  11.8 4.0 %copy-start.8 = (s32[256]{0:T(256)}, s32[256]{0:T(256)S(1)}, u32[]{:S(2)}) copy-start(s32[256]{0:T(256)S(1)} %get-tuple-element.13) | copy-start | bytes 3076
  11.8 4.0 %copy-start.10 = (s32[256]{0:T(256)}, s32[256]{0:T(256)S(1)}, u32[]{:S(2)}) copy-start(s32[256]{0:T(256)S(1)} %get-tuple-element.14) | copy-start | bytes 3076
  12.9 0.7 copy-start.20
  12.9 0.7 copy-start.21
  13.2 11.8 %copy-start = (f32[9,40,8,128]{3,1,2,0:T(8,128)}, f32[9,40,8,128]{3,1,2,0:T(8,128)S(1)}, u32[]{:S(2)}) copy-start(f32[9,40,8,128]{3,1,2,0:T(8,128)S(1)} %copy.27) | copy-start | bytes 4423684
  21.7 3.3 %copy-start.1 = (f32[9,40,8,18]{3,1,2,0:T(8,128)}, f32[9,40,8,18]{3,1,2,0:T(8,128)S(1)}, u32[]{:S(2)}) copy-start(f32[9,40,8,18]{3,1,2,0:T(8,128)S(1)} %copy.26) | copy-start | bytes 622084
  25.0 1.8 %copy-start.2 = (f32[9,40,8,18]{3,1,2,0:T(8,128)S(1)}, f32[9,40,8,18]{3,1,2,0:T(8,128)}, u32[]{:S(2)}) copy-start(f32[9,40,8,18]{3,1,2,0:T(8,128)} %copy.28) | copy-start | bytes 622084
  30.0 20.5 %collective-permute-start.3 = (f32[3,40,1,164]{3,1,2,0:T(8,128)}, f32[3,40,1,164]{3,1,2,0:T(8,128)}, u32[]{:S(2)}, u32[]{:S(2)}) collective-permute-start(f32[3,40,1,164]{3,1,2,0:T(8,128)} %get-tuple-element.26), channel_id=1, source_target_pairs={{0,1},{1,2},{2,3},{3,4},{4,5},{5,6},{6,7},{7,8},{8,9},{9,10},{10,1... | collective-permute-start | bytes 236168 | tf_op jit(solution)/shard_map/ppermute | solution.py:39
  39.1 20.1 %collective-permute-start.2 = (f32[3,40,1,164]{3,1,2,0:T(8,128)}, f32[3,40,1,164]{3,1,2,0:T(8,128)}, u32[]{:S(2)}, u32[]{:S(2)}) collective-permute-start(f32[3,40,1,164]{3,1,2,0:T(8,128)} %get-tuple-element.27), channel_id=1, source_target_pairs={{1,0},{2,1},{3,2},{4,3},{5,4},{6,5},{7,6},{8,7},{9,8},{10,9},{11,1... | collective-permute-start | bytes 236168 | tf_op jit(solution)/shard_map/ppermute | solution.py:40
  62.6 23.7 %copy-start.17 = (f32[8]{0:T(128)S(1)}, f32[8]{0:T(128)}, u32[]{:S(2)}) copy-start(f32[8]{0:T(128)} %sine_multiply_fusion) | copy-start | bytes 100
  62.6 19.4 %collective-permute-start.5 = (f32[3,40,1,164]{3,1,2,0:T(8,128)S(1)}, f32[3,40,1,164]{3,1,2,0:T(8,128)S(1)}, u32[]{:S(2)}, u32[]{:S(2)}) collective-permute-start(f32[3,40,1,164]{3,1,2,0:T(8,128)S(1)} %get-tuple-element.59), channel_id=1, source_target_pairs={{0,1},{1,2},{2,3},{3,4},{4,5},{5,6},{6,7},{7,8},{8,9},{9,10},{10,1... | collective-permute-start | bytes 236168 | tf_op jit(solution)/shard_map/ppermute | solution.py:39
  71.3 15.0 %collective-permute-start.4 = (f32[3,40,1,164]{3,1,2,0:T(8,128)S(1)}, f32[3,40,1,164]{3,1,2,0:T(8,128)S(1)}, u32[]{:S(2)}, u32[]{:S(2)}) collective-permute-start(f32[3,40,1,164]{3,1,2,0:T(8,128)S(1)} %get-tuple-element.60), channel_id=1, source_target_pairs={{1,0},{2,1},{3,2},{4,3},{5,4},{6,5},{7,6},{8,7},{9,8},{10,9},{11,1... | collective-permute-start | bytes 236168 | tf_op jit(solution)/shard_map/ppermute | solution.py:40
  87.1 15.4 %collective-permute-start.7 = (f32[3,40,1,164]{3,1,2,0:T(8,128)S(1)}, f32[3,40,1,164]{3,1,2,0:T(8,128)S(1)}, u32[]{:S(2)}, u32[]{:S(2)}) collective-permute-start(f32[3,40,1,164]{3,1,2,0:T(8,128)S(1)} %get-tuple-element.47), channel_id=1, source_target_pairs={{0,1},{1,2},{2,3},{3,4},{4,5},{5,6},{6,7},{7,8},{8,9},{9,10},{10,1... | collective-permute-start | bytes 236168 | tf_op jit(solution)/shard_map/ppermute | solution.py:39
  92.5 13.6 %collective-permute-start.6 = (f32[3,40,1,164]{3,1,2,0:T(8,128)S(1)}, f32[3,40,1,164]{3,1,2,0:T(8,128)S(1)}, u32[]{:S(2)}, u32[]{:S(2)}) collective-permute-start(f32[3,40,1,164]{3,1,2,0:T(8,128)S(1)} %get-tuple-element.48), channel_id=1, source_target_pairs={{1,0},{2,1},{3,2},{4,3},{5,4},{6,5},{7,6},{8,7},{9,8},{10,9},{11,1... | collective-permute-start | bytes 236168 | tf_op jit(solution)/shard_map/ppermute | solution.py:40
  98.2 7.8 %copy-start.18 = (f32[3]{0:T(128)S(1)}, f32[3]{0:T(128)}, u32[]{:S(2)}) copy-start(f32[3]{0:T(128)} %constant.115) | copy-start | bytes 40
  107.4 14.4 %collective-permute-start.9 = (f32[3,40,1,164]{3,1,2,0:T(8,128)S(1)}, f32[3,40,1,164]{3,1,2,0:T(8,128)S(1)}, u32[]{:S(2)}, u32[]{:S(2)}) collective-permute-start(f32[3,40,1,164]{3,1,2,0:T(8,128)S(1)} %get-tuple-element.40), channel_id=1, source_target_pairs={{0,1},{1,2},{2,3},{3,4},{4,5},{5,6},{6,7},{7,8},{8,9},{9,10},{10,1... | collective-permute-start | bytes 236168 | tf_op jit(solution)/shard_map/ppermute | solution.py:39
  109.9 14.4 %collective-permute-start.8 = (f32[3,40,1,164]{3,1,2,0:T(8,128)S(1)}, f32[3,40,1,164]{3,1,2,0:T(8,128)S(1)}, u32[]{:S(2)}, u32[]{:S(2)}) collective-permute-start(f32[3,40,1,164]{3,1,2,0:T(8,128)S(1)} %get-tuple-element.41), channel_id=1, source_target_pairs={{1,0},{2,1},{3,2},{4,3},{5,4},{6,5},{7,6},{8,7},{9,8},{10,9},{11,1... | collective-permute-start | bytes 236168 | tf_op jit(solution)/shard_map/ppermute | solution.py:40
  125.0 0.7 copy-start.16
  125.6 38.5 %copy-start.15 = (f32[256]{0:T(256)S(1)}, f32[256]{0:T(256)}, u32[]{:S(2)}) copy-start(f32[256]{0:T(256)} %get-tuple-element.7) | copy-start | bytes 3076
  125.6 38.5 %copy-start.7 = (s32[256]{0:T(256)S(1)}, s32[256]{0:T(256)}, u32[]{:S(2)}) copy-start(s32[256]{0:T(256)} %copy-done.6) | copy-start | bytes 3076
  125.6 38.5 %copy-start.9 = (s32[256]{0:T(256)S(1)}, s32[256]{0:T(256)}, u32[]{:S(2)}) copy-start(s32[256]{0:T(256)} %copy-done.8) | copy-start | bytes 3076
  125.6 38.5 %copy-start.11 = (s32[256]{0:T(256)S(1)}, s32[256]{0:T(256)}, u32[]{:S(2)}) copy-start(s32[256]{0:T(256)} %copy-done.10) | copy-start | bytes 3076
  128.3 35.8 %collective-permute-start.13 = (f32[256,40]{0,1:T(8,128)S(1)}, f32[256,40]{0,1:T(8,128)S(1)}, u32[]{:S(2)}, u32[]{:S(2)}) collective-permute-start(f32[256,40]{0,1:T(8,128)S(1)} %slice.283), channel_id=1, source_target_pairs={{2,0},{3,1},{4,2},{5,3},{6,4},{7,5},{8,6},{9,7},{10,8},{11,9},{12,... | collective-permute-start | bytes 122888 | tf_op jit(solution)/shard_map/ppermute | solution.py:144
  135.8 28.3 %collective-permute-start.12 = (f32[256,40]{0,1:T(8,128)S(1)}, f32[256,40]{0,1:T(8,128)S(1)}, u32[]{:S(2)}, u32[]{:S(2)}) collective-permute-start(f32[256,40]{0,1:T(8,128)S(1)} %slice.283), channel_id=1, source_target_pairs={{0,2},{1,3},{2,4},{3,5},{4,6},{5,7},{6,8},{7,9},{8,10},{9,11},{10,... | collective-permute-start | bytes 122888 | tf_op jit(solution)/shard_map/ppermute | solution.py:144
  142.8 13.6 %collective-permute-start.11 = (f32[512,40]{0,1:T(8,128)S(1)}, f32[512,40]{0,1:T(8,128)S(1)}, u32[]{:S(2)}, u32[]{:S(2)}) collective-permute-start(f32[512,40]{0,1:T(8,128)S(1)} %fusion.29), channel_id=1, source_target_pairs={{1,0},{2,1},{3,2},{4,3},{5,4},{6,5},{7,6},{8,7},{9,8},{10,9},{11,1... | collective-permute-start | bytes 245768 | tf_op jit(solution)/shard_map/ppermute | solution.py:144
  152.9 11.1 %collective-permute-start.10 = (f32[512,40]{0,1:T(8,128)S(1)}, f32[512,40]{0,1:T(8,128)S(1)}, u32[]{:S(2)}, u32[]{:S(2)}) collective-permute-start(f32[512,40]{0,1:T(8,128)S(1)} %fusion.29), channel_id=1, source_target_pairs={{0,1},{1,2},{2,3},{3,4},{4,5},{5,6},{6,7},{7,8},{8,9},{9,10},{10,1... | collective-permute-start | bytes 245768 | tf_op jit(solution)/shard_map/ppermute | solution.py:144
  164.1 0.6 copy-start.14
  164.7 4.1 %copy-start.5 = (f32[256,1024]{0,1:T(8,128)S(1)}, f32[256,1024]{0,1:T(8,128)}, u32[]{:S(2)}) copy-start(f32[256,1024]{0,1:T(8,128)} %get-tuple-element.68) | copy-start | bytes 3145732
  168.8 4.4 %copy-start.13 = (f32[256]{0:T(256)S(1)}, f32[256]{0:T(256)}, u32[]{:S(2)}) copy-start(f32[256]{0:T(256)} %get-tuple-element.5) | copy-start | bytes 3076
  168.8 4.4 %copy-start.12 = (f32[256]{0:T(256)S(1)}, f32[256]{0:T(256)}, u32[]{:S(2)}) copy-start(f32[256]{0:T(256)} %get-tuple-element.8) | copy-start | bytes 3076
  173.3 4.1 %copy-start.4 = (f32[256,1024]{0,1:T(8,128)S(1)}, f32[256,1024]{0,1:T(8,128)}, u32[]{:S(2)}) copy-start(f32[256,1024]{0,1:T(8,128)} %get-tuple-element.67) | copy-start | bytes 3145732

commit v7 on v6

--- a/solution.py
+++ b/solution.py
@@ -90,8 +90,11 @@
 
 def lon_widened(state, width):
     size = lax.axis_size("lon")
-    left = lax.ppermute(state[..., -width:], "lon", ring_pairs(size, 1))
-    right = lax.ppermute(state[..., :width], "lon", ring_pairs(size, -1))
+    order = (0, 3, 2, 1)
+    left = lax.ppermute(jnp.transpose(state[..., -width:], order), "lon", ring_pairs(size, 1))
+    right = lax.ppermute(jnp.transpose(state[..., :width], order), "lon", ring_pairs(size, -1))
+    left = jnp.transpose(left, order)
+    right = jnp.transpose(right, order)
     return jnp.concatenate([left, state, right], axis=3)
 
 

time: 184 us -> 176 us (0.957)
  local copies, waits for them, and re-layouts: 23.3 us -> 15 us
  waiting for transfers between devices: 45.1 us -> 51.6 us
  other arithmetic: 15.6 us -> 9.82 us
    ppermute x4, waiting for transfers between devices: 19.1 us -> 26.1 us  [lat_edges(): after = lax.ppermute(array[:, :, :1, :], 'lat', down)]
    ppermute x2, local copies, waits for them, and re-layouts: 4.9 us -> 2.2 us  [the longest x1 1.64 us: lon_widened(): lax.ppermute(jnp.transpose(state[..., :width], order), 'lon', ring_pairs(...]
    slice x7 -> x5, local copies, waits for them, and re-layouts: 3.29 us -> 0.81 us  [zonal_inside(): return zonal(values, values[..., :1], values[..., -1:])]
    ppermute x4, waiting for transfers between devices: 16 us -> 13.9 us  [lat_edges(): before = lax.ppermute(array[:, :, -1:, :], 'lat', up)]
    sub x2, other arithmetic: 3.37 us -> 1.33 us  [march_prediction(): height - RATE * depths * (zonal_inside(eastward_speed) + meridional(merid...]
    ppermute x4, starting transfers between devices: 25.6 us -> 23.7 us  [lat_edges(): before = lax.ppermute(array[:, :, -1:, :], 'lat', up)]
    ppermute x4, starting transfers between devices: 21.4 us -> 23.3 us  [lat_edges(): after = lax.ppermute(array[:, :, :1, :], 'lat', down)]
    concatenate x1, other arithmetic: 3.12 us -> 1.22 us  [lon_widened(): return jnp.concatenate([left, state, right], axis=3)]
  transfers between devices with their start and end apart: 14 -> 14, of which waited for: 10 -> 11; matrix products, arithmetic and copies ran while one was open for 10% -> 6% of each run, Pallas kernels for 0% -> 0%
where the time goes in v7:
time: 176 us; the launch traced here: 175 us
  starting transfers between devices  78.1 us (44%)
  waiting for transfers between devices  51.6 us (29%)
  matrix products  20.1 us (11%)
  local copies, waits for them, and re-layouts  15 us (9%)
  other arithmetic  9.82 us (6%)
    ppermute x4, starting transfers between devices, lat_shift(): return lax.ppermute(array, 'lat', pairs)  26.5 us
    ppermute x4, waiting for transfers between devices, lat_edges(): after = lax.ppermute(array[:, :, :1, :], 'lat', down)  26.1 us
    ppermute x4, starting transfers between devices, lat_edges(): before = lax.ppermute(array[:, :, -1:, :], 'lat', up)  23.7 us
    ppermute x4, starting transfers between devices, lat_edges(): after = lax.ppermute(array[:, :, :1, :], 'lat', down)  23.3 us
    ppermute x4, waiting for transfers between devices, lat_edges(): before = lax.ppermute(array[:, :, -1:, :], 'lat', up)  13.9 us
    ppermute x4, waiting for transfers between devices, lat_shift(): return lax.ppermute(array, 'lat', pairs)  10 us
    dot_general x2, matrix products, update(): jnp.einsum('om,foc->fmc', gains, covariance * weights[None], precision=la...  8.8 us
    dot_general x2, matrix products, update(): jnp.einsum('om,fmc->foc', anomaly, deviation, precision=lax.Precision.HIGH)  7.98 us
  transfers between devices with their start and end apart: 14, of which 11 were waited for; matrix products, arithmetic and copies ran while one was open for 6% of the time, Pallas kernels for 0%

profile of v7, /device:TPU:30, one launch (start us, length us, event | category | flops | bytes accessed | tf_op | source)
XLA Modules:
  0.0 175.2 jit_solution(3117938247719087580)
XLA Ops:
  0.0 2.3 %fusion.110 = (f32[9,40,8,18]{3,2,1,0:T(8,128)S(1)}, f32[9,40,8,18]{3,2,1,0:T(8,128)S(1)}) fusion(f32[9,40,8,128]{3,2,1,0:T(8,128)} %param.10), kind=kLoop, calls=%fused_computation.190 | loop fusion | bytes 829440 | tf_op jit(solution)/shard_map/slice | solution.py:94
  2.3 1.4 copy.38
  3.8 2.3 %collective-permute-start.1 = (f32[9,18,8,40]{3,2,1,0:T(8,128)}, f32[9,18,8,40]{3,2,1,0:T(8,128)}, u32[]{:S(2)}, u32[]{:S(2)}) collective-permute-start(f32[9,18,8,40]{3,2,1,0:T(8,128)} %bitcast.89), channel_id=1, source_target_pairs={{0,496},{16,0},{32,16},{48,32},{64,48},{80,64},{96,80},{112,96},{1... | collective-permute-start | bytes 622088 | tf_op jit(solution)/shard_map/ppermute | solution.py:95
  6.1 0.6 copy.37
  6.7 2.3 %collective-permute-start = (f32[9,18,8,40]{3,2,1,0:T(8,128)S(1)}, f32[9,18,8,40]{3,2,1,0:T(8,128)S(1)}, u32[]{:S(2)}, u32[]{:S(2)}) collective-permute-start(f32[9,18,8,40]{3,2,1,0:T(8,128)S(1)} %bitcast.90), channel_id=1, source_target_pairs={{0,16},{16,32},{32,48},{48,64},{64,80},{80,96},{96,112},{112,128},... | collective-permute-start | bytes 622088 | tf_op jit(solution)/shard_map/ppermute | solution.py:94
  9.1 0.1 copy.30
  9.3 1.0 gather_fusion
  10.3 0.3 fusion.75
  10.6 0.3 slice_reduce_fusion.4
  10.9 0.4 slice_reduce_fusion
  11.4 1.4 copy.28
  12.9 0.1 copy.31
  13.0 1.0 gather_fusion.1
  14.1 0.3 slice_reduce_fusion.2
  14.4 2.9 %multiply_multiply_fusion = (f32[256,1024]{0,1:T(8,128)}, f32[256,1024]{0,1:T(8,128)}) fusion(f32[256]{0:T(256)S(1)} %get-tuple-element.9, s32[256]{0:T(256)S(1)} %get-tuple-element.12, s32[256]{0:T(256)S(1)} %get-tuple-element.11, s32[1024]{0:T(1024)S(1)} %get-tuple-element.82, s32[1024]{0:T(1024)S(1)} %get-tuple-element.83, f32[256]{0:T(256)S(1)} %get-tuple-element.10, ...), kind=kLoop, calls=%fused_computation.58 | loop fusion | flops 12582912 | bytes 2111488 | tf_op jit(solution)/shard_map/mul | solution.py:185
  17.3 1.5 collective-permute-done
  18.8 0.6 copy.25
  19.4 1.6 copy.27
  21.1 1.1 pad_maximum_fusion.4
  22.2 0.3 copy-done
  22.5 1.2 pad_maximum_fusion
  23.7 9.1 %collective-permute-start.3 = (f32[3,40,1,164]{3,1,2,0:T(8,128)S(1)}, f32[3,40,1,164]{3,1,2,0:T(8,128)S(1)}, u32[]{:S(2)}, u32[]{:S(2)}) collective-permute-start(f32[3,40,1,164]{3,1,2,0:T(8,128)S(1)} %get-tuple-element.26), channel_id=1, source_target_pairs={{0,1},{1,2},{2,3},{3,4},{4,5},{5,6},{6,7},{7,8},{8,9},{9,10},{10,1... | collective-permute-start | bytes 236168 | tf_op jit(solution)/shard_map/ppermute | solution.py:39
  32.8 5.7 %collective-permute-start.2 = (f32[3,40,1,164]{3,1,2,0:T(8,128)S(1)}, f32[3,40,1,164]{3,1,2,0:T(8,128)S(1)}, u32[]{:S(2)}, u32[]{:S(2)}) collective-permute-start(f32[3,40,1,164]{3,1,2,0:T(8,128)S(1)} %get-tuple-element.27), channel_id=1, source_target_pairs={{1,0},{2,1},{3,2},{4,3},{5,4},{6,5},{7,6},{8,7},{9,8},{10,9},{11,1... | collective-permute-start | bytes 236168 | tf_op jit(solution)/shard_map/ppermute | solution.py:40
  38.6 0.3 fusion.109
  39.1 0.2 slice.242
  39.3 0.9 collective-permute-done.3
  40.1 13.3 %collective-permute-done.2 = f32[3,40,1,164]{3,1,2,0:T(8,128)S(1)} collective-permute-done((f32[3,40,1,164]{3,1,2,0:T(8,128)S(1)}, f32[3,40,1,164]{3,1,2,0:T(8,128)S(1)}, u32[]{:S(2)}, u32[]{:S(2)}) %collective-permute-start.2) | collective-permute-done | bytes 78752 | tf_op jit(solution)/shard_map/ppermute | solution.py:40
  53.5 0.7 slice_subtract_fusion
  54.5 0.3 fusion.119
  54.8 8.0 %collective-permute-start.5 = (f32[3,40,1,164]{3,1,2,0:T(8,128)S(1)}, f32[3,40,1,164]{3,1,2,0:T(8,128)S(1)}, u32[]{:S(2)}, u32[]{:S(2)}) collective-permute-start(f32[3,40,1,164]{3,1,2,0:T(8,128)S(1)} %get-tuple-element.59), channel_id=1, source_target_pairs={{0,1},{1,2},{2,3},{3,4},{4,5},{5,6},{6,7},{7,8},{8,9},{9,10},{10,1... | collective-permute-start | bytes 236168 | tf_op jit(solution)/shard_map/ppermute | solution.py:39
  62.8 2.7 %collective-permute-start.4 = (f32[3,40,1,164]{3,1,2,0:T(8,128)S(1)}, f32[3,40,1,164]{3,1,2,0:T(8,128)S(1)}, u32[]{:S(2)}, u32[]{:S(2)}) collective-permute-start(f32[3,40,1,164]{3,1,2,0:T(8,128)S(1)} %get-tuple-element.60), channel_id=1, source_target_pairs={{1,0},{2,1},{3,2},{4,3},{5,4},{6,5},{7,6},{8,7},{9,8},{10,9},{11,1... | collective-permute-start | bytes 236168 | tf_op jit(solution)/shard_map/ppermute | solution.py:40
  65.5 0.2 fusion.120
  65.7 7.3 %collective-permute-done.5 = f32[3,40,1,164]{3,1,2,0:T(8,128)S(1)} collective-permute-done((f32[3,40,1,164]{3,1,2,0:T(8,128)S(1)}, f32[3,40,1,164]{3,1,2,0:T(8,128)S(1)}, u32[]{:S(2)}, u32[]{:S(2)}) %collective-permute-start.5) | collective-permute-done | bytes 78752 | tf_op jit(solution)/shard_map/ppermute | solution.py:39
  73.0 6.2 %collective-permute-done.4 = f32[3,40,1,164]{3,1,2,0:T(8,128)S(1)} collective-permute-done((f32[3,40,1,164]{3,1,2,0:T(8,128)S(1)}, f32[3,40,1,164]{3,1,2,0:T(8,128)S(1)}, u32[]{:S(2)}, u32[]{:S(2)}) %collective-permute-start.4) | collective-permute-done | bytes 78752 | tf_op jit(solution)/shard_map/ppermute | solution.py:40
  79.2 0.7 fusion.55
  80.0 4.0 %collective-permute-start.7 = (f32[3,40,1,164]{3,1,2,0:T(8,128)S(1)}, f32[3,40,1,164]{3,1,2,0:T(8,128)S(1)}, u32[]{:S(2)}, u32[]{:S(2)}) collective-permute-start(f32[3,40,1,164]{3,1,2,0:T(8,128)S(1)} %get-tuple-element.47), channel_id=1, source_target_pairs={{0,1},{1,2},{2,3},{3,4},{4,5},{5,6},{6,7},{7,8},{8,9},{9,10},{10,1... | collective-permute-start | bytes 236168 | tf_op jit(solution)/shard_map/ppermute | solution.py:39
  84.0 6.7 %collective-permute-start.6 = (f32[3,40,1,164]{3,1,2,0:T(8,128)S(1)}, f32[3,40,1,164]{3,1,2,0:T(8,128)S(1)}, u32[]{:S(2)}, u32[]{:S(2)}) collective-permute-start(f32[3,40,1,164]{3,1,2,0:T(8,128)S(1)} %get-tuple-element.48), channel_id=1, source_target_pairs={{1,0},{2,1},{3,2},{4,3},{5,4},{6,5},{7,6},{8,7},{9,8},{10,9},{11,1... | collective-permute-start | bytes 236168 | tf_op jit(solution)/shard_map/ppermute | solution.py:40
  90.7 0.3 fusion.118
  91.0 0.2 fusion.117
  91.2 2.2 %collective-permute-done.7 = f32[3,40,1,164]{3,1,2,0:T(8,128)S(1)} collective-permute-done((f32[3,40,1,164]{3,1,2,0:T(8,128)S(1)}, f32[3,40,1,164]{3,1,2,0:T(8,128)S(1)}, u32[]{:S(2)}, u32[]{:S(2)}) %collective-permute-start.7) | collective-permute-done | bytes 78752 | tf_op jit(solution)/shard_map/ppermute | solution.py:39
  93.4 2.1 %collective-permute-done.6 = f32[3,40,1,164]{3,1,2,0:T(8,128)S(1)} collective-permute-done((f32[3,40,1,164]{3,1,2,0:T(8,128)S(1)}, f32[3,40,1,164]{3,1,2,0:T(8,128)S(1)}, u32[]{:S(2)}, u32[]{:S(2)}) %collective-permute-start.6) | collective-permute-done | bytes 78752 | tf_op jit(solution)/shard_map/ppermute | solution.py:40
  95.5 0.7 fusion.53
  96.5 0.3 fusion.111
  96.8 2.7 %collective-permute-start.9 = (f32[3,40,1,164]{3,1,2,0:T(8,128)S(1)}, f32[3,40,1,164]{3,1,2,0:T(8,128)S(1)}, u32[]{:S(2)}, u32[]{:S(2)}) collective-permute-start(f32[3,40,1,164]{3,1,2,0:T(8,128)S(1)} %get-tuple-element.40), channel_id=1, source_target_pairs={{0,1},{1,2},{2,3},{3,4},{4,5},{5,6},{6,7},{7,8},{8,9},{9,10},{10,1... | collective-permute-start | bytes 236168 | tf_op jit(solution)/shard_map/ppermute | solution.py:39
  99.5 8.2 %collective-permute-start.8 = (f32[3,40,1,164]{3,1,2,0:T(8,128)S(1)}, f32[3,40,1,164]{3,1,2,0:T(8,128)S(1)}, u32[]{:S(2)}, u32[]{:S(2)}) collective-permute-start(f32[3,40,1,164]{3,1,2,0:T(8,128)S(1)} %get-tuple-element.41), channel_id=1, source_target_pairs={{1,0},{2,1},{3,2},{4,3},{5,4},{6,5},{7,6},{8,7},{9,8},{10,9},{11,1... | collective-permute-start | bytes 236168 | tf_op jit(solution)/shard_map/ppermute | solution.py:40
  107.7 0.2 fusion.112
  107.9 3.6 %collective-permute-done.9 = f32[3,40,1,164]{3,1,2,0:T(8,128)S(1)} collective-permute-done((f32[3,40,1,164]{3,1,2,0:T(8,128)S(1)}, f32[3,40,1,164]{3,1,2,0:T(8,128)S(1)}, u32[]{:S(2)}, u32[]{:S(2)}) %collective-permute-start.9) | collective-permute-done | bytes 78752 | tf_op jit(solution)/shard_map/ppermute | solution.py:39
  111.5 4.5 %collective-permute-done.8 = f32[3,40,1,164]{3,1,2,0:T(8,128)S(1)} collective-permute-done((f32[3,40,1,164]{3,1,2,0:T(8,128)S(1)}, f32[3,40,1,164]{3,1,2,0:T(8,128)S(1)}, u32[]{:S(2)}, u32[]{:S(2)}) %collective-permute-start.8) | collective-permute-done | bytes 78752 | tf_op jit(solution)/shard_map/ppermute | solution.py:40
  115.9 0.7 fusion.59
  116.7 0.5 fusion.63
  117.2 2.6 %fusion.29 = f32[512,40]{0,1:T(8,128)S(1)} fusion(f32[3,40,8,164]{3,1,2,0:T(8,128)S(1)} %get-tuple-element.22, f32[3,40,8,164]{3,1,2,0:T(8,128)S(1)} %get-tuple-element.23, f32[3,40,8,164]{3,1,2,0:T(8,128)S(1)} %fusion.53, pred[512,164]{0,1:T(8,128)(4,1)S(1)} %fusion.62, pred[512,8]{0,1:T(8,128)(4,1)S(1)} %iota_compare_fusion.2, ...), kind=kOutput, calls=%fused_computation.42 | convolution fusion | flops 2903898624 | bytes 2063872 | tf_op jit(solution)/shard_map/jrc,fmrc->jfm/dot_general | solution.py:161
  119.8 8.2 %collective-permute-start.13 = (f32[256,40]{0,1:T(8,128)S(1)}, f32[256,40]{0,1:T(8,128)S(1)}, u32[]{:S(2)}, u32[]{:S(2)}) collective-permute-start(f32[256,40]{0,1:T(8,128)S(1)} %slice.283), channel_id=1, source_target_pairs={{2,0},{3,1},{4,2},{5,3},{6,4},{7,5},{8,6},{9,7},{10,8},{11,9},{12,... | collective-permute-start | bytes 122888 | tf_op jit(solution)/shard_map/ppermute | solution.py:147
  128.0 6.3 %collective-permute-start.12 = (f32[256,40]{0,1:T(8,128)S(1)}, f32[256,40]{0,1:T(8,128)S(1)}, u32[]{:S(2)}, u32[]{:S(2)}) collective-permute-start(f32[256,40]{0,1:T(8,128)S(1)} %slice.283), channel_id=1, source_target_pairs={{0,2},{1,3},{2,4},{3,5},{4,6},{5,7},{6,8},{7,9},{8,10},{9,11},{10,... | collective-permute-start | bytes 122888 | tf_op jit(solution)/shard_map/ppermute | solution.py:147
  134.4 10.1 %collective-permute-start.11 = (f32[512,40]{0,1:T(8,128)S(1)}, f32[512,40]{0,1:T(8,128)S(1)}, u32[]{:S(2)}, u32[]{:S(2)}) collective-permute-start(f32[512,40]{0,1:T(8,128)S(1)} %fusion.29), channel_id=1, source_target_pairs={{1,0},{2,1},{3,2},{4,3},{5,4},{6,5},{7,6},{8,7},{9,8},{10,9},{11,1... | collective-permute-start | bytes 245768 | tf_op jit(solution)/shard_map/ppermute | solution.py:147
  144.4 1.9 %collective-permute-start.10 = (f32[512,40]{0,1:T(8,128)S(1)}, f32[512,40]{0,1:T(8,128)S(1)}, u32[]{:S(2)}, u32[]{:S(2)}) collective-permute-start(f32[512,40]{0,1:T(8,128)S(1)} %fusion.29), channel_id=1, source_target_pairs={{0,1},{1,2},{2,3},{3,4},{4,5},{5,6},{6,7},{7,8},{8,9},{9,10},{10,1... | collective-permute-start | bytes 245768 | tf_op jit(solution)/shard_map/ppermute | solution.py:147
  146.4 0.9 collective-permute-done.11
  147.3 9.2 %collective-permute-done.10 = f32[512,40]{0,1:T(8,128)S(1)} collective-permute-done((f32[512,40]{0,1:T(8,128)S(1)}, f32[512,40]{0,1:T(8,128)S(1)}, u32[]{:S(2)}, u32[]{:S(2)}) %collective-permute-start.10) | collective-permute-done | bytes 81952 | tf_op jit(solution)/shard_map/ppermute | solution.py:147
  156.6 0.5 fusion.34
  157.1 3.9 %fusion.12 = f32[9,1024,256]{2,1,0:T(8,128)S(1)} fusion(f32[9,8,5,8,128]{4,3,2,1,0:T(8,128)S(1)} %get-tuple-element.29, f32[9,1024]{1,0:T(8,128)S(1)} %bitcast.91, f32[256,40]{0,1:T(8,128)S(1)} %get-tuple-element.19, f32[256]{0:T(256)S(1)} %get-tuple-element.76), kind=kOutput, calls=%fused_computation.31 | convolution fusion | flops 566609920 | bytes 10990592 | tf_op jit(solution)/shard_map/om,fmc->foc/dot_general | solution.py:181
  161.0 0.2 fusion.124
  161.2 4.3 %fusion.123 = (f32[9,1024]{1,0:T(8,128)S(1)}, f32[9,40,1024]{2,1,0:T(8,128)S(1)}) fusion(f32[256]{0:T(256)S(1)} %get-tuple-element.72, f32[256,40]{0,1:T(8,128)S(1)} %get-tuple-element.19, f32[256]{0:T(256)S(1)} %get-tuple-element.76, f32[256]{0:T(256)S(1)} %get-tuple-element.71, f32[256]{0:T(256)S(1)} %get-tuple-element.75, ...), kind=kOutput, calls=%fused_computation.203 | convolution fusion | flops 569359360 | bytes 13516800 | tf_op jit(solution)/shard_map/om,foc->fmc/dot_general | solution.py:184
  165.6 4.1 %fusion.14 = f32[9,1024,256]{2,1,0:T(8,128)S(1)} fusion(f32[9,40,1024]{2,1,0:T(8,128)S(1)} %get-tuple-element.78, f32[9,1024]{1,0:T(8,128)S(1)} %broadcast_multiply_fusion, f32[256,40]{0,1:T(8,128)S(1)} %get-tuple-element.80, f32[256]{0:T(256)S(1)} %get-tuple-element.74), kind=kOutput, calls=%fused_computation.35 | convolution fusion | flops 566609920 | bytes 10990592 | tf_op jit(solution)/shard_map/om,fmc->foc/dot_general | solution.py:181
  169.7 4.5 %fusion.13 = bf16[9,40,1024]{2,1,0:T(8,128)(2,1)S(1)} fusion(f32[9,40,1024]{2,1,0:T(8,128)S(1)} %get-tuple-element.78, f32[9,1024,256]{2,1,0:T(8,128)S(1)} %fusion.14, f32[256,1024]{0,1:T(8,128)S(1)} %copy-done.2, f32[256,40]{0,1:T(8,128)S(1)} %get-tuple-element.80, f32[256]{0:T(256)S(1)} %get-tuple-element.70, f32[256]{0:T(256)S(1)} %get-tuple-element.69, ...), kind=kOutput, calls=%fused_computation.34 | convolution fusion | flops 569368576 | bytes 12742656 | tf_op jit(solution)/shard_map/om,foc->fmc/dot_general | solution.py:184
  174.2 1.0 copy.41
  (61 shorter events, 1.4 us)
Async XLA Ops:
  3.8 5.3 %copy-start.5 = (s32[512]{0:T(512)S(1)}, s32[512]{0:T(512)}, u32[]{:S(2)}) copy-start(s32[512]{0:T(512)} %param.15) | copy-start | bytes 6148
  3.8 5.3 %copy-start.8 = (s32[512]{0:T(512)S(1)}, s32[512]{0:T(512)}, u32[]{:S(2)}) copy-start(s32[512]{0:T(512)} %param.14) | copy-start | bytes 6148
  3.8 5.3 %copy-start.9 = (s32[512]{0:T(512)S(1)}, s32[512]{0:T(512)}, u32[]{:S(2)}) copy-start(s32[512]{0:T(512)} %param.13) | copy-start | bytes 6148
  3.8 5.3 %copy-start.10 = (s32[512]{0:T(512)S(1)}, s32[512]{0:T(512)}, u32[]{:S(2)}) copy-start(s32[512]{0:T(512)} %param.12) | copy-start | bytes 6148
  3.8 5.3 %copy-start.11 = (s32[512]{0:T(512)S(1)}, s32[512]{0:T(512)}, u32[]{:S(2)}) copy-start(s32[512]{0:T(512)} %param.11) | copy-start | bytes 6148
  3.8 15.6 %collective-permute-start.1 = (f32[9,18,8,40]{3,2,1,0:T(8,128)}, f32[9,18,8,40]{3,2,1,0:T(8,128)}, u32[]{:S(2)}, u32[]{:S(2)}) collective-permute-start(f32[9,18,8,40]{3,2,1,0:T(8,128)} %bitcast.89), channel_id=1, source_target_pairs={{0,496},{16,0},{32,16},{48,32},{64,48},{80,64},{96,80},{112,96},{1... | collective-permute-start | bytes 622088 | tf_op jit(solution)/shard_map/ppermute | solution.py:95
  6.7 4.7 %copy-start.1 = (f32[9,40,8,128]{3,2,1,0:T(8,128)S(1)}, f32[9,40,8,128]{3,2,1,0:T(8,128)}, u32[]{:S(2)}) copy-start(f32[9,40,8,128]{3,2,1,0:T(8,128)} %param.10) | copy-start | bytes 4423684
  6.7 12.1 %collective-permute-start = (f32[9,18,8,40]{3,2,1,0:T(8,128)S(1)}, f32[9,18,8,40]{3,2,1,0:T(8,128)S(1)}, u32[]{:S(2)}, u32[]{:S(2)}) collective-permute-start(f32[9,18,8,40]{3,2,1,0:T(8,128)S(1)} %bitcast.90), channel_id=1, source_target_pairs={{0,16},{16,32},{32,48},{48,64},{64,80},{80,96},{96,112},{112,128},... | collective-permute-start | bytes 622088 | tf_op jit(solution)/shard_map/ppermute | solution.py:94
  11.4 1.4 copy-start.6
  11.4 1.4 copy-start.7
  21.1 1.4 copy-start
  23.7 16.4 %collective-permute-start.3 = (f32[3,40,1,164]{3,1,2,0:T(8,128)S(1)}, f32[3,40,1,164]{3,1,2,0:T(8,128)S(1)}, u32[]{:S(2)}, u32[]{:S(2)}) collective-permute-start(f32[3,40,1,164]{3,1,2,0:T(8,128)S(1)} %get-tuple-element.26), channel_id=1, source_target_pairs={{0,1},{1,2},{2,3},{3,4},{4,5},{5,6},{6,7},{7,8},{8,9},{9,10},{10,1... | collective-permute-start | bytes 236168 | tf_op jit(solution)/shard_map/ppermute | solution.py:39
  32.8 20.7 %collective-permute-start.2 = (f32[3,40,1,164]{3,1,2,0:T(8,128)S(1)}, f32[3,40,1,164]{3,1,2,0:T(8,128)S(1)}, u32[]{:S(2)}, u32[]{:S(2)}) collective-permute-start(f32[3,40,1,164]{3,1,2,0:T(8,128)S(1)} %get-tuple-element.27), channel_id=1, source_target_pairs={{1,0},{2,1},{3,2},{4,3},{5,4},{6,5},{7,6},{8,7},{9,8},{10,9},{11,1... | collective-permute-start | bytes 236168 | tf_op jit(solution)/shard_map/ppermute | solution.py:40
  39.0 14.4 %copy-start.4 = (f32[3]{0:T(128)S(1)}, f32[3]{0:T(128)}, u32[]{:S(2)}) copy-start(f32[3]{0:T(128)} %constant.115) | copy-start | bytes 40
  54.8 18.1 %collective-permute-start.5 = (f32[3,40,1,164]{3,1,2,0:T(8,128)S(1)}, f32[3,40,1,164]{3,1,2,0:T(8,128)S(1)}, u32[]{:S(2)}, u32[]{:S(2)}) collective-permute-start(f32[3,40,1,164]{3,1,2,0:T(8,128)S(1)} %get-tuple-element.59), channel_id=1, source_target_pairs={{0,1},{1,2},{2,3},{3,4},{4,5},{5,6},{6,7},{7,8},{8,9},{9,10},{10,1... | collective-permute-start | bytes 236168 | tf_op jit(solution)/shard_map/ppermute | solution.py:39
  62.8 16.3 %collective-permute-start.4 = (f32[3,40,1,164]{3,1,2,0:T(8,128)S(1)}, f32[3,40,1,164]{3,1,2,0:T(8,128)S(1)}, u32[]{:S(2)}, u32[]{:S(2)}) collective-permute-start(f32[3,40,1,164]{3,1,2,0:T(8,128)S(1)} %get-tuple-element.60), channel_id=1, source_target_pairs={{1,0},{2,1},{3,2},{4,3},{5,4},{6,5},{7,6},{8,7},{9,8},{10,9},{11,1... | collective-permute-start | bytes 236168 | tf_op jit(solution)/shard_map/ppermute | solution.py:40
  80.0 13.4 %collective-permute-start.7 = (f32[3,40,1,164]{3,1,2,0:T(8,128)S(1)}, f32[3,40,1,164]{3,1,2,0:T(8,128)S(1)}, u32[]{:S(2)}, u32[]{:S(2)}) collective-permute-start(f32[3,40,1,164]{3,1,2,0:T(8,128)S(1)} %get-tuple-element.47), channel_id=1, source_target_pairs={{0,1},{1,2},{2,3},{3,4},{4,5},{5,6},{6,7},{7,8},{8,9},{9,10},{10,1... | collective-permute-start | bytes 236168 | tf_op jit(solution)/shard_map/ppermute | solution.py:39
  84.0 11.5 %collective-permute-start.6 = (f32[3,40,1,164]{3,1,2,0:T(8,128)S(1)}, f32[3,40,1,164]{3,1,2,0:T(8,128)S(1)}, u32[]{:S(2)}, u32[]{:S(2)}) collective-permute-start(f32[3,40,1,164]{3,1,2,0:T(8,128)S(1)} %get-tuple-element.48), channel_id=1, source_target_pairs={{1,0},{2,1},{3,2},{4,3},{5,4},{6,5},{7,6},{8,7},{9,8},{10,9},{11,1... | collective-permute-start | bytes 236168 | tf_op jit(solution)/shard_map/ppermute | solution.py:40
  96.8 14.6 %collective-permute-start.9 = (f32[3,40,1,164]{3,1,2,0:T(8,128)S(1)}, f32[3,40,1,164]{3,1,2,0:T(8,128)S(1)}, u32[]{:S(2)}, u32[]{:S(2)}) collective-permute-start(f32[3,40,1,164]{3,1,2,0:T(8,128)S(1)} %get-tuple-element.40), channel_id=1, source_target_pairs={{0,1},{1,2},{2,3},{3,4},{4,5},{5,6},{6,7},{7,8},{8,9},{9,10},{10,1... | collective-permute-start | bytes 236168 | tf_op jit(solution)/shard_map/ppermute | solution.py:39
  99.5 16.4 %collective-permute-start.8 = (f32[3,40,1,164]{3,1,2,0:T(8,128)S(1)}, f32[3,40,1,164]{3,1,2,0:T(8,128)S(1)}, u32[]{:S(2)}, u32[]{:S(2)}) collective-permute-start(f32[3,40,1,164]{3,1,2,0:T(8,128)S(1)} %get-tuple-element.41), channel_id=1, source_target_pairs={{1,0},{2,1},{3,2},{4,3},{5,4},{6,5},{7,6},{8,7},{9,8},{10,9},{11,1... | collective-permute-start | bytes 236168 | tf_op jit(solution)/shard_map/ppermute | solution.py:40
  119.8 36.7 %collective-permute-start.13 = (f32[256,40]{0,1:T(8,128)S(1)}, f32[256,40]{0,1:T(8,128)S(1)}, u32[]{:S(2)}, u32[]{:S(2)}) collective-permute-start(f32[256,40]{0,1:T(8,128)S(1)} %slice.283), channel_id=1, source_target_pairs={{2,0},{3,1},{4,2},{5,3},{6,4},{7,5},{8,6},{9,7},{10,8},{11,9},{12,... | collective-permute-start | bytes 122888 | tf_op jit(solution)/shard_map/ppermute | solution.py:147
  128.0 28.4 %collective-permute-start.12 = (f32[256,40]{0,1:T(8,128)S(1)}, f32[256,40]{0,1:T(8,128)S(1)}, u32[]{:S(2)}, u32[]{:S(2)}) collective-permute-start(f32[256,40]{0,1:T(8,128)S(1)} %slice.283), channel_id=1, source_target_pairs={{0,2},{1,3},{2,4},{3,5},{4,6},{5,7},{6,8},{7,9},{8,10},{9,11},{10,... | collective-permute-start | bytes 122888 | tf_op jit(solution)/shard_map/ppermute | solution.py:147
  134.4 12.9 %collective-permute-start.11 = (f32[512,40]{0,1:T(8,128)S(1)}, f32[512,40]{0,1:T(8,128)S(1)}, u32[]{:S(2)}, u32[]{:S(2)}) collective-permute-start(f32[512,40]{0,1:T(8,128)S(1)} %fusion.29), channel_id=1, source_target_pairs={{1,0},{2,1},{3,2},{4,3},{5,4},{6,5},{7,6},{8,7},{9,8},{10,9},{11,1... | collective-permute-start | bytes 245768 | tf_op jit(solution)/shard_map/ppermute | solution.py:147
  144.4 12.0 %collective-permute-start.10 = (f32[512,40]{0,1:T(8,128)S(1)}, f32[512,40]{0,1:T(8,128)S(1)}, u32[]{:S(2)}, u32[]{:S(2)}) collective-permute-start(f32[512,40]{0,1:T(8,128)S(1)} %fusion.29), channel_id=1, source_target_pairs={{0,1},{1,2},{2,3},{3,4},{4,5},{5,6},{6,7},{7,8},{8,9},{9,10},{10,1... | collective-permute-start | bytes 245768 | tf_op jit(solution)/shard_map/ppermute | solution.py:147
  157.1 4.1 %copy-start.3 = (f32[256,1024]{0,1:T(8,128)S(1)}, f32[256,1024]{0,1:T(8,128)}, u32[]{:S(2)}) copy-start(f32[256,1024]{0,1:T(8,128)} %get-tuple-element.68) | copy-start | bytes 3145732
  165.6 4.1 %copy-start.2 = (f32[256,1024]{0,1:T(8,128)S(1)}, f32[256,1024]{0,1:T(8,128)}, u32[]{:S(2)}) copy-start(f32[256,1024]{0,1:T(8,128)} %get-tuple-element.67) | copy-start | bytes 3145732

commit v8 on v7

--- a/solution.py
+++ b/solution.py
@@ -228,8 +228,11 @@
     (lon1, lat1, kind1, radius1), (value1, error1) = batches[1]
     table0 = band[:NB]
     both = band + lat_shift(band, 1) + lat_shift(band, -1)
+    raw1 = both[NB:]
+    gains, anomaly = statistics(both[:NB], value0, error0, member_count)
+    state = update(state, gains, anomaly, tile_weights(state, lon0, lat0, radius0))
+    table0, state = lax.optimization_barrier((table0, state))
     priors = both[:NB] + lat_shift(table0, 2) + lat_shift(table0, -2)
-    raw1 = both[NB:]
     gains, anomaly = statistics(priors, value0, error0, member_count)
     deviation = raw1 - jnp.mean(raw1, axis=1, keepdims=True)
     covariance = jnp.einsum(
@@ -238,7 +241,6 @@
     weights = localize(lon1, lat1, lon0, lat0, radius0, grid_lon)
     increment = jnp.einsum("om,oj->jm", gains, covariance * weights, precision=lax.Precision.HIGH)
     priors1 = raw1 + increment
-    state = update(state, gains, anomaly, tile_weights(state, lon0, lat0, radius0))
     gains, anomaly = statistics(priors1, value1, error1, member_count)
     state = update(state, gains, anomaly, tile_weights(state, lon1, lat1, radius1))
     return state.astype(jnp.bfloat16)

time: 176 us -> 180 us (1.023)
  the two profiles are of different devices: /device:TPU:30 before, /device:TPU:94 now
where the time goes in v8:
time: 180 us; the launch traced here: 179 us
  starting transfers between devices  76.4 us (42%)
  waiting for transfers between devices  57.1 us (32%)
  matrix products  19.6 us (11%)
  local copies, waits for them, and re-layouts  15.6 us (9%)
  other arithmetic  9.97 us (6%)
    ppermute x4, starting transfers between devices, lat_shift(): return lax.ppermute(array, 'lat', pairs)  25 us
    ppermute x4, starting transfers between devices, lat_edges(): before = lax.ppermute(array[:, :, -1:, :], 'lat', up)  24.6 us
    ppermute x4, starting transfers between devices, lat_edges(): after = lax.ppermute(array[:, :, :1, :], 'lat', down)  22.2 us
    ppermute x4, waiting for transfers between devices, lat_edges(): before = lax.ppermute(array[:, :, -1:, :], 'lat', up)  20.4 us
    ppermute x4, waiting for transfers between devices, lat_edges(): after = lax.ppermute(array[:, :, :1, :], 'lat', down)  17.7 us
    ppermute x4, waiting for transfers between devices, lat_shift(): return lax.ppermute(array, 'lat', pairs)  17.5 us
    dot_general x2, matrix products, update(): jnp.einsum('om,foc->fmc', gains, covariance * weights[None], precision=la...  8.55 us
    dot_general x2, matrix products, update(): jnp.einsum('om,fmc->foc', anomaly, deviation, precision=lax.Precision.HIGH)  7.76 us
  transfers between devices with their start and end apart: 14, of which 13 were waited for; matrix products, arithmetic and copies ran while one was open for 6% of the time, Pallas kernels for 0%

profile of v8, /device:TPU:94, one launch (start us, length us, event | category | flops | bytes accessed | tf_op | source)
XLA Modules:
  0.0 179.4 jit_solution(1372994198739771530)
XLA Ops:
  0.0 2.3 %fusion.123 = (f32[9,40,8,18]{3,2,1,0:T(8,128)S(1)}, f32[9,40,8,18]{3,2,1,0:T(8,128)S(1)}) fusion(f32[9,40,8,128]{3,2,1,0:T(8,128)} %param.10), kind=kLoop, calls=%fused_computation.209 | loop fusion | bytes 829440 | tf_op jit(solution)/shard_map/slice | solution.py:94
  2.3 1.4 copy.38
  3.8 2.3 %collective-permute-start.1 = (f32[9,18,8,40]{3,2,1,0:T(8,128)}, f32[9,18,8,40]{3,2,1,0:T(8,128)}, u32[]{:S(2)}, u32[]{:S(2)}) collective-permute-start(f32[9,18,8,40]{3,2,1,0:T(8,128)} %bitcast.97), channel_id=1, source_target_pairs={{0,496},{16,0},{32,16},{48,32},{64,48},{80,64},{96,80},{112,96},{1... | collective-permute-start | bytes 622088 | tf_op jit(solution)/shard_map/ppermute | solution.py:95
  6.1 0.6 copy.37
  6.7 2.3 %collective-permute-start = (f32[9,18,8,40]{3,2,1,0:T(8,128)S(1)}, f32[9,18,8,40]{3,2,1,0:T(8,128)S(1)}, u32[]{:S(2)}, u32[]{:S(2)}) collective-permute-start(f32[9,18,8,40]{3,2,1,0:T(8,128)S(1)} %bitcast.98), channel_id=1, source_target_pairs={{0,16},{16,32},{32,48},{48,64},{64,80},{80,96},{96,112},{112,128},... | collective-permute-start | bytes 622088 | tf_op jit(solution)/shard_map/ppermute | solution.py:94
  9.3 1.0 gather_fusion
  10.3 0.3 fusion.75
  10.6 0.3 slice_reduce_fusion.4
  10.9 0.4 slice_reduce_fusion
  11.4 1.4 copy.29
  13.0 1.0 gather_fusion.1
  14.1 0.3 slice_reduce_fusion.2
  14.4 2.9 %multiply_multiply_fusion = (f32[256,1024]{0,1:T(8,128)}, f32[256,1024]{0,1:T(8,128)}) fusion(f32[256]{0:T(256)S(1)} %get-tuple-element.13, s32[256]{0:T(256)S(1)} %get-tuple-element.16, s32[256]{0:T(256)S(1)} %get-tuple-element.15, s32[1024]{0:T(1024)S(1)} %get-tuple-element.88, s32[1024]{0:T(1024)S(1)} %get-tuple-element.89, f32[256]{0:T(256)S(1)} %get-tuple-element.14, ...), kind=kLoop, calls=%fused_computation.58 | loop fusion | flops 12582912 | bytes 2111488 | tf_op jit(solution)/shard_map/mul | solution.py:185
  17.3 1.5 collective-permute-done
  18.8 0.6 copy.26
  19.4 1.6 copy.28
  21.1 1.1 pad_maximum_fusion.4
  22.2 0.3 copy-done
  22.5 1.2 pad_maximum_fusion
  23.7 9.1 %collective-permute-start.3 = (f32[3,40,1,164]{3,1,2,0:T(8,128)S(1)}, f32[3,40,1,164]{3,1,2,0:T(8,128)S(1)}, u32[]{:S(2)}, u32[]{:S(2)}) collective-permute-start(f32[3,40,1,164]{3,1,2,0:T(8,128)S(1)} %get-tuple-element.32), channel_id=1, source_target_pairs={{0,1},{1,2},{2,3},{3,4},{4,5},{5,6},{6,7},{7,8},{8,9},{9,10},{10,1... | collective-permute-start | bytes 236168 | tf_op jit(solution)/shard_map/ppermute | solution.py:39
  32.8 3.9 %collective-permute-start.2 = (f32[3,40,1,164]{3,1,2,0:T(8,128)S(1)}, f32[3,40,1,164]{3,1,2,0:T(8,128)S(1)}, u32[]{:S(2)}, u32[]{:S(2)}) collective-permute-start(f32[3,40,1,164]{3,1,2,0:T(8,128)S(1)} %get-tuple-element.33), channel_id=1, source_target_pairs={{1,0},{2,1},{3,2},{4,3},{5,4},{6,5},{7,6},{8,7},{9,8},{10,9},{11,1... | collective-permute-start | bytes 236168 | tf_op jit(solution)/shard_map/ppermute | solution.py:40
  36.8 0.3 fusion.122
  37.5 6.8 %collective-permute-done.3 = f32[3,40,1,164]{3,1,2,0:T(8,128)S(1)} collective-permute-done((f32[3,40,1,164]{3,1,2,0:T(8,128)S(1)}, f32[3,40,1,164]{3,1,2,0:T(8,128)S(1)}, u32[]{:S(2)}, u32[]{:S(2)}) %collective-permute-start.3) | collective-permute-done | bytes 78752 | tf_op jit(solution)/shard_map/ppermute | solution.py:39
  44.3 1.7 collective-permute-done.2
  46.0 0.7 slice_subtract_fusion
  47.0 0.3 fusion.132
  47.4 10.4 %collective-permute-start.5 = (f32[3,40,1,164]{3,1,2,0:T(8,128)S(1)}, f32[3,40,1,164]{3,1,2,0:T(8,128)S(1)}, u32[]{:S(2)}, u32[]{:S(2)}) collective-permute-start(f32[3,40,1,164]{3,1,2,0:T(8,128)S(1)} %get-tuple-element.65), channel_id=1, source_target_pairs={{0,1},{1,2},{2,3},{3,4},{4,5},{5,6},{6,7},{7,8},{8,9},{9,10},{10,1... | collective-permute-start | bytes 236168 | tf_op jit(solution)/shard_map/ppermute | solution.py:39
  57.8 1.9 %collective-permute-start.4 = (f32[3,40,1,164]{3,1,2,0:T(8,128)S(1)}, f32[3,40,1,164]{3,1,2,0:T(8,128)S(1)}, u32[]{:S(2)}, u32[]{:S(2)}) collective-permute-start(f32[3,40,1,164]{3,1,2,0:T(8,128)S(1)} %get-tuple-element.66), channel_id=1, source_target_pairs={{1,0},{2,1},{3,2},{4,3},{5,4},{6,5},{7,6},{8,7},{9,8},{10,9},{11,1... | collective-permute-start | bytes 236168 | tf_op jit(solution)/shard_map/ppermute | solution.py:40
  59.9 6.6 %collective-permute-done.5 = f32[3,40,1,164]{3,1,2,0:T(8,128)S(1)} collective-permute-done((f32[3,40,1,164]{3,1,2,0:T(8,128)S(1)}, f32[3,40,1,164]{3,1,2,0:T(8,128)S(1)}, u32[]{:S(2)}, u32[]{:S(2)}) %collective-permute-start.5) | collective-permute-done | bytes 78752 | tf_op jit(solution)/shard_map/ppermute | solution.py:39
  66.5 6.6 %collective-permute-done.4 = f32[3,40,1,164]{3,1,2,0:T(8,128)S(1)} collective-permute-done((f32[3,40,1,164]{3,1,2,0:T(8,128)S(1)}, f32[3,40,1,164]{3,1,2,0:T(8,128)S(1)}, u32[]{:S(2)}, u32[]{:S(2)}) %collective-permute-start.4) | collective-permute-done | bytes 78752 | tf_op jit(solution)/shard_map/ppermute | solution.py:40
  73.1 0.7 fusion.55
  73.9 2.9 %collective-permute-start.7 = (f32[3,40,1,164]{3,1,2,0:T(8,128)S(1)}, f32[3,40,1,164]{3,1,2,0:T(8,128)S(1)}, u32[]{:S(2)}, u32[]{:S(2)}) collective-permute-start(f32[3,40,1,164]{3,1,2,0:T(8,128)S(1)} %get-tuple-element.53), channel_id=1, source_target_pairs={{0,1},{1,2},{2,3},{3,4},{4,5},{5,6},{6,7},{7,8},{8,9},{9,10},{10,1... | collective-permute-start | bytes 236168 | tf_op jit(solution)/shard_map/ppermute | solution.py:39
  76.8 7.8 %collective-permute-start.6 = (f32[3,40,1,164]{3,1,2,0:T(8,128)S(1)}, f32[3,40,1,164]{3,1,2,0:T(8,128)S(1)}, u32[]{:S(2)}, u32[]{:S(2)}) collective-permute-start(f32[3,40,1,164]{3,1,2,0:T(8,128)S(1)} %get-tuple-element.54), channel_id=1, source_target_pairs={{1,0},{2,1},{3,2},{4,3},{5,4},{6,5},{7,6},{8,7},{9,8},{10,9},{11,1... | collective-permute-start | bytes 236168 | tf_op jit(solution)/shard_map/ppermute | solution.py:40
  84.5 0.3 fusion.131
  84.9 0.2 fusion.130
  85.1 3.6 %collective-permute-done.7 = f32[3,40,1,164]{3,1,2,0:T(8,128)S(1)} collective-permute-done((f32[3,40,1,164]{3,1,2,0:T(8,128)S(1)}, f32[3,40,1,164]{3,1,2,0:T(8,128)S(1)}, u32[]{:S(2)}, u32[]{:S(2)}) %collective-permute-start.7) | collective-permute-done | bytes 78752 | tf_op jit(solution)/shard_map/ppermute | solution.py:39
  88.7 6.7 %collective-permute-done.6 = f32[3,40,1,164]{3,1,2,0:T(8,128)S(1)} collective-permute-done((f32[3,40,1,164]{3,1,2,0:T(8,128)S(1)}, f32[3,40,1,164]{3,1,2,0:T(8,128)S(1)}, u32[]{:S(2)}, u32[]{:S(2)}) %collective-permute-start.6) | collective-permute-done | bytes 78752 | tf_op jit(solution)/shard_map/ppermute | solution.py:40
  95.3 0.7 fusion.53
  96.4 0.3 fusion.124
  96.7 2.2 %collective-permute-start.9 = (f32[3,40,1,164]{3,1,2,0:T(8,128)S(1)}, f32[3,40,1,164]{3,1,2,0:T(8,128)S(1)}, u32[]{:S(2)}, u32[]{:S(2)}) collective-permute-start(f32[3,40,1,164]{3,1,2,0:T(8,128)S(1)} %get-tuple-element.46), channel_id=1, source_target_pairs={{0,1},{1,2},{2,3},{3,4},{4,5},{5,6},{6,7},{7,8},{8,9},{9,10},{10,1... | collective-permute-start | bytes 236168 | tf_op jit(solution)/shard_map/ppermute | solution.py:39
  99.0 8.6 %collective-permute-start.8 = (f32[3,40,1,164]{3,1,2,0:T(8,128)S(1)}, f32[3,40,1,164]{3,1,2,0:T(8,128)S(1)}, u32[]{:S(2)}, u32[]{:S(2)}) collective-permute-start(f32[3,40,1,164]{3,1,2,0:T(8,128)S(1)} %get-tuple-element.47), channel_id=1, source_target_pairs={{1,0},{2,1},{3,2},{4,3},{5,4},{6,5},{7,6},{8,7},{9,8},{10,9},{11,1... | collective-permute-start | bytes 236168 | tf_op jit(solution)/shard_map/ppermute | solution.py:40
  107.6 0.2 fusion.125
  107.8 3.3 %collective-permute-done.9 = f32[3,40,1,164]{3,1,2,0:T(8,128)S(1)} collective-permute-done((f32[3,40,1,164]{3,1,2,0:T(8,128)S(1)}, f32[3,40,1,164]{3,1,2,0:T(8,128)S(1)}, u32[]{:S(2)}, u32[]{:S(2)}) %collective-permute-start.9) | collective-permute-done | bytes 78752 | tf_op jit(solution)/shard_map/ppermute | solution.py:39
  111.1 2.8 %collective-permute-done.8 = f32[3,40,1,164]{3,1,2,0:T(8,128)S(1)} collective-permute-done((f32[3,40,1,164]{3,1,2,0:T(8,128)S(1)}, f32[3,40,1,164]{3,1,2,0:T(8,128)S(1)}, u32[]{:S(2)}, u32[]{:S(2)}) %collective-permute-start.8) | collective-permute-done | bytes 78752 | tf_op jit(solution)/shard_map/ppermute | solution.py:40
  113.9 0.7 fusion.59
  114.6 0.5 fusion.63
  115.1 2.6 %fusion.29 = f32[512,40]{0,1:T(8,128)S(1)} fusion(f32[3,40,8,164]{3,1,2,0:T(8,128)S(1)} %get-tuple-element.28, f32[3,40,8,164]{3,1,2,0:T(8,128)S(1)} %get-tuple-element.29, f32[3,40,8,164]{3,1,2,0:T(8,128)S(1)} %fusion.53, pred[512,164]{0,1:T(8,128)(4,1)S(1)} %fusion.62, pred[512,8]{0,1:T(8,128)(4,1)S(1)} %iota_compare_fusion.2, ...), kind=kOutput, calls=%fused_computation.42 | convolution fusion | flops 2903898624 | bytes 2063872 | tf_op jit(solution)/shard_map/jrc,fmrc->jfm/dot_general | solution.py:161
  117.8 8.3 %collective-permute-start.11 = (f32[512,40]{0,1:T(8,128)S(1)}, f32[512,40]{0,1:T(8,128)S(1)}, u32[]{:S(2)}, u32[]{:S(2)}) collective-permute-start(f32[512,40]{0,1:T(8,128)S(1)} %fusion.29), channel_id=1, source_target_pairs={{1,0},{2,1},{3,2},{4,3},{5,4},{6,5},{7,6},{8,7},{9,8},{10,9},{11,1... | collective-permute-start | bytes 245768 | tf_op jit(solution)/shard_map/ppermute | solution.py:147
  126.0 1.9 %collective-permute-start.10 = (f32[512,40]{0,1:T(8,128)S(1)}, f32[512,40]{0,1:T(8,128)S(1)}, u32[]{:S(2)}, u32[]{:S(2)}) collective-permute-start(f32[512,40]{0,1:T(8,128)S(1)} %fusion.29), channel_id=1, source_target_pairs={{0,1},{1,2},{2,3},{3,4},{4,5},{5,6},{6,7},{7,8},{8,9},{9,10},{10,1... | collective-permute-start | bytes 245768 | tf_op jit(solution)/shard_map/ppermute | solution.py:147
  128.0 1.6 collective-permute-done.11
  129.6 8.6 %collective-permute-done.10 = f32[512,40]{0,1:T(8,128)S(1)} collective-permute-done((f32[512,40]{0,1:T(8,128)S(1)}, f32[512,40]{0,1:T(8,128)S(1)}, u32[]{:S(2)}, u32[]{:S(2)}) %collective-permute-start.10) | collective-permute-done | bytes 81952 | tf_op jit(solution)/shard_map/ppermute | solution.py:147
  138.3 3.9 %fusion.12 = f32[9,1024,256]{2,1,0:T(8,128)S(1)} fusion(f32[9,8,5,8,128]{4,3,2,1,0:T(8,128)S(1)} %get-tuple-element.35, f32[9,1024]{1,0:T(8,128)S(1)} %bitcast.100, f32[512,40]{0,1:T(8,128)S(1)} %add_add_fusion.2, f32[256]{0:T(256)S(1)} %get-tuple-element.85), kind=kOutput, calls=%fused_computation.31 | convolution fusion | flops 566609920 | bytes 11019264 | tf_op jit(solution)/shard_map/om,fmc->foc/dot_general | solution.py:181
  142.2 4.3 %bitcast_add_fusion = f32[9,40,1024]{2,1,0:T(8,128)S(1)} fusion(f32[9,1024,256]{2,1,0:T(8,128)S(1)} %fusion.12, f32[256,1024]{0,1:T(8,128)S(1)} %copy-done.3, f32[9,8,5,8,128]{4,3,2,1,0:T(8,128)S(1)} %get-tuple-element.35, f32[512,40]{0,1:T(8,128)S(1)} %add_add_fusion.2, f32[256]{0:T(256)S(1)} %get-tuple-element.79, f32[256]{0:T(256)S(1)} %get-tuple-element.78, ...), kind=kOutput, calls=%fused_computation.29 | convolution fusion | flops 568999936 | bytes 13479936 | tf_op jit(solution)/shard_map/om,foc->fmc/dot_general | solution.py:184
  146.5 0.3 copy.41
  146.8 6.8 %collective-permute-start.13 = (f32[256,40]{0,1:T(8,128)S(1)}, f32[256,40]{0,1:T(8,128)S(1)}, u32[]{:S(2)}, u32[]{:S(2)}) collective-permute-start(f32[256,40]{0,1:T(8,128)S(1)} %slice.283), channel_id=1, source_target_pairs={{2,0},{3,1},{4,2},{5,3},{6,4},{7,5},{8,6},{9,7},{10,8},{11,9},{12,... | collective-permute-start | bytes 122888 | tf_op jit(solution)/shard_map/ppermute | solution.py:147
  153.7 7.9 %collective-permute-start.12 = (f32[256,40]{0,1:T(8,128)S(1)}, f32[256,40]{0,1:T(8,128)S(1)}, u32[]{:S(2)}, u32[]{:S(2)}) collective-permute-start(f32[256,40]{0,1:T(8,128)S(1)} %slice.283), channel_id=1, source_target_pairs={{0,2},{1,3},{2,4},{3,5},{4,6},{5,7},{6,8},{7,9},{8,10},{9,11},{10,... | collective-permute-start | bytes 122888 | tf_op jit(solution)/shard_map/ppermute | solution.py:147
  161.7 0.2 reshape.497
  162.0 0.3 collective-permute-done.13
  162.3 7.0 %collective-permute-done.12 = f32[256,40]{0,1:T(8,128)S(1)} collective-permute-done((f32[256,40]{0,1:T(8,128)S(1)}, f32[256,40]{0,1:T(8,128)S(1)}, u32[]{:S(2)}, u32[]{:S(2)}) %collective-permute-start.12) | collective-permute-done | bytes 40992 | tf_op jit(solution)/shard_map/ppermute | solution.py:147
  169.4 0.5 fusion.34
  169.9 0.2 fusion.136
  170.2 3.9 %fusion.14 = f32[9,1024,256]{2,1,0:T(8,128)S(1)} fusion(f32[9,40,1024]{2,1,0:T(8,128)S(1)} %reshape.497, f32[9,1024]{1,0:T(8,128)S(1)} %bitcast.99, f32[256,40]{0,1:T(8,128)S(1)} %get-tuple-element.87, f32[256]{0:T(256)S(1)} %get-tuple-element.81), kind=kOutput, calls=%fused_computation.35 | convolution fusion | flops 566609920 | bytes 10990592 | tf_op jit(solution)/shard_map/om,fmc->foc/dot_general | solution.py:181
  174.1 4.3 %fusion.13 = bf16[9,40,1024]{2,1,0:T(8,128)(2,1)S(1)} fusion(f32[9,40,1024]{2,1,0:T(8,128)S(1)} %reshape.497, f32[9,1024,256]{2,1,0:T(8,128)S(1)} %fusion.14, f32[256,1024]{0,1:T(8,128)S(1)} %copy-done.2, f32[256,40]{0,1:T(8,128)S(1)} %get-tuple-element.87, f32[256]{0:T(256)S(1)} %get-tuple-element.75, f32[256]{0:T(256)S(1)} %get-tuple-element.74, ...), kind=kOutput, calls=%fused_computation.34 | convolution fusion | flops 569368576 | bytes 12742656 | tf_op jit(solution)/shard_map/om,foc->fmc/dot_general | solution.py:184
  178.3 1.0 copy.43
  (71 shorter events, 2.2 us)
Async XLA Ops:
  3.8 5.3 %copy-start.5 = (s32[512]{0:T(512)S(1)}, s32[512]{0:T(512)}, u32[]{:S(2)}) copy-start(s32[512]{0:T(512)} %param.15) | copy-start | bytes 6148
  3.8 5.3 %copy-start.8 = (s32[512]{0:T(512)S(1)}, s32[512]{0:T(512)}, u32[]{:S(2)}) copy-start(s32[512]{0:T(512)} %param.14) | copy-start | bytes 6148
  3.8 5.3 %copy-start.9 = (s32[512]{0:T(512)S(1)}, s32[512]{0:T(512)}, u32[]{:S(2)}) copy-start(s32[512]{0:T(512)} %param.13) | copy-start | bytes 6148
  3.8 5.3 %copy-start.10 = (s32[512]{0:T(512)S(1)}, s32[512]{0:T(512)}, u32[]{:S(2)}) copy-start(s32[512]{0:T(512)} %param.12) | copy-start | bytes 6148
  3.8 5.3 %copy-start.11 = (s32[512]{0:T(512)S(1)}, s32[512]{0:T(512)}, u32[]{:S(2)}) copy-start(s32[512]{0:T(512)} %param.11) | copy-start | bytes 6148
  3.8 15.6 %collective-permute-start.1 = (f32[9,18,8,40]{3,2,1,0:T(8,128)}, f32[9,18,8,40]{3,2,1,0:T(8,128)}, u32[]{:S(2)}, u32[]{:S(2)}) collective-permute-start(f32[9,18,8,40]{3,2,1,0:T(8,128)} %bitcast.97), channel_id=1, source_target_pairs={{0,496},{16,0},{32,16},{48,32},{64,48},{80,64},{96,80},{112,96},{1... | collective-permute-start | bytes 622088 | tf_op jit(solution)/shard_map/ppermute | solution.py:95
  6.7 4.7 %copy-start.1 = (f32[9,40,8,128]{3,2,1,0:T(8,128)S(1)}, f32[9,40,8,128]{3,2,1,0:T(8,128)}, u32[]{:S(2)}) copy-start(f32[9,40,8,128]{3,2,1,0:T(8,128)} %param.10) | copy-start | bytes 4423684
  6.7 12.1 %collective-permute-start = (f32[9,18,8,40]{3,2,1,0:T(8,128)S(1)}, f32[9,18,8,40]{3,2,1,0:T(8,128)S(1)}, u32[]{:S(2)}, u32[]{:S(2)}) collective-permute-start(f32[9,18,8,40]{3,2,1,0:T(8,128)S(1)} %bitcast.98), channel_id=1, source_target_pairs={{0,16},{16,32},{32,48},{48,64},{64,80},{80,96},{96,112},{112,128},... | collective-permute-start | bytes 622088 | tf_op jit(solution)/shard_map/ppermute | solution.py:94
  11.4 1.4 copy-start.6
  11.4 1.4 copy-start.7
  21.1 1.4 copy-start
  23.7 20.6 %collective-permute-start.3 = (f32[3,40,1,164]{3,1,2,0:T(8,128)S(1)}, f32[3,40,1,164]{3,1,2,0:T(8,128)S(1)}, u32[]{:S(2)}, u32[]{:S(2)}) collective-permute-start(f32[3,40,1,164]{3,1,2,0:T(8,128)S(1)} %get-tuple-element.32), channel_id=1, source_target_pairs={{0,1},{1,2},{2,3},{3,4},{4,5},{5,6},{6,7},{7,8},{8,9},{9,10},{10,1... | collective-permute-start | bytes 236168 | tf_op jit(solution)/shard_map/ppermute | solution.py:39
  32.8 13.2 %collective-permute-start.2 = (f32[3,40,1,164]{3,1,2,0:T(8,128)S(1)}, f32[3,40,1,164]{3,1,2,0:T(8,128)S(1)}, u32[]{:S(2)}, u32[]{:S(2)}) collective-permute-start(f32[3,40,1,164]{3,1,2,0:T(8,128)S(1)} %get-tuple-element.33), channel_id=1, source_target_pairs={{1,0},{2,1},{3,2},{4,3},{5,4},{6,5},{7,6},{8,7},{9,8},{10,9},{11,1... | collective-permute-start | bytes 236168 | tf_op jit(solution)/shard_map/ppermute | solution.py:40
  37.2 8.8 %copy-start.4 = (f32[3]{0:T(128)S(1)}, f32[3]{0:T(128)}, u32[]{:S(2)}) copy-start(f32[3]{0:T(128)} %constant.117) | copy-start | bytes 40
  47.4 19.1 %collective-permute-start.5 = (f32[3,40,1,164]{3,1,2,0:T(8,128)S(1)}, f32[3,40,1,164]{3,1,2,0:T(8,128)S(1)}, u32[]{:S(2)}, u32[]{:S(2)}) collective-permute-start(f32[3,40,1,164]{3,1,2,0:T(8,128)S(1)} %get-tuple-element.65), channel_id=1, source_target_pairs={{0,1},{1,2},{2,3},{3,4},{4,5},{5,6},{6,7},{7,8},{8,9},{9,10},{10,1... | collective-permute-start | bytes 236168 | tf_op jit(solution)/shard_map/ppermute | solution.py:39
  57.8 15.3 %collective-permute-start.4 = (f32[3,40,1,164]{3,1,2,0:T(8,128)S(1)}, f32[3,40,1,164]{3,1,2,0:T(8,128)S(1)}, u32[]{:S(2)}, u32[]{:S(2)}) collective-permute-start(f32[3,40,1,164]{3,1,2,0:T(8,128)S(1)} %get-tuple-element.66), channel_id=1, source_target_pairs={{1,0},{2,1},{3,2},{4,3},{5,4},{6,5},{7,6},{8,7},{9,8},{10,9},{11,1... | collective-permute-start | bytes 236168 | tf_op jit(solution)/shard_map/ppermute | solution.py:40
  73.9 14.8 %collective-permute-start.7 = (f32[3,40,1,164]{3,1,2,0:T(8,128)S(1)}, f32[3,40,1,164]{3,1,2,0:T(8,128)S(1)}, u32[]{:S(2)}, u32[]{:S(2)}) collective-permute-start(f32[3,40,1,164]{3,1,2,0:T(8,128)S(1)} %get-tuple-element.53), channel_id=1, source_target_pairs={{0,1},{1,2},{2,3},{3,4},{4,5},{5,6},{6,7},{7,8},{8,9},{9,10},{10,1... | collective-permute-start | bytes 236168 | tf_op jit(solution)/shard_map/ppermute | solution.py:39
  76.8 18.6 %collective-permute-start.6 = (f32[3,40,1,164]{3,1,2,0:T(8,128)S(1)}, f32[3,40,1,164]{3,1,2,0:T(8,128)S(1)}, u32[]{:S(2)}, u32[]{:S(2)}) collective-permute-start(f32[3,40,1,164]{3,1,2,0:T(8,128)S(1)} %get-tuple-element.54), channel_id=1, source_target_pairs={{1,0},{2,1},{3,2},{4,3},{5,4},{6,5},{7,6},{8,7},{9,8},{10,9},{11,1... | collective-permute-start | bytes 236168 | tf_op jit(solution)/shard_map/ppermute | solution.py:40
  96.7 14.4 %collective-permute-start.9 = (f32[3,40,1,164]{3,1,2,0:T(8,128)S(1)}, f32[3,40,1,164]{3,1,2,0:T(8,128)S(1)}, u32[]{:S(2)}, u32[]{:S(2)}) collective-permute-start(f32[3,40,1,164]{3,1,2,0:T(8,128)S(1)} %get-tuple-element.46), channel_id=1, source_target_pairs={{0,1},{1,2},{2,3},{3,4},{4,5},{5,6},{6,7},{7,8},{8,9},{9,10},{10,1... | collective-permute-start | bytes 236168 | tf_op jit(solution)/shard_map/ppermute | solution.py:39
  99.0 15.0 %collective-permute-start.8 = (f32[3,40,1,164]{3,1,2,0:T(8,128)S(1)}, f32[3,40,1,164]{3,1,2,0:T(8,128)S(1)}, u32[]{:S(2)}, u32[]{:S(2)}) collective-permute-start(f32[3,40,1,164]{3,1,2,0:T(8,128)S(1)} %get-tuple-element.47), channel_id=1, source_target_pairs={{1,0},{2,1},{3,2},{4,3},{5,4},{6,5},{7,6},{8,7},{9,8},{10,9},{11,1... | collective-permute-start | bytes 236168 | tf_op jit(solution)/shard_map/ppermute | solution.py:40
  117.8 11.9 %collective-permute-start.11 = (f32[512,40]{0,1:T(8,128)S(1)}, f32[512,40]{0,1:T(8,128)S(1)}, u32[]{:S(2)}, u32[]{:S(2)}) collective-permute-start(f32[512,40]{0,1:T(8,128)S(1)} %fusion.29), channel_id=1, source_target_pairs={{1,0},{2,1},{3,2},{4,3},{5,4},{6,5},{7,6},{8,7},{9,8},{10,9},{11,1... | collective-permute-start | bytes 245768 | tf_op jit(solution)/shard_map/ppermute | solution.py:147
  126.0 12.1 %collective-permute-start.10 = (f32[512,40]{0,1:T(8,128)S(1)}, f32[512,40]{0,1:T(8,128)S(1)}, u32[]{:S(2)}, u32[]{:S(2)}) collective-permute-start(f32[512,40]{0,1:T(8,128)S(1)} %fusion.29), channel_id=1, source_target_pairs={{0,1},{1,2},{2,3},{3,4},{4,5},{5,6},{6,7},{7,8},{8,9},{9,10},{10,1... | collective-permute-start | bytes 245768 | tf_op jit(solution)/shard_map/ppermute | solution.py:147
  138.3 3.9 %copy-start.3 = (f32[256,1024]{0,1:T(8,128)S(1)}, f32[256,1024]{0,1:T(8,128)}, u32[]{:S(2)}) copy-start(f32[256,1024]{0,1:T(8,128)} %get-tuple-element.73) | copy-start | bytes 3145732
  146.8 15.5 %collective-permute-start.13 = (f32[256,40]{0,1:T(8,128)S(1)}, f32[256,40]{0,1:T(8,128)S(1)}, u32[]{:S(2)}, u32[]{:S(2)}) collective-permute-start(f32[256,40]{0,1:T(8,128)S(1)} %slice.283), channel_id=1, source_target_pairs={{2,0},{3,1},{4,2},{5,3},{6,4},{7,5},{8,6},{9,7},{10,8},{11,9},{12,... | collective-permute-start | bytes 122888 | tf_op jit(solution)/shard_map/ppermute | solution.py:147
  153.7 15.7 %collective-permute-start.12 = (f32[256,40]{0,1:T(8,128)S(1)}, f32[256,40]{0,1:T(8,128)S(1)}, u32[]{:S(2)}, u32[]{:S(2)}) collective-permute-start(f32[256,40]{0,1:T(8,128)S(1)} %slice.283), channel_id=1, source_target_pairs={{0,2},{1,3},{2,4},{3,5},{4,6},{5,7},{6,8},{7,9},{8,10},{9,11},{10,... | collective-permute-start | bytes 122888 | tf_op jit(solution)/shard_map/ppermute | solution.py:147
  170.2 3.9 %copy-start.2 = (f32[256,1024]{0,1:T(8,128)S(1)}, f32[256,1024]{0,1:T(8,128)}, u32[]{:S(2)}) copy-start(f32[256,1024]{0,1:T(8,128)} %get-tuple-element.72) | copy-start | bytes 3145732

commit v9 on v7

--- a/solution.py
+++ b/solution.py
@@ -158,7 +158,7 @@
     row_hit = jnp.arange(rows_tile, dtype=jnp.int32)[None, :] == (lat_obs - lat_base)[:, None]
     col_hit = (jnp.arange(wide_cols, dtype=jnp.int32)[None, :] == column[:, None]) & inside[:, None]
     cell = (row_hit[:, :, None] & col_hit[:, None, :]).astype(jnp.float32)
-    picked = jnp.einsum("jrc,fmrc->jfm", cell, wide, precision=lax.Precision.HIGHEST)
+    picked = jnp.einsum("jrc,fmrc->jfm", cell, wide, precision=lax.Precision.HIGH)
     field_hit = jnp.arange(fields_count, dtype=jnp.int32)[None, :] == kind_obs[:, None]
     return jnp.sum(jnp.where(field_hit[:, :, None], picked, 0.0), axis=1)
 

time: 176 us -> 174 us (0.989)
  the two profiles are of different devices: /device:TPU:30 before, /device:TPU:26 now
where the time goes in v9:
time: 174 us; the launch traced here: 173 us
  starting transfers between devices  78.2 us (45%)
  waiting for transfers between devices  50 us (29%)
  matrix products  19.2 us (11%)
  local copies, waits for them, and re-layouts  15 us (9%)
  other arithmetic  9.82 us (6%)
    ppermute x4, starting transfers between devices, lat_shift(): return lax.ppermute(array, 'lat', pairs)  26.6 us
    ppermute x4, starting transfers between devices, lat_edges(): after = lax.ppermute(array[:, :, :1, :], 'lat', down)  24.8 us
    ppermute x4, waiting for transfers between devices, lat_edges(): after = lax.ppermute(array[:, :, :1, :], 'lat', down)  24.4 us
    ppermute x4, starting transfers between devices, lat_edges(): before = lax.ppermute(array[:, :, -1:, :], 'lat', up)  22.2 us
    ppermute x4, waiting for transfers between devices, lat_edges(): before = lax.ppermute(array[:, :, -1:, :], 'lat', up)  12.9 us
    ppermute x4, waiting for transfers between devices, lat_shift(): return lax.ppermute(array, 'lat', pairs)  11.4 us
    dot_general x2, matrix products, update(): jnp.einsum('om,foc->fmc', gains, covariance * weights[None], precision=la...  8.8 us
    dot_general x2, matrix products, update(): jnp.einsum('om,fmc->foc', anomaly, deviation, precision=lax.Precision.HIGH)  7.98 us
  transfers between devices with their start and end apart: 14, of which 11 were waited for; matrix products, arithmetic and copies ran while one was open for 6% of the time, Pallas kernels for 0%

profile of v9, /device:TPU:26, one launch (start us, length us, event | category | flops | bytes accessed | tf_op | source)
XLA Modules:
  0.0 172.9 jit_solution(4053349188089786169)
XLA Ops:
  0.0 2.3 %fusion.110 = (f32[9,40,8,18]{3,2,1,0:T(8,128)S(1)}, f32[9,40,8,18]{3,2,1,0:T(8,128)S(1)}) fusion(f32[9,40,8,128]{3,2,1,0:T(8,128)} %param.10), kind=kLoop, calls=%fused_computation.190 | loop fusion | bytes 829440 | tf_op jit(solution)/shard_map/slice | solution.py:94
  2.3 1.4 copy.38
  3.8 2.1 %collective-permute-start.1 = (f32[9,18,8,40]{3,2,1,0:T(8,128)}, f32[9,18,8,40]{3,2,1,0:T(8,128)}, u32[]{:S(2)}, u32[]{:S(2)}) collective-permute-start(f32[9,18,8,40]{3,2,1,0:T(8,128)} %bitcast.89), channel_id=1, source_target_pairs={{0,496},{16,0},{32,16},{48,32},{64,48},{80,64},{96,80},{112,96},{1... | collective-permute-start | bytes 622088 | tf_op jit(solution)/shard_map/ppermute | solution.py:95
  5.8 0.6 copy.37
  6.5 2.5 %collective-permute-start = (f32[9,18,8,40]{3,2,1,0:T(8,128)S(1)}, f32[9,18,8,40]{3,2,1,0:T(8,128)S(1)}, u32[]{:S(2)}, u32[]{:S(2)}) collective-permute-start(f32[9,18,8,40]{3,2,1,0:T(8,128)S(1)} %bitcast.90), channel_id=1, source_target_pairs={{0,16},{16,32},{32,48},{48,64},{64,80},{80,96},{96,112},{112,128},... | collective-permute-start | bytes 622088 | tf_op jit(solution)/shard_map/ppermute | solution.py:94
  9.1 0.1 copy.30
  9.3 1.0 gather_fusion
  10.3 0.3 fusion.75
  10.6 0.3 slice_reduce_fusion.4
  10.9 0.4 slice_reduce_fusion
  11.4 1.4 copy.28
  12.9 0.1 copy.31
  13.0 1.0 gather_fusion.1
  14.1 0.3 slice_reduce_fusion.2
  14.4 2.9 %multiply_multiply_fusion = (f32[256,1024]{0,1:T(8,128)}, f32[256,1024]{0,1:T(8,128)}) fusion(f32[256]{0:T(256)S(1)} %get-tuple-element.9, s32[256]{0:T(256)S(1)} %get-tuple-element.12, s32[256]{0:T(256)S(1)} %get-tuple-element.11, s32[1024]{0:T(1024)S(1)} %get-tuple-element.82, s32[1024]{0:T(1024)S(1)} %get-tuple-element.83, f32[256]{0:T(256)S(1)} %get-tuple-element.10, ...), kind=kLoop, calls=%fused_computation.58 | loop fusion | flops 12582912 | bytes 2111488 | tf_op jit(solution)/shard_map/mul | solution.py:185
  17.3 1.2 collective-permute-done
  18.6 0.6 copy.25
  19.2 1.6 copy.27
  20.8 1.1 pad_maximum_fusion.4
  22.0 0.3 copy-done
  22.3 1.2 pad_maximum_fusion
  23.5 9.1 %collective-permute-start.3 = (f32[3,40,1,164]{3,1,2,0:T(8,128)S(1)}, f32[3,40,1,164]{3,1,2,0:T(8,128)S(1)}, u32[]{:S(2)}, u32[]{:S(2)}) collective-permute-start(f32[3,40,1,164]{3,1,2,0:T(8,128)S(1)} %get-tuple-element.26), channel_id=1, source_target_pairs={{0,1},{1,2},{2,3},{3,4},{4,5},{5,6},{6,7},{7,8},{8,9},{9,10},{10,1... | collective-permute-start | bytes 236168 | tf_op jit(solution)/shard_map/ppermute | solution.py:39
  32.6 5.7 %collective-permute-start.2 = (f32[3,40,1,164]{3,1,2,0:T(8,128)S(1)}, f32[3,40,1,164]{3,1,2,0:T(8,128)S(1)}, u32[]{:S(2)}, u32[]{:S(2)}) collective-permute-start(f32[3,40,1,164]{3,1,2,0:T(8,128)S(1)} %get-tuple-element.27), channel_id=1, source_target_pairs={{1,0},{2,1},{3,2},{4,3},{5,4},{6,5},{7,6},{8,7},{9,8},{10,9},{11,1... | collective-permute-start | bytes 236168 | tf_op jit(solution)/shard_map/ppermute | solution.py:40
  38.3 0.3 fusion.109
  38.8 0.2 slice.242
  39.0 1.0 collective-permute-done.3
  40.0 12.7 %collective-permute-done.2 = f32[3,40,1,164]{3,1,2,0:T(8,128)S(1)} collective-permute-done((f32[3,40,1,164]{3,1,2,0:T(8,128)S(1)}, f32[3,40,1,164]{3,1,2,0:T(8,128)S(1)}, u32[]{:S(2)}, u32[]{:S(2)}) %collective-permute-start.2) | collective-permute-done | bytes 78752 | tf_op jit(solution)/shard_map/ppermute | solution.py:40
  52.7 0.7 slice_subtract_fusion
  53.8 0.3 fusion.119
  54.1 7.5 %collective-permute-start.5 = (f32[3,40,1,164]{3,1,2,0:T(8,128)S(1)}, f32[3,40,1,164]{3,1,2,0:T(8,128)S(1)}, u32[]{:S(2)}, u32[]{:S(2)}) collective-permute-start(f32[3,40,1,164]{3,1,2,0:T(8,128)S(1)} %get-tuple-element.59), channel_id=1, source_target_pairs={{0,1},{1,2},{2,3},{3,4},{4,5},{5,6},{6,7},{7,8},{8,9},{9,10},{10,1... | collective-permute-start | bytes 236168 | tf_op jit(solution)/shard_map/ppermute | solution.py:39
  61.6 3.2 %collective-permute-start.4 = (f32[3,40,1,164]{3,1,2,0:T(8,128)S(1)}, f32[3,40,1,164]{3,1,2,0:T(8,128)S(1)}, u32[]{:S(2)}, u32[]{:S(2)}) collective-permute-start(f32[3,40,1,164]{3,1,2,0:T(8,128)S(1)} %get-tuple-element.60), channel_id=1, source_target_pairs={{1,0},{2,1},{3,2},{4,3},{5,4},{6,5},{7,6},{8,7},{9,8},{10,9},{11,1... | collective-permute-start | bytes 236168 | tf_op jit(solution)/shard_map/ppermute | solution.py:40
  64.8 0.2 fusion.120
  65.0 5.8 %collective-permute-done.5 = f32[3,40,1,164]{3,1,2,0:T(8,128)S(1)} collective-permute-done((f32[3,40,1,164]{3,1,2,0:T(8,128)S(1)}, f32[3,40,1,164]{3,1,2,0:T(8,128)S(1)}, u32[]{:S(2)}, u32[]{:S(2)}) %collective-permute-start.5) | collective-permute-done | bytes 78752 | tf_op jit(solution)/shard_map/ppermute | solution.py:39
  70.8 6.4 %collective-permute-done.4 = f32[3,40,1,164]{3,1,2,0:T(8,128)S(1)} collective-permute-done((f32[3,40,1,164]{3,1,2,0:T(8,128)S(1)}, f32[3,40,1,164]{3,1,2,0:T(8,128)S(1)}, u32[]{:S(2)}, u32[]{:S(2)}) %collective-permute-start.4) | collective-permute-done | bytes 78752 | tf_op jit(solution)/shard_map/ppermute | solution.py:40
  77.2 0.7 fusion.55
  78.0 3.1 %collective-permute-start.7 = (f32[3,40,1,164]{3,1,2,0:T(8,128)S(1)}, f32[3,40,1,164]{3,1,2,0:T(8,128)S(1)}, u32[]{:S(2)}, u32[]{:S(2)}) collective-permute-start(f32[3,40,1,164]{3,1,2,0:T(8,128)S(1)} %get-tuple-element.47), channel_id=1, source_target_pairs={{0,1},{1,2},{2,3},{3,4},{4,5},{5,6},{6,7},{7,8},{8,9},{9,10},{10,1... | collective-permute-start | bytes 236168 | tf_op jit(solution)/shard_map/ppermute | solution.py:39
  81.0 7.6 %collective-permute-start.6 = (f32[3,40,1,164]{3,1,2,0:T(8,128)S(1)}, f32[3,40,1,164]{3,1,2,0:T(8,128)S(1)}, u32[]{:S(2)}, u32[]{:S(2)}) collective-permute-start(f32[3,40,1,164]{3,1,2,0:T(8,128)S(1)} %get-tuple-element.48), channel_id=1, source_target_pairs={{1,0},{2,1},{3,2},{4,3},{5,4},{6,5},{7,6},{8,7},{9,8},{10,9},{11,1... | collective-permute-start | bytes 236168 | tf_op jit(solution)/shard_map/ppermute | solution.py:40
  88.6 0.3 fusion.118
  89.0 0.2 fusion.117
  89.2 1.4 collective-permute-done.7
  90.6 2.9 %collective-permute-done.6 = f32[3,40,1,164]{3,1,2,0:T(8,128)S(1)} collective-permute-done((f32[3,40,1,164]{3,1,2,0:T(8,128)S(1)}, f32[3,40,1,164]{3,1,2,0:T(8,128)S(1)}, u32[]{:S(2)}, u32[]{:S(2)}) %collective-permute-start.6) | collective-permute-done | bytes 78752 | tf_op jit(solution)/shard_map/ppermute | solution.py:40
  93.4 0.7 fusion.53
  94.5 0.3 fusion.111
  94.8 2.6 %collective-permute-start.9 = (f32[3,40,1,164]{3,1,2,0:T(8,128)S(1)}, f32[3,40,1,164]{3,1,2,0:T(8,128)S(1)}, u32[]{:S(2)}, u32[]{:S(2)}) collective-permute-start(f32[3,40,1,164]{3,1,2,0:T(8,128)S(1)} %get-tuple-element.40), channel_id=1, source_target_pairs={{0,1},{1,2},{2,3},{3,4},{4,5},{5,6},{6,7},{7,8},{8,9},{9,10},{10,1... | collective-permute-start | bytes 236168 | tf_op jit(solution)/shard_map/ppermute | solution.py:39
  97.4 8.3 %collective-permute-start.8 = (f32[3,40,1,164]{3,1,2,0:T(8,128)S(1)}, f32[3,40,1,164]{3,1,2,0:T(8,128)S(1)}, u32[]{:S(2)}, u32[]{:S(2)}) collective-permute-start(f32[3,40,1,164]{3,1,2,0:T(8,128)S(1)} %get-tuple-element.41), channel_id=1, source_target_pairs={{1,0},{2,1},{3,2},{4,3},{5,4},{6,5},{7,6},{8,7},{9,8},{10,9},{11,1... | collective-permute-start | bytes 236168 | tf_op jit(solution)/shard_map/ppermute | solution.py:40
  105.7 0.2 fusion.112
  105.9 4.7 %collective-permute-done.9 = f32[3,40,1,164]{3,1,2,0:T(8,128)S(1)} collective-permute-done((f32[3,40,1,164]{3,1,2,0:T(8,128)S(1)}, f32[3,40,1,164]{3,1,2,0:T(8,128)S(1)}, u32[]{:S(2)}, u32[]{:S(2)}) %collective-permute-start.9) | collective-permute-done | bytes 78752 | tf_op jit(solution)/shard_map/ppermute | solution.py:39
  110.5 2.4 %collective-permute-done.8 = f32[3,40,1,164]{3,1,2,0:T(8,128)S(1)} collective-permute-done((f32[3,40,1,164]{3,1,2,0:T(8,128)S(1)}, f32[3,40,1,164]{3,1,2,0:T(8,128)S(1)}, u32[]{:S(2)}, u32[]{:S(2)}) %collective-permute-start.8) | collective-permute-done | bytes 78752 | tf_op jit(solution)/shard_map/ppermute | solution.py:40
  112.9 0.7 fusion.59
  113.7 0.5 fusion.63
  114.2 1.8 %fusion.29 = f32[512,40]{0,1:T(8,128)S(1)} fusion(f32[3,40,8,164]{3,1,2,0:T(8,128)S(1)} %get-tuple-element.22, f32[3,40,8,164]{3,1,2,0:T(8,128)S(1)} %get-tuple-element.23, f32[3,40,8,164]{3,1,2,0:T(8,128)S(1)} %fusion.53, pred[512,164]{0,1:T(8,128)(4,1)S(1)} %fusion.62, pred[512,8]{0,1:T(8,128)(4,1)S(1)} %iota_compare_fusion.2, ...), kind=kOutput, calls=%fused_computation.42 | convolution fusion | flops 1452931584 | bytes 2063872 | tf_op jit(solution)/shard_map/jrc,fmrc->jfm/dot_general | solution.py:161
  115.9 9.1 %collective-permute-start.13 = (f32[256,40]{0,1:T(8,128)S(1)}, f32[256,40]{0,1:T(8,128)S(1)}, u32[]{:S(2)}, u32[]{:S(2)}) collective-permute-start(f32[256,40]{0,1:T(8,128)S(1)} %slice.283), channel_id=1, source_target_pairs={{2,0},{3,1},{4,2},{5,3},{6,4},{7,5},{8,6},{9,7},{10,8},{11,9},{12,... | collective-permute-start | bytes 122888 | tf_op jit(solution)/shard_map/ppermute | solution.py:147
  125.0 5.5 %collective-permute-start.12 = (f32[256,40]{0,1:T(8,128)S(1)}, f32[256,40]{0,1:T(8,128)S(1)}, u32[]{:S(2)}, u32[]{:S(2)}) collective-permute-start(f32[256,40]{0,1:T(8,128)S(1)} %slice.283), channel_id=1, source_target_pairs={{0,2},{1,3},{2,4},{3,5},{4,6},{5,7},{6,8},{7,9},{8,10},{9,11},{10,... | collective-permute-start | bytes 122888 | tf_op jit(solution)/shard_map/ppermute | solution.py:147
  130.5 10.2 %collective-permute-start.11 = (f32[512,40]{0,1:T(8,128)S(1)}, f32[512,40]{0,1:T(8,128)S(1)}, u32[]{:S(2)}, u32[]{:S(2)}) collective-permute-start(f32[512,40]{0,1:T(8,128)S(1)} %fusion.29), channel_id=1, source_target_pairs={{1,0},{2,1},{3,2},{4,3},{5,4},{6,5},{7,6},{8,7},{9,8},{10,9},{11,1... | collective-permute-start | bytes 245768 | tf_op jit(solution)/shard_map/ppermute | solution.py:147
  140.7 1.9 %collective-permute-start.10 = (f32[512,40]{0,1:T(8,128)S(1)}, f32[512,40]{0,1:T(8,128)S(1)}, u32[]{:S(2)}, u32[]{:S(2)}) collective-permute-start(f32[512,40]{0,1:T(8,128)S(1)} %fusion.29), channel_id=1, source_target_pairs={{0,1},{1,2},{2,3},{3,4},{4,5},{5,6},{6,7},{7,8},{8,9},{9,10},{10,1... | collective-permute-start | bytes 245768 | tf_op jit(solution)/shard_map/ppermute | solution.py:147
  142.6 1.5 collective-permute-done.11
  144.1 10.0 %collective-permute-done.10 = f32[512,40]{0,1:T(8,128)S(1)} collective-permute-done((f32[512,40]{0,1:T(8,128)S(1)}, f32[512,40]{0,1:T(8,128)S(1)}, u32[]{:S(2)}, u32[]{:S(2)}) %collective-permute-start.10) | collective-permute-done | bytes 81952 | tf_op jit(solution)/shard_map/ppermute | solution.py:147
  154.2 0.5 fusion.34
  154.7 3.9 %fusion.12 = f32[9,1024,256]{2,1,0:T(8,128)S(1)} fusion(f32[9,8,5,8,128]{4,3,2,1,0:T(8,128)S(1)} %get-tuple-element.29, f32[9,1024]{1,0:T(8,128)S(1)} %bitcast.91, f32[256,40]{0,1:T(8,128)S(1)} %get-tuple-element.19, f32[256]{0:T(256)S(1)} %get-tuple-element.76), kind=kOutput, calls=%fused_computation.31 | convolution fusion | flops 566609920 | bytes 10990592 | tf_op jit(solution)/shard_map/om,fmc->foc/dot_general | solution.py:181
  158.6 0.2 fusion.124
  158.8 4.3 %fusion.123 = (f32[9,1024]{1,0:T(8,128)S(1)}, f32[9,40,1024]{2,1,0:T(8,128)S(1)}) fusion(f32[256]{0:T(256)S(1)} %get-tuple-element.72, f32[256,40]{0,1:T(8,128)S(1)} %get-tuple-element.19, f32[256]{0:T(256)S(1)} %get-tuple-element.76, f32[256]{0:T(256)S(1)} %get-tuple-element.71, f32[256]{0:T(256)S(1)} %get-tuple-element.75, ...), kind=kOutput, calls=%fused_computation.203 | convolution fusion | flops 569359360 | bytes 13516800 | tf_op jit(solution)/shard_map/om,foc->fmc/dot_general | solution.py:184
  163.2 4.1 %fusion.14 = f32[9,1024,256]{2,1,0:T(8,128)S(1)} fusion(f32[9,40,1024]{2,1,0:T(8,128)S(1)} %get-tuple-element.78, f32[9,1024]{1,0:T(8,128)S(1)} %broadcast_multiply_fusion, f32[256,40]{0,1:T(8,128)S(1)} %get-tuple-element.80, f32[256]{0:T(256)S(1)} %get-tuple-element.74), kind=kOutput, calls=%fused_computation.35 | convolution fusion | flops 566609920 | bytes 10990592 | tf_op jit(solution)/shard_map/om,fmc->foc/dot_general | solution.py:181
  167.3 4.5 %fusion.13 = bf16[9,40,1024]{2,1,0:T(8,128)(2,1)S(1)} fusion(f32[9,40,1024]{2,1,0:T(8,128)S(1)} %get-tuple-element.78, f32[9,1024,256]{2,1,0:T(8,128)S(1)} %fusion.14, f32[256,1024]{0,1:T(8,128)S(1)} %copy-done.2, f32[256,40]{0,1:T(8,128)S(1)} %get-tuple-element.80, f32[256]{0:T(256)S(1)} %get-tuple-element.70, f32[256]{0:T(256)S(1)} %get-tuple-element.69, ...), kind=kOutput, calls=%fused_computation.34 | convolution fusion | flops 569368576 | bytes 12742656 | tf_op jit(solution)/shard_map/om,foc->fmc/dot_general | solution.py:184
  171.8 1.0 copy.41
  (61 shorter events, 1.4 us)
Async XLA Ops:
  3.8 5.3 %copy-start.5 = (s32[512]{0:T(512)S(1)}, s32[512]{0:T(512)}, u32[]{:S(2)}) copy-start(s32[512]{0:T(512)} %param.15) | copy-start | bytes 6148
  3.8 5.3 %copy-start.8 = (s32[512]{0:T(512)S(1)}, s32[512]{0:T(512)}, u32[]{:S(2)}) copy-start(s32[512]{0:T(512)} %param.14) | copy-start | bytes 6148
  3.8 5.3 %copy-start.9 = (s32[512]{0:T(512)S(1)}, s32[512]{0:T(512)}, u32[]{:S(2)}) copy-start(s32[512]{0:T(512)} %param.13) | copy-start | bytes 6148
  3.8 5.3 %copy-start.10 = (s32[512]{0:T(512)S(1)}, s32[512]{0:T(512)}, u32[]{:S(2)}) copy-start(s32[512]{0:T(512)} %param.12) | copy-start | bytes 6148
  3.8 5.3 %copy-start.11 = (s32[512]{0:T(512)S(1)}, s32[512]{0:T(512)}, u32[]{:S(2)}) copy-start(s32[512]{0:T(512)} %param.11) | copy-start | bytes 6148
  3.8 15.4 %collective-permute-start.1 = (f32[9,18,8,40]{3,2,1,0:T(8,128)}, f32[9,18,8,40]{3,2,1,0:T(8,128)}, u32[]{:S(2)}, u32[]{:S(2)}) collective-permute-start(f32[9,18,8,40]{3,2,1,0:T(8,128)} %bitcast.89), channel_id=1, source_target_pairs={{0,496},{16,0},{32,16},{48,32},{64,48},{80,64},{96,80},{112,96},{1... | collective-permute-start | bytes 622088 | tf_op jit(solution)/shard_map/ppermute | solution.py:95
  6.4 4.9 %copy-start.1 = (f32[9,40,8,128]{3,2,1,0:T(8,128)S(1)}, f32[9,40,8,128]{3,2,1,0:T(8,128)}, u32[]{:S(2)}) copy-start(f32[9,40,8,128]{3,2,1,0:T(8,128)} %param.10) | copy-start | bytes 4423684
  6.5 12.1 %collective-permute-start = (f32[9,18,8,40]{3,2,1,0:T(8,128)S(1)}, f32[9,18,8,40]{3,2,1,0:T(8,128)S(1)}, u32[]{:S(2)}, u32[]{:S(2)}) collective-permute-start(f32[9,18,8,40]{3,2,1,0:T(8,128)S(1)} %bitcast.90), channel_id=1, source_target_pairs={{0,16},{16,32},{32,48},{48,64},{64,80},{80,96},{96,112},{112,128},... | collective-permute-start | bytes 622088 | tf_op jit(solution)/shard_map/ppermute | solution.py:94
  11.4 1.4 copy-start.6
  11.4 1.4 copy-start.7
  20.8 1.4 copy-start
  23.5 16.6 %collective-permute-start.3 = (f32[3,40,1,164]{3,1,2,0:T(8,128)S(1)}, f32[3,40,1,164]{3,1,2,0:T(8,128)S(1)}, u32[]{:S(2)}, u32[]{:S(2)}) collective-permute-start(f32[3,40,1,164]{3,1,2,0:T(8,128)S(1)} %get-tuple-element.26), channel_id=1, source_target_pairs={{0,1},{1,2},{2,3},{3,4},{4,5},{5,6},{6,7},{7,8},{8,9},{9,10},{10,1... | collective-permute-start | bytes 236168 | tf_op jit(solution)/shard_map/ppermute | solution.py:39
  32.6 20.2 %collective-permute-start.2 = (f32[3,40,1,164]{3,1,2,0:T(8,128)S(1)}, f32[3,40,1,164]{3,1,2,0:T(8,128)S(1)}, u32[]{:S(2)}, u32[]{:S(2)}) collective-permute-start(f32[3,40,1,164]{3,1,2,0:T(8,128)S(1)} %get-tuple-element.27), channel_id=1, source_target_pairs={{1,0},{2,1},{3,2},{4,3},{5,4},{6,5},{7,6},{8,7},{9,8},{10,9},{11,1... | collective-permute-start | bytes 236168 | tf_op jit(solution)/shard_map/ppermute | solution.py:40
  38.8 14.0 %copy-start.4 = (f32[3]{0:T(128)S(1)}, f32[3]{0:T(128)}, u32[]{:S(2)}) copy-start(f32[3]{0:T(128)} %constant.115) | copy-start | bytes 40
  54.1 16.7 %collective-permute-start.5 = (f32[3,40,1,164]{3,1,2,0:T(8,128)S(1)}, f32[3,40,1,164]{3,1,2,0:T(8,128)S(1)}, u32[]{:S(2)}, u32[]{:S(2)}) collective-permute-start(f32[3,40,1,164]{3,1,2,0:T(8,128)S(1)} %get-tuple-element.59), channel_id=1, source_target_pairs={{0,1},{1,2},{2,3},{3,4},{4,5},{5,6},{6,7},{7,8},{8,9},{9,10},{10,1... | collective-permute-start | bytes 236168 | tf_op jit(solution)/shard_map/ppermute | solution.py:39
  61.6 15.6 %collective-permute-start.4 = (f32[3,40,1,164]{3,1,2,0:T(8,128)S(1)}, f32[3,40,1,164]{3,1,2,0:T(8,128)S(1)}, u32[]{:S(2)}, u32[]{:S(2)}) collective-permute-start(f32[3,40,1,164]{3,1,2,0:T(8,128)S(1)} %get-tuple-element.60), channel_id=1, source_target_pairs={{1,0},{2,1},{3,2},{4,3},{5,4},{6,5},{7,6},{8,7},{9,8},{10,9},{11,1... | collective-permute-start | bytes 236168 | tf_op jit(solution)/shard_map/ppermute | solution.py:40
  78.0 12.6 %collective-permute-start.7 = (f32[3,40,1,164]{3,1,2,0:T(8,128)S(1)}, f32[3,40,1,164]{3,1,2,0:T(8,128)S(1)}, u32[]{:S(2)}, u32[]{:S(2)}) collective-permute-start(f32[3,40,1,164]{3,1,2,0:T(8,128)S(1)} %get-tuple-element.47), channel_id=1, source_target_pairs={{0,1},{1,2},{2,3},{3,4},{4,5},{5,6},{6,7},{7,8},{8,9},{9,10},{10,1... | collective-permute-start | bytes 236168 | tf_op jit(solution)/shard_map/ppermute | solution.py:39
  81.0 12.4 %collective-permute-start.6 = (f32[3,40,1,164]{3,1,2,0:T(8,128)S(1)}, f32[3,40,1,164]{3,1,2,0:T(8,128)S(1)}, u32[]{:S(2)}, u32[]{:S(2)}) collective-permute-start(f32[3,40,1,164]{3,1,2,0:T(8,128)S(1)} %get-tuple-element.48), channel_id=1, source_target_pairs={{1,0},{2,1},{3,2},{4,3},{5,4},{6,5},{7,6},{8,7},{9,8},{10,9},{11,1... | collective-permute-start | bytes 236168 | tf_op jit(solution)/shard_map/ppermute | solution.py:40
  94.8 15.7 %collective-permute-start.9 = (f32[3,40,1,164]{3,1,2,0:T(8,128)S(1)}, f32[3,40,1,164]{3,1,2,0:T(8,128)S(1)}, u32[]{:S(2)}, u32[]{:S(2)}) collective-permute-start(f32[3,40,1,164]{3,1,2,0:T(8,128)S(1)} %get-tuple-element.40), channel_id=1, source_target_pairs={{0,1},{1,2},{2,3},{3,4},{4,5},{5,6},{6,7},{7,8},{8,9},{9,10},{10,1... | collective-permute-start | bytes 236168 | tf_op jit(solution)/shard_map/ppermute | solution.py:39
  97.4 15.6 %collective-permute-start.8 = (f32[3,40,1,164]{3,1,2,0:T(8,128)S(1)}, f32[3,40,1,164]{3,1,2,0:T(8,128)S(1)}, u32[]{:S(2)}, u32[]{:S(2)}) collective-permute-start(f32[3,40,1,164]{3,1,2,0:T(8,128)S(1)} %get-tuple-element.41), channel_id=1, source_target_pairs={{1,0},{2,1},{3,2},{4,3},{5,4},{6,5},{7,6},{8,7},{9,8},{10,9},{11,1... | collective-permute-start | bytes 236168 | tf_op jit(solution)/shard_map/ppermute | solution.py:40
  115.9 38.2 %collective-permute-start.13 = (f32[256,40]{0,1:T(8,128)S(1)}, f32[256,40]{0,1:T(8,128)S(1)}, u32[]{:S(2)}, u32[]{:S(2)}) collective-permute-start(f32[256,40]{0,1:T(8,128)S(1)} %slice.283), channel_id=1, source_target_pairs={{2,0},{3,1},{4,2},{5,3},{6,4},{7,5},{8,6},{9,7},{10,8},{11,9},{12,... | collective-permute-start | bytes 122888 | tf_op jit(solution)/shard_map/ppermute | solution.py:147
  125.0 29.1 %collective-permute-start.12 = (f32[256,40]{0,1:T(8,128)S(1)}, f32[256,40]{0,1:T(8,128)S(1)}, u32[]{:S(2)}, u32[]{:S(2)}) collective-permute-start(f32[256,40]{0,1:T(8,128)S(1)} %slice.283), channel_id=1, source_target_pairs={{0,2},{1,3},{2,4},{3,5},{4,6},{5,7},{6,8},{7,9},{8,10},{9,11},{10,... | collective-permute-start | bytes 122888 | tf_op jit(solution)/shard_map/ppermute | solution.py:147
  130.5 13.6 %collective-permute-start.11 = (f32[512,40]{0,1:T(8,128)S(1)}, f32[512,40]{0,1:T(8,128)S(1)}, u32[]{:S(2)}, u32[]{:S(2)}) collective-permute-start(f32[512,40]{0,1:T(8,128)S(1)} %fusion.29), channel_id=1, source_target_pairs={{1,0},{2,1},{3,2},{4,3},{5,4},{6,5},{7,6},{8,7},{9,8},{10,9},{11,1... | collective-permute-start | bytes 245768 | tf_op jit(solution)/shard_map/ppermute | solution.py:147
  140.7 13.4 %collective-permute-start.10 = (f32[512,40]{0,1:T(8,128)S(1)}, f32[512,40]{0,1:T(8,128)S(1)}, u32[]{:S(2)}, u32[]{:S(2)}) collective-permute-start(f32[512,40]{0,1:T(8,128)S(1)} %fusion.29), channel_id=1, source_target_pairs={{0,1},{1,2},{2,3},{3,4},{4,5},{5,6},{6,7},{7,8},{8,9},{9,10},{10,1... | collective-permute-start | bytes 245768 | tf_op jit(solution)/shard_map/ppermute | solution.py:147
  154.7 4.1 %copy-start.3 = (f32[256,1024]{0,1:T(8,128)S(1)}, f32[256,1024]{0,1:T(8,128)}, u32[]{:S(2)}) copy-start(f32[256,1024]{0,1:T(8,128)} %get-tuple-element.68) | copy-start | bytes 3145732
  163.2 4.1 %copy-start.2 = (f32[256,1024]{0,1:T(8,128)S(1)}, f32[256,1024]{0,1:T(8,128)}, u32[]{:S(2)}) copy-start(f32[256,1024]{0,1:T(8,128)} %get-tuple-element.67) | copy-start | bytes 3145732
